TPU v7x, 512 devices: a whole 4x8x8 slice. The times are simulated.
512 devices in a mesh: grp: 16 (over z, core), shard: 32 (over x, y).
Axes of the slice: x: 4, y: 8, z: 8, core: 2. Of those that a mesh axis runs over, the one named last changes fastest.
Arguments:
- src_rows: bfloat16 [128, 128, 5376], P('grp', 'shard'), may hold values from -6 to 6
- src_act: bfloat16 [128, 128], P('grp', 'shard'), may hold values from 0.29882812 to 3
- encoder: bfloat16 [16, 32, 3, 5376, 128], P('grp', 'shard'), may hold values from -0.078125 to 0.078125
- dest_list: int32 [16, 6], replicated, may hold values from -1 to 127, as said below
- pair_list: int32 [16, 32, 18, 2], P('grp', 'shard'), may hold values from 0 to 5, as said below
- pair_count: int32 [16, 32], P('grp', 'shard'), may hold values from 1 to 18, as said below
Outputs:
- edges: bfloat16 [16, 32, 18, 128, 128], P('grp', 'shard')
Inputs may be any that keep to these rules, and one draw needn't show every extreme that they name: `dest_list`: row g holds between 3 and 6 source blocks followed by -1; the blocks of one row come from distinct source groups (block // 8); some row is full. `pair_list`: entries are (slot, encoder block) with slot < 6 and block < 3; the first pair_count entries of a device are distinct pairs whose slot holds a block of its group. `pair_count`: at most 3 times the number of blocks of the device's group; some device has 18.
All inputs are finite; a program needn't handle non-finite values.
Results may differ from a plain program's by a relative error of at most 0.001.
Values may be sent and summed in bfloat16 or wider, within the bound.
No kernel may reach another device: no remote copies, remote signals or barrier semaphores. Data moves between devices by JAX's collectives and lax.ppermute only.
A program may use at most 64 MiB of HBM per device.

v0:
```python
import jax
import jax.numpy as jnp
from jax import lax
from jax.sharding import PartitionSpec as P


def local(src_rows, src_act, encoder, dest_list, pair_list, pair_count):
    my_group = lax.axis_index("grp")
    my_list = lax.dynamic_index_in_dim(dest_list, my_group, 0, keepdims=False)
    is_valid = my_list >= 0
    picked = jnp.maximum(my_list, 0)
    all_rows, all_scale = (
        lax.all_gather(src_rows, "grp", axis=0, tiled=True),
        lax.all_gather(src_act, "grp", axis=0, tiled=True),
    )
    slot_rows = jnp.take(all_rows, picked, axis=0)
    slot_scale = jnp.take(all_scale, picked, axis=0)
    slot_rows = jnp.where(is_valid[:, None, None], slot_rows, jnp.zeros((), slot_rows.dtype))
    slot_scale = jnp.where(is_valid[:, None], slot_scale, jnp.zeros((), slot_scale.dtype))
    full_rows, full_scale = (
        lax.all_gather(slot_rows, "shard", axis=1, tiled=True),
        lax.all_gather(slot_scale, "shard", axis=1, tiled=True),
    )
    weights = encoder[0, 0]
    dev_pairs = pair_list[0, 0]
    slot_ids = dev_pairs[:, 0]
    block_ids = dev_pairs[:, 1]
    amount = pair_count[0, 0]
    slots_total = full_rows.shape[0]
    tile_rows = full_rows.shape[1]
    width = full_rows.shape[2]
    enc_count = weights.shape[0]
    tile_cols = weights.shape[2]
    pair_total = dev_pairs.shape[0]
    stacked = full_rows.reshape(slots_total * tile_rows, width)
    products = jnp.einsum("rd,edc->rec", stacked, weights, preferred_element_type=jnp.float32)
    products = products.reshape(slots_total, tile_rows, enc_count, tile_cols)
    chosen = products[slot_ids, :, block_ids, :]
    scales = jnp.take(full_scale, slot_ids, axis=0).astype(jnp.float32)
    is_live = jnp.arange(pair_total) < amount
    result = jnp.where(
        is_live[:, None, None], scales[:, :, None] * chosen, jnp.zeros((), jnp.float32)
    ).astype(jnp.bfloat16)
    return result[None, None]


def solution(mesh):
    return jax.shard_map(
        local,
        mesh=mesh,
        in_specs=(
            P("grp", "shard", None),
            P("grp", "shard"),
            P("grp", "shard", None, None, None),
            P(),
            P("grp", "shard", None, None),
            P("grp", "shard"),
        ),
        out_specs=P("grp", "shard", None, None, None),
        check_vma=False,
    )
```

profile of v0, /device:TPU:6, one launch (start us, length us, event | category | flops | bytes accessed | tf_op | source)
XLA Modules:
  0.0 195.3 jit_solution(8817233090064426488)
XLA Ops:
  6.5 0.0 copy-start
  6.5 0.0 all-gather.5.cloned.1.call-start
  6.5 0.7 all-gather.5.cloned.1.call-update
  7.3 0.0 copy-start.1
  7.3 0.0 all-gather.7.cloned.1.call-start
  7.3 0.9 maximum_reduce_fusion
  8.2 0.9 compare_reduce_fusion.1
  9.1 52.2 %all-gather.5.cloned.1.call-done = bf16[128,4,5376]{2,1,0:T(4,128)(2,1)} async-done(((bf16[8,4,5376]{2,1,0:T(4,128)(2,1)}), bf16[128,4,5376]{2,1,0:T(4,128)(2,1)}) %all-gather.5.cloned.1.call-update) | async-done | bytes 5505040 | tf_op jit(solution)/shard_map/all_gather | solution.py:13
  61.3 3.3 %gather_fusion.2 = bf16[6,4,5376]{2,1,0:T(4,128)(2,1)S(1)} fusion(bf16[128,4,5376]{2,1,0:T(4,128)(2,1)} %all-gather.5.cloned.1.call-done, s32[1024]{0:T(1024)S(1)} %pad_clamp_fusion.1), kind=kCustom, calls=%fused_computation.2 | custom fusion | bytes 516120 | tf_op jit(solution)/shard_map/jit(_take)/gather | solution.py:16
  64.7 0.2 select_select_fusion
  64.9 0.8 copy.16
  65.6 0.0 all-gather.7.cloned.1.call-update
  65.7 0.0 copy-done
  65.7 16.2 %all-gather = bf16[16,8,4]{1,2,0:T(4,128)(2,1)S(1)} all-gather(bf16[1,8,4]{1,2,0:T(4,128)(2,1)S(1)} %bitcast.32), channel_id=1, replica_groups=mesh['grp'=16,'shard'=32] {'grp'}, dimensions={0}, use_global_device_ids=true | all-gather | bytes 1088 | tf_op jit(solution)/shard_map/all_gather | solution.py:14
  81.9 0.2 copy.13
  82.1 0.6 gather_fusion
  82.6 0.1 select_bitcast_fusion
  82.7 0.1 copy.14
  82.8 37.9 %all-gather.1 = bf16[32,4,6]{2,1,0:T(4,128)(2,1)S(1)} all-gather(bf16[1,4,6]{2,1,0:T(4,128)(2,1)S(1)} %bitcast.31), channel_id=1, replica_groups=mesh['grp'=16,'shard'=32] {'shard'}, dimensions={0}, use_global_device_ids=true | all-gather | bytes 1584 | tf_op jit(solution)/shard_map/all_gather | solution.py:22
  120.7 0.1 copy.19
  121.5 0.0 copy-done.1
  121.5 0.6 gather_fusion.1
  122.1 0.1 select_convert_fusion
  122.2 56.0 %all-gather.7.cloned.1.call-done = bf16[6,128,5376]{2,0,1:T(8,128)(2,1)} async-done(((bf16[6,4,5376]{2,0,1:T(8,128)(2,1)}), bf16[6,128,5376]{2,0,1:T(8,128)(2,1)}) %all-gather.7.cloned.1.call-update) | async-done | bytes 8257552 | tf_op jit(solution)/shard_map/all_gather | solution.py:21
  178.2 8.4 %fusion = f32[6,128,3,128]{3,1,2,0:T(8,128)S(1)} fusion(bf16[6,128,5376,1]{2,0,1,3:T(8,128)(2,1)} %bitcast.35, bf16[1,1,3,5376,128]{4,3,2,1,0:T(8,128)(2,1)} %param.8), kind=kOutput, calls=%fused_computation.4 | convolution fusion | flops 3170893824 | bytes 13565952 | tf_op jit(solution)/shard_map/rd,edc->rec/dot_general | solution.py:36
  186.6 0.7 gather_fusion.3
  187.3 1.2 fusion.4
  (5 shorter events, 0.0 us)
Async XLA Ops:
  6.5 59.1 %copy-start = (bf16[8,4]{0,1:T(4,128)(2,1)S(1)}, bf16[8,4]{0,1:T(4,128)(2,1)}, u32[]{:S(2)}) copy-start(bf16[8,4]{0,1:T(4,128)(2,1)} %param.7) | copy-start | bytes 196
  6.5 54.8 %all-gather.5.cloned.1.call-start = ((), (), s32[]{:S(2)}) async-start(), calls=%async_computation | async-start | bytes 5849088 | tf_op jit(solution)/shard_map/all_gather | solution.py:13
  7.3 114.2 %copy-start.1 = (s32[1,1,18,2]{2,3,1,0:T(2,128)S(1)}, s32[1,1,18,2]{2,3,1,0:T(2,128)}, u32[]{:S(2)}) copy-start(s32[1,1,18,2]{2,3,1,0:T(2,128)} %param.10) | copy-start | bytes 436
  7.3 170.9 %all-gather.7.cloned.1.call-start = ((), (), s32[]{:S(2)}) async-start(), calls=%async_computation.1 | async-start | bytes 11354112 | tf_op jit(solution)/shard_map/all_gather | solution.py:21
Sparse Core Ops, SparseCore 0:
  9.5 51.8 all-gather.4
  65.8 112.3 all-gather.6
where the time goes:
time: 198 us; the launch traced here: 195 us
  waiting for transfers between devices  109 us (55%)
  blocking collectives  54.1 us (27%)
  between operations  14.2 us (7%)
  matrix products  8.42 us (4%)
  local copies, waits for them, and re-layouts  6.26 us (3%)
  other arithmetic  3.4 us (2%)
    all_gather x1, waiting for transfers between devices, local(): lax.all_gather(slot_rows, 'shard', axis=1, tiled=True)  56 us
    all_gather x1, waiting for transfers between devices, local(): lax.all_gather(src_rows, 'grp', axis=0, tiled=True)  52.2 us
    all_gather x1, blocking collectives, local(): lax.all_gather(slot_scale, 'shard', axis=1, tiled=True)  37.9 us
    all_gather x1, blocking collectives, local(): lax.all_gather(src_act, 'grp', axis=0, tiled=True)  16.2 us
    dot_general x1, matrix products, local(): jnp.einsum('rd,edc->rec', stacked, weights, preferred_element_type=jnp.fl...  8.42 us
  transfers between devices with their start and end apart: 2, of which 2 were waited for; matrix products, arithmetic and copies ran while one was open for 2% of the time, Pallas kernels for 0%

commit v1 on v0

v1 whole, which is shorter than its diff:
```python
import jax
import jax.numpy as jnp
from jax import lax
from jax.sharding import Mesh
from jax.sharding import PartitionSpec as P

GRP = ("z", "c")
SHARD = ("x", "y")


def local(src_rows, src_act, encoder, dest_list, pair_list, pair_count):
    n_grp = lax.psum(1, GRP)
    nb_g = src_rows.shape[0]
    width = src_rows.shape[2]
    lanes = 128
    my_group = lax.axis_index("z") * lax.psum(1, "c") + lax.axis_index("c")

    act_block = jnp.zeros(src_act.shape + (lanes,), src_rows.dtype)
    act_block = act_block.at[:, :, 0].set(src_act)
    rows_ext = jnp.concatenate([src_rows, act_block], axis=-1)

    is_valid = dest_list >= 0
    from_me = is_valid & (dest_list // nb_g == my_group)
    sel = jnp.sum(jnp.where(from_me, dest_list % nb_g, 0), axis=1)
    send = jnp.take(rows_ext, sel, axis=0)
    recv = lax.all_to_all(send, GRP, 0, 0, tiled=True)

    my_list = lax.dynamic_index_in_dim(dest_list, my_group, 0, keepdims=False)
    my_valid = my_list >= 0
    source = jnp.where(my_valid, my_list // nb_g, 0)
    slot_rows = jnp.take(recv, source, axis=0)
    slot_rows = jnp.where(my_valid[:, None, None], slot_rows, jnp.zeros((), slot_rows.dtype))

    full = lax.all_gather(slot_rows, "y", axis=1, tiled=True)
    full = lax.all_gather(full, "x", axis=1, tiled=True)

    weights = encoder[0, 0]
    weights = jnp.pad(weights, ((0, 0), (0, lanes), (0, 0)))
    dev_pairs = pair_list[0, 0]
    slot_ids = dev_pairs[:, 0]
    block_ids = dev_pairs[:, 1]
    amount = pair_count[0, 0]
    slots_total, tile_rows, ext_width = full.shape
    enc_count = weights.shape[0]
    tile_cols = weights.shape[2]
    pair_total = dev_pairs.shape[0]
    full_scale = full[:, :, width]
    stacked = full.reshape(slots_total * tile_rows, ext_width)
    products = jnp.einsum("rd,edc->rec", stacked, weights, preferred_element_type=jnp.float32)
    products = products.reshape(slots_total, tile_rows, enc_count, tile_cols)
    chosen = products[slot_ids, :, block_ids, :]
    scales = jnp.take(full_scale, slot_ids, axis=0).astype(jnp.float32)
    is_live = jnp.arange(pair_total) < amount
    result = jnp.where(
        is_live[:, None, None], scales[:, :, None] * chosen, jnp.zeros((), jnp.float32)
    ).astype(jnp.bfloat16)
    return result[None, None]


def solution(mesh):
    n_grp, n_shard = mesh.devices.shape
    n_c = 2
    n_x = 4
    devs = mesh.devices.reshape(n_grp // n_c, n_c, n_x, n_shard // n_x)
    mesh4 = Mesh(devs, ("z", "c", "x", "y"))
    return jax.shard_map(
        local,
        mesh=mesh4,
        in_specs=(
            P(GRP, SHARD, None),
            P(GRP, SHARD),
            P(GRP, SHARD, None, None, None),
            P(),
            P(GRP, SHARD, None, None),
            P(GRP, SHARD),
        ),
        out_specs=P(GRP, SHARD, None, None, None),
        check_vma=False,
    )
```

time: 198 us -> 199 us (level)
  blocking collectives: 54.1 us -> 0 us
  waiting for transfers between devices: 109 us -> 150 us
  starting transfers between devices: 0.04 us -> 10.5 us
  local copies, waits for them, and re-layouts: 6.26 us -> 9.37 us
    all_gather x2 -> x0, blocking collectives: 54.1 us -> none  [the longest x1 37.9 us: local(): lax.all_gather(slot_scale, 'shard', axis=1, tiled=True)]
    all_gather x2, waiting for transfers between devices: 108 us -> 131 us  [the longest x1 86.1 us: local(): full = lax.all_gather(full, 'x', axis=1, tiled=True)]
    all_to_all x0 -> x1, waiting for transfers between devices: none -> 18.8 us  [local(): recv = lax.all_to_all(send, GRP, 0, 0, tiled=True)]
    all_to_all x0 -> x1, starting transfers between devices: none -> 10.4 us  [local(): recv = lax.all_to_all(send, GRP, 0, 0, tiled=True)]
    all_gather x1, local copies, waits for them, and re-layouts: 0.18 us -> 3.37 us  [local(): full = lax.all_gather(slot_rows, 'y', axis=1, tiled=True)]
  transfers between devices with their start and end apart: 2 -> 3, of which waited for: 2 -> 3; matrix products, arithmetic and copies ran while one was open for 2% -> 0% of each run, Pallas kernels for 0% -> 0%
where the time goes in v1:
time: 199 us; the launch traced here: 196 us
  waiting for transfers between devices  150 us (75%)
  between operations  14.2 us (7%)
  starting transfers between devices  10.5 us (5%)
  local copies, waits for them, and re-layouts  9.37 us (5%)
  matrix products  8.15 us (4%)
  other arithmetic  4.69 us (2%)
    all_gather x1, waiting for transfers between devices, local(): full = lax.all_gather(full, 'x', axis=1, tiled=True)  86.1 us
    all_gather x1, waiting for transfers between devices, local(): full = lax.all_gather(slot_rows, 'y', axis=1, tiled=True)  44.6 us
    all_to_all x1, waiting for transfers between devices, local(): recv = lax.all_to_all(send, GRP, 0, 0, tiled=True)  18.8 us
    all_to_all x1, starting transfers between devices, local(): recv = lax.all_to_all(send, GRP, 0, 0, tiled=True)  10.4 us
    dot_general x1, matrix products, local(): jnp.einsum('rd,edc->rec', stacked, weights, preferred_element_type=jnp.fl...  8.15 us
  transfers between devices with their start and end apart: 3, of which 3 were waited for; matrix products, arithmetic and copies ran while one was open for 0% of the time, Pallas kernels for 0%

profile of v1, /device:TPU:6, one launch (start us, length us, event | category | flops | bytes accessed | tf_op | source)
XLA Modules:
  0.0 196.4 jit_solution(11695745111876405396)
XLA Ops:
  6.5 0.7 fusion.10
  7.3 0.8 copy.15
  8.1 1.1 fusion.7
  9.2 0.0 copy-start
  9.2 1.2 gather_fusion
  10.4 1.2 broadcast_select_fusion
  11.6 10.4 %all-to-all-start = ((bf16[16,4,5504]{2,1,0:T(4,128)(2,1)}), bf16[16,4,5504]{2,1,0:T(4,128)(2,1)S(1)}, u32[]{:S(2)}, u32[]{:S(2)}) async-start(bf16[16,4,5504]{2,1,0:T(4,128)(2,1)} %broadcast_select_fusion), calls=%async_computation | async-start | bytes 1409024 | tf_op jit(solution)/shard_map/all_to_all | solution.py:26
  22.1 0.0 all-gather.3.cloned.1.call-start
  22.1 0.0 copy-done
  22.1 0.2 dynamic-slice_reduce_fusion
  22.4 18.8 %all-to-all-done = bf16[16,4,5504]{2,1,0:T(4,128)(2,1)S(1)} async-done(((bf16[16,4,5504]{2,1,0:T(4,128)(2,1)}), bf16[16,4,5504]{2,1,0:T(4,128)(2,1)S(1)}, u32[]{:S(2)}, u32[]{:S(2)}) %all-to-all-start) | async-done | bytes 704544 | tf_op jit(solution)/shard_map/all_to_all | solution.py:26
  41.2 0.8 gather_fusion.1
  42.0 0.2 select_select_fusion
  42.2 0.8 copy.12
  43.0 0.0 all-gather.3.cloned.1.call-update
  43.0 0.0 all-gather.5.cloned.1.call-start
  43.0 44.6 %all-gather.3.cloned.1.call-done = bf16[6,32,5504]{2,0,1:T(8,128)(2,1)} async-done(((bf16[6,4,5504]{2,0,1:T(8,128)(2,1)}), bf16[6,32,5504]{2,0,1:T(8,128)(2,1)}) %all-gather.3.cloned.1.call-update) | async-done | bytes 2113552 | tf_op jit(solution)/shard_map/all_gather | solution.py:34
  87.6 3.4 %copy.13 = bf16[6,32,5504]{2,1,0:T(8,128)(2,1)} copy(bf16[6,32,5504]{2,0,1:T(8,128)(2,1)} %all-gather.3.cloned.1.call-done) | data formatting | bytes 4227072 | tf_op jit(solution)/shard_map/all_gather | solution.py:34
  91.0 0.0 copy-start.1
  91.0 0.0 all-gather.5.cloned.1.call-update
  91.7 0.0 copy-done.1
  91.7 86.1 %all-gather.5.cloned.1.call-done = bf16[6,128,5504]{2,1,0:T(8,128)(2,1)} async-done(((bf16[6,32,5504]{2,1,0:T(8,128)(2,1)}), bf16[6,128,5504]{2,1,0:T(8,128)(2,1)}) %all-gather.5.cloned.1.call-update) | async-done | bytes 8454160 | tf_op jit(solution)/shard_map/all_gather | solution.py:35
  177.8 1.1 slice_reduce_fusion
  178.9 0.6 gather_fusion.2
  179.5 0.1 select_convert_fusion
  179.5 8.1 %fusion = f32[6,128,3,128]{3,1,2,0:T(8,128)S(1)} fusion(bf16[6,128,5504]{2,1,0:T(8,128)(2,1)} %all-gather.5.cloned.1.call-done, bf16[3,5376,128]{2,1,0:T(8,128)(2,1)} %bitcast.44), kind=kOutput, calls=%fused_computation.4 | convolution fusion | flops 3246391296 | bytes 13762560 | tf_op jit(solution)/shard_map/rd,edc->rec/dot_general | solution.py:49
  187.7 0.7 gather_fusion.3
  188.4 1.2 fusion.5
  (10 shorter events, 0.1 us)
Async XLA Ops:
  9.2 12.9 %copy-start = (s32[16,6]{0,1:T(8,128)S(1)}, s32[16,6]{0,1:T(8,128)}, u32[]{:S(2)}) copy-start(s32[16,6]{0,1:T(8,128)} %param.11) | copy-start | bytes 1156
  11.6 29.6 %all-to-all-start = ((bf16[16,4,5504]{2,1,0:T(4,128)(2,1)}), bf16[16,4,5504]{2,1,0:T(4,128)(2,1)S(1)}, u32[]{:S(2)}, u32[]{:S(2)}) async-start(bf16[16,4,5504]{2,1,0:T(4,128)(2,1)} %broadcast_select_fusion), calls=%async_computation | async-start | bytes 1409024 | tf_op jit(solution)/shard_map/all_to_all | solution.py:26
  22.1 65.6 %all-gather.3.cloned.1.call-start = ((), (), s32[]{:S(2)}) async-start(), calls=%async_computation.1 | async-start | bytes 3170304 | tf_op jit(solution)/shard_map/all_gather | solution.py:34
  43.0 134.8 %all-gather.5.cloned.1.call-start = ((), (), s32[]{:S(2)}) async-start(), calls=%async_computation.2 | async-start | bytes 10567680 | tf_op jit(solution)/shard_map/all_gather | solution.py:35
  91.0 0.7 copy-start.1
Sparse Core Ops, SparseCore 0:
  43.1 44.4 all-gather.2
  91.1 86.6 all-gather.4

commit v2 on v1

--- a/solution.py
+++ b/solution.py
@@ -6,18 +6,44 @@
 
 GRP = ("z", "c")
 SHARD = ("x", "y")
+LANES = 128
+
+
+def ring_parts(block, axis, n):
+    parts = [None] * n
+    parts[0] = block
+    left = block
+    right = block
+    up = [(i, (i + 1) % n) for i in range(n)]
+    down = [(i, (i - 1) % n) for i in range(n)]
+    for step in range(1, n // 2 + 1):
+        if 2 * step == n:
+            cols = block.shape[-1]
+            half = (cols // 2) // LANES * LANES
+            got_left = lax.ppermute(left[..., :half], axis, up)
+            got_right = lax.ppermute(right[..., half:], axis, down)
+            parts[step] = jnp.concatenate([got_left, got_right], axis=-1)
+        else:
+            left = lax.ppermute(left, axis, up)
+            right = lax.ppermute(right, axis, down)
+            parts[n - step] = left
+            parts[step] = right
+    return parts
 
 
 def local(src_rows, src_act, encoder, dest_list, pair_list, pair_count):
-    n_grp = lax.psum(1, GRP)
     nb_g = src_rows.shape[0]
     width = src_rows.shape[2]
-    lanes = 128
+    n_x = lax.psum(1, "x")
+    n_y = lax.psum(1, "y")
     my_group = lax.axis_index("z") * lax.psum(1, "c") + lax.axis_index("c")
+    my_x = lax.axis_index("x")
+    my_y = lax.axis_index("y")
 
-    act_block = jnp.zeros(src_act.shape + (lanes,), src_rows.dtype)
+    act_block = jnp.zeros(src_act.shape + (LANES,), src_rows.dtype)
     act_block = act_block.at[:, :, 0].set(src_act)
     rows_ext = jnp.concatenate([src_rows, act_block], axis=-1)
+    ext_width = rows_ext.shape[-1]
 
     is_valid = dest_list >= 0
     from_me = is_valid & (dest_list // nb_g == my_group)
@@ -30,26 +56,47 @@
     source = jnp.where(my_valid, my_list // nb_g, 0)
     slot_rows = jnp.take(recv, source, axis=0)
     slot_rows = jnp.where(my_valid[:, None, None], slot_rows, jnp.zeros((), slot_rows.dtype))
+    slots, rows_dev, _ = slot_rows.shape
 
-    full = lax.all_gather(slot_rows, "y", axis=1, tiled=True)
-    full = lax.all_gather(full, "x", axis=1, tiled=True)
+    split = (ext_width // 2) // LANES * LANES
+    part_a = slot_rows[..., :split]
+    part_b = slot_rows[..., split:]
 
     weights = encoder[0, 0]
-    weights = jnp.pad(weights, ((0, 0), (0, lanes), (0, 0)))
+    enc_count, _, tile_cols = weights.shape
+    enc_a = weights[:, :split, :]
+    enc_b = jnp.pad(weights[:, split:, :], ((0, 0), (0, ext_width - width), (0, 0)))
+
+    def mm(block, enc):
+        flat = block.reshape(-1, block.shape[-1])
+        return jnp.einsum("rd,edc->rec", flat, enc, preferred_element_type=jnp.float32)
+
+    a_x = jnp.stack(ring_parts(part_a, "x", n_x), axis=0)
+    prod_a = [mm(blk, enc_a) for blk in ring_parts(a_x, "y", n_y)]
+    prod_a = jnp.stack(prod_a, axis=0).reshape(n_y, n_x, slots, rows_dev, enc_count, tile_cols)
+
+    b_y = jnp.stack(ring_parts(part_b, "y", n_y), axis=0)
+    b_parts = ring_parts(b_y, "x", n_x)
+    prod_b = [mm(blk, enc_b) for blk in b_parts]
+    prod_b = jnp.stack(prod_b, axis=0).reshape(n_x, n_y, slots, rows_dev, enc_count, tile_cols)
+    scale_b = jnp.stack([blk[..., width - split] for blk in b_parts], axis=0)
+
+    products = prod_a + jnp.transpose(prod_b, (1, 0, 2, 3, 4, 5))
+
     dev_pairs = pair_list[0, 0]
     slot_ids = dev_pairs[:, 0]
     block_ids = dev_pairs[:, 1]
     amount = pair_count[0, 0]
-    slots_total, tile_rows, ext_width = full.shape
-    enc_count = weights.shape[0]
-    tile_cols = weights.shape[2]
     pair_total = dev_pairs.shape[0]
-    full_scale = full[:, :, width]
-    stacked = full.reshape(slots_total * tile_rows, ext_width)
-    products = jnp.einsum("rd,edc->rec", stacked, weights, preferred_element_type=jnp.float32)
-    products = products.reshape(slots_total, tile_rows, enc_count, tile_cols)
-    chosen = products[slot_ids, :, block_ids, :]
-    scales = jnp.take(full_scale, slot_ids, axis=0).astype(jnp.float32)
+
+    rows_all = jnp.arange(n_x * n_y * rows_dev)
+    rr = rows_all % rows_dev
+    shard_abs = rows_all // rows_dev
+    kx = (shard_abs // n_y - my_x) % n_x
+    ky = (shard_abs % n_y - my_y) % n_y
+
+    chosen = products[ky[None, :], kx[None, :], slot_ids[:, None], rr[None, :], block_ids[:, None], :]
+    scales = scale_b[kx[None, :], ky[None, :], slot_ids[:, None], rr[None, :]].astype(jnp.float32)
     is_live = jnp.arange(pair_total) < amount
     result = jnp.where(
         is_live[:, None, None], scales[:, :, None] * chosen, jnp.zeros((), jnp.float32)

time: 199 us -> 231 us (1.16)
  waiting for transfers between devices: 150 us -> 37.2 us
  starting transfers between devices: 10.5 us -> 96.8 us
  local copies, waits for them, and re-layouts: 9.37 us -> 64.8 us
  matrix products: 8.15 us -> 22.5 us
  between operations: 14.2 us -> 1.39 us
    all_gather x2 -> x0, waiting for transfers between devices: 131 us -> none  [the longest x1 86.1 us: local(): full = lax.all_gather(full, 'x', axis=1, tiled=True)]
    ppermute x0 -> x24, starting transfers between devices: none -> 86.4 us  [the longest x8 37 us: ring_parts(): right = lax.ppermute(right, axis, down)]
    gather x2, local copies, waits for them, and re-layouts: 1.23 us -> 40.8 us  [the longest x1 24.8 us: local(): scale_b[kx[None, :], ky[None, :], slot_ids[:, None], rr[None, :]]]
    ppermute x0 -> x24, waiting for transfers between devices: none -> 20.9 us  [the longest x8 13.7 us: ring_parts(): left = lax.ppermute(left, axis, up)]
    dot_general x1 -> x12, matrix products: 8.15 us -> 22.5 us  [mm(): jnp.einsum('rd,edc->rec', flat, enc, preferred_element_type=jnp.float32)]
    slice x1 -> x15, local copies, waits for them, and re-layouts: 1.07 us -> 10.9 us  [the longest x5 3.32 us: local(): scale_b = jnp.stack([blk[..., width - split] for blk in b_parts], axis=0)]
    another operation x0 -> x9, local copies, waits for them, and re-layouts: none -> 4.37 us  [the longest x2 1.59 us: local(): b_y = jnp.stack(ring_parts(part_b, 'y', n_y), axis=0)]
    unnamed x5 -> x30, local copies, waits for them, and re-layouts: 0.81 us -> 4.51 us
  transfers between devices with their start and end apart: 3 -> 25, of which waited for: 3 -> 7; matrix products, arithmetic and copies ran while one was open for 0% -> 29% of each run, Pallas kernels for 0% -> 0%
where the time goes in v2:
time: 231 us; the launch traced here: 229 us
  starting transfers between devices  96.8 us (42%)
  local copies, waits for them, and re-layouts  64.8 us (28%)
  waiting for transfers between devices  37.2 us (16%)
  matrix products  22.5 us (10%)
  other arithmetic  6.67 us (3%)
    ppermute x8, starting transfers between devices, ring_parts(): right = lax.ppermute(right, axis, down)  37 us
    gather x1, local copies, waits for them, and re-layouts, local(): scale_b[kx[None, :], ky[None, :], slot_ids[:, None], rr[None, :]]  24.8 us
    dot_general x12, matrix products, mm(): jnp.einsum('rd,edc->rec', flat, enc, preferred_element_type=jnp.float32)  22.5 us
    ppermute x8, starting transfers between devices, ring_parts(): left = lax.ppermute(left, axis, up)  21 us
    all_to_all x1, waiting for transfers between devices, local(): recv = lax.all_to_all(send, GRP, 0, 0, tiled=True)  16.4 us
    gather x1, local copies, waits for them, and re-layouts, local(): products[ky[None, :], kx[None, :], slot_ids[:, None], rr[None, :], block_...  15.9 us
    ppermute x4, starting transfers between devices, ring_parts(): got_right = lax.ppermute(right[..., half:], axis, down)  14.3 us
    ppermute x4, starting transfers between devices, ring_parts(): got_left = lax.ppermute(left[..., :half], axis, up)  14.1 us
  transfers between devices with their start and end apart: 25, of which 7 were waited for; matrix products, arithmetic and copies ran while one was open for 29% of the time, Pallas kernels for 0%

profile of v2, /device:TPU:6, one launch (start us, length us, event | category | flops | bytes accessed | tf_op | source)
XLA Modules:
  0.0 229.3 jit_solution(3734769146950722566)
XLA Ops:
  0.0 0.7 fusion.49
  0.7 0.8 copy.131
  1.5 1.1 fusion.44
  2.7 1.2 gather_fusion
  3.9 1.3 broadcast_select_fusion
  5.1 10.4 %all-to-all-start = ((bf16[16,4,5504]{2,1,0:T(4,128)(2,1)}), bf16[16,4,5504]{2,1,0:T(4,128)(2,1)S(1)}, u32[]{:S(2)}, u32[]{:S(2)}) async-start(bf16[16,4,5504]{2,1,0:T(4,128)(2,1)} %broadcast_select_fusion), calls=%async_computation | async-start | bytes 1409024 | tf_op jit(solution)/shard_map/all_to_all | solution.py:52
  15.7 1.7 slice.118
  18.3 16.4 %all-to-all-done = bf16[16,4,5504]{2,1,0:T(4,128)(2,1)S(1)} async-done(((bf16[16,4,5504]{2,1,0:T(4,128)(2,1)}), bf16[16,4,5504]{2,1,0:T(4,128)(2,1)S(1)}, u32[]{:S(2)}, u32[]{:S(2)}) %all-to-all-start) | async-done | bytes 704544 | tf_op jit(solution)/shard_map/all_to_all | solution.py:52
  34.7 0.8 gather_fusion.1
  35.7 3.0 %collective-permute-start.11 = (bf16[6,4,2688]{2,0,1:T(8,128)(2,1)S(1)}, bf16[6,4,2688]{2,0,1:T(8,128)(2,1)S(1)}, u32[]{:S(2)}, u32[]{:S(2)}) collective-permute-start(bf16[6,4,2688]{2,0,1:T(8,128)(2,1)S(1)} %get-tuple-element.18), channel_id=1, source_target_pairs={{0,24},{8,0},{16,8},{24,16},{1,25},{9,1},{17,9},{25,17},{2,26},{10... | collective-permute-start | bytes 387080 | tf_op jit(solution)/shard_map/ppermute | solution.py:28
  38.7 4.3 %collective-permute-start.12 = (bf16[6,4,2688]{2,0,1:T(8,128)(2,1)S(1)}, bf16[6,4,2688]{2,0,1:T(8,128)(2,1)S(1)}, u32[]{:S(2)}, u32[]{:S(2)}) collective-permute-start(bf16[6,4,2688]{2,0,1:T(8,128)(2,1)S(1)} %get-tuple-element.18), channel_id=1, source_target_pairs={{0,8},{8,16},{16,24},{24,0},{1,9},{9,17},{17,25},{25,1},{2,10},{10... | collective-permute-start | bytes 387080 | tf_op jit(solution)/shard_map/ppermute | solution.py:27
  43.0 5.4 %collective-permute-start = (bf16[6,4,2816]{2,0,1:T(8,128)(2,1)S(1)}, bf16[6,4,2816]{2,0,1:T(8,128)(2,1)S(1)}, u32[]{:S(2)}, u32[]{:S(2)}) collective-permute-start(bf16[6,4,2816]{2,0,1:T(8,128)(2,1)S(1)} %slice.104), channel_id=1, source_target_pairs={{0,7},{1,0},{2,1},{3,2},{4,3},{5,4},{6,5},{7,6},{8,15},{9,8},{10,9... | collective-permute-start | bytes 405512 | tf_op jit(solution)/shard_map/ppermute | solution.py:28
  48.4 1.9 collective-permute-start.3
  50.3 1.9 collective-permute-start.14
  52.3 5.1 %collective-permute-start.13 = (bf16[6,4,1280]{2,0,1:T(8,128)(2,1)S(1)}, bf16[6,4,1280]{2,0,1:T(8,128)(2,1)S(1)}, u32[]{:S(2)}, u32[]{:S(2)}) collective-permute-start(bf16[6,4,1280]{2,0,1:T(8,128)(2,1)S(1)} %slice.113), channel_id=1, source_target_pairs={{0,8},{8,16},{16,24},{24,0},{1,9},{9,17},{17,25},{25,1},{2,10},{10... | collective-permute-start | bytes 184328 | tf_op jit(solution)/shard_map/ppermute | solution.py:23
  57.5 5.1 %collective-permute-start.1 = (bf16[6,4,2816]{2,0,1:T(8,128)(2,1)S(1)}, bf16[6,4,2816]{2,0,1:T(8,128)(2,1)S(1)}, u32[]{:S(2)}, u32[]{:S(2)}) collective-permute-start(bf16[6,4,2816]{2,0,1:T(8,128)(2,1)S(1)} %collective-permute-done), channel_id=1, source_target_pairs={{0,7},{1,0},{2,1},{3,2},{4,3},{5,4},{6,5},{7,6},{8,15},{9,8},{10,9... | collective-permute-start | bytes 405512 | tf_op jit(solution)/shard_map/ppermute | solution.py:28
  62.6 1.9 collective-permute-start.4
  64.9 1.4 fusion.25
  66.3 1.0 copy.73
  67.2 5.1 %collective-permute-start.15 = (bf16[4,6,4,2688]{3,2,1,0:T(4,128)(2,1)}, bf16[4,6,4,2688]{3,2,1,0:T(4,128)(2,1)}, u32[]{:S(2)}, u32[]{:S(2)}) collective-permute-start(bf16[4,6,4,2688]{3,2,1,0:T(4,128)(2,1)} %copy.73), channel_id=1, source_target_pairs={{0,7},{1,0},{2,1},{3,2},{4,3},{5,4},{6,5},{7,6},{8,15},{9,8},{10,9... | collective-permute-start | bytes 1548296 | tf_op jit(solution)/shard_map/ppermute | solution.py:28
  72.4 1.9 collective-permute-start.18
  74.3 5.1 %collective-permute-start.2 = (bf16[6,4,2816]{2,0,1:T(8,128)(2,1)S(1)}, bf16[6,4,2816]{2,0,1:T(8,128)(2,1)S(1)}, u32[]{:S(2)}, u32[]{:S(2)}) collective-permute-start(bf16[6,4,2816]{2,0,1:T(8,128)(2,1)S(1)} %collective-permute-done.1), channel_id=1, source_target_pairs={{0,7},{1,0},{2,1},{3,2},{4,3},{5,4},{6,5},{7,6},{8,15},{9,8},{10,9... | collective-permute-start | bytes 405512 | tf_op jit(solution)/shard_map/ppermute | solution.py:28
  79.5 1.9 collective-permute-start.5
  81.4 11.5 %collective-permute-done.5 = bf16[6,4,2816]{2,0,1:T(8,128)(2,1)S(1)} collective-permute-done((bf16[6,4,2816]{2,0,1:T(8,128)(2,1)S(1)}, bf16[6,4,2816]{2,0,1:T(8,128)(2,1)S(1)}, u32[]{:S(2)}, u32[]{:S(2)}) %collective-permute-start.5) | collective-permute-done | bytes 135200 | tf_op jit(solution)/shard_map/ppermute | solution.py:27
  93.0 1.9 collective-permute-start.6
  94.9 5.1 %collective-permute-start.7 = (bf16[6,4,1408]{2,0,1:T(8,128)(2,1)S(1)}, bf16[6,4,1408]{2,0,1:T(8,128)(2,1)S(1)}, u32[]{:S(2)}, u32[]{:S(2)}) collective-permute-start(bf16[6,4,1408]{2,0,1:T(8,128)(2,1)S(1)} %slice.106), channel_id=1, source_target_pairs={{0,7},{1,0},{2,1},{3,2},{4,3},{5,4},{6,5},{7,6},{8,15},{9,8},{10,9... | collective-permute-start | bytes 202760 | tf_op jit(solution)/shard_map/ppermute | solution.py:24
  100.6 1.6 collective-permute-done.7
  102.3 1.6 copy.67
  103.8 1.9 collective-permute-start.8
  105.8 5.1 %collective-permute-start.10 = (bf16[8,6,4,2816]{3,0,2,1:T(8,128)(2,1)}, bf16[8,6,4,2816]{3,0,2,1:T(8,128)(2,1)}, u32[]{:S(2)}, u32[]{:S(2)}) collective-permute-start(bf16[8,6,4,2816]{3,0,2,1:T(8,128)(2,1)} %copy.67), channel_id=1, source_target_pairs={{0,8},{8,16},{16,24},{24,0},{1,9},{9,17},{17,25},{25,1},{2,10},{10... | collective-permute-start | bytes 3244040 | tf_op jit(solution)/shard_map/ppermute | solution.py:27
  111.5 1.1 copy.66
  112.7 2.0 fusion.16
  114.8 5.8 %collective-permute-start.16 = (bf16[4,6,4,2688]{3,2,1,0:T(4,128)(2,1)}, bf16[4,6,4,2688]{3,2,1,0:T(4,128)(2,1)}, u32[]{:S(2)}, u32[]{:S(2)}) collective-permute-start(bf16[4,6,4,2688]{3,2,1,0:T(4,128)(2,1)} %collective-permute-done.15), channel_id=1, source_target_pairs={{0,7},{1,0},{2,1},{3,2},{4,3},{5,4},{6,5},{7,6},{8,15},{9,8},{10,9... | collective-permute-start | bytes 1548296 | tf_op jit(solution)/shard_map/ppermute | solution.py:28
  120.5 2.4 %fusion.42 = f32[4,6,4,3,128]{4,2,3,1,0:T(4,128)S(1)} fusion(bf16[4,6,4,2688]{3,2,1,0:T(4,128)(2,1)} %collective-permute-done.15, bf16[3,5376,128]{2,1,0:T(8,128)(2,1)} %bitcast.190), kind=kOutput, calls=%fused_computation.50 | convolution fusion | flops 198180864 | bytes 2727936 | tf_op jit(solution)/shard_map/rd,edc->rec/dot_general | solution.py:72
  122.9 1.9 collective-permute-start.19
  124.9 2.4 %fusion.32 = f32[4,6,4,3,128]{4,2,3,1,0:T(4,128)} fusion(bf16[4,6,4,2688]{3,2,1,0:T(4,128)(2,1)} %collective-permute-done.18, bf16[3,5376,128]{2,1,0:T(8,128)(2,1)S(1)} %bitcast.192), kind=kOutput, calls=%fused_computation.40 | convolution fusion | flops 198180864 | bytes 2727936 | tf_op jit(solution)/shard_map/rd,edc->rec/dot_general | solution.py:72
  127.9 0.9 collective-permute-done.16
  128.9 5.6 %collective-permute-start.17 = (bf16[4,6,4,2688]{3,2,1,0:T(4,128)(2,1)}, bf16[4,6,4,2688]{3,2,1,0:T(4,128)(2,1)}, u32[]{:S(2)}, u32[]{:S(2)}) collective-permute-start(bf16[4,6,4,2688]{3,2,1,0:T(4,128)(2,1)} %collective-permute-done.16), channel_id=1, source_target_pairs={{0,7},{1,0},{2,1},{3,2},{4,3},{5,4},{6,5},{7,6},{8,15},{9,8},{10,9... | collective-permute-start | bytes 1548296 | tf_op jit(solution)/shard_map/ppermute | solution.py:28
  134.5 2.1 collective-permute-done.19
  136.6 1.9 collective-permute-start.20
  138.5 1.7 fusion.40
  141.0 2.4 %fusion.34 = f32[4,6,4,3,128]{4,2,3,1,0:T(4,128)} fusion(bf16[4,6,4,2688]{3,2,1,0:T(4,128)(2,1)} %collective-permute-done.19, bf16[3,5376,128]{2,1,0:T(8,128)(2,1)S(1)} %bitcast.194), kind=kOutput, calls=%fused_computation.42 | convolution fusion | flops 198180864 | bytes 2727936 | tf_op jit(solution)/shard_map/rd,edc->rec/dot_general | solution.py:72
  143.3 1.9 slice.109
  145.2 1.9 collective-permute-start.9
  147.1 0.8 slice.108
  148.3 0.8 slice.111
  149.4 1.9 slice.119
  151.3 5.1 %collective-permute-start.23 = (bf16[8,6,4,1408]{3,0,2,1:T(8,128)(2,1)}, bf16[8,6,4,1408]{3,0,2,1:T(8,128)(2,1)}, u32[]{:S(2)}, u32[]{:S(2)}) collective-permute-start(bf16[8,6,4,1408]{3,0,2,1:T(8,128)(2,1)} %slice.119), channel_id=1, source_target_pairs={{0,8},{8,16},{16,24},{24,0},{1,9},{9,17},{17,25},{25,1},{2,10},{10... | collective-permute-start | bytes 1622024 | tf_op jit(solution)/shard_map/ppermute | solution.py:23
  156.4 2.0 fusion.4
  158.6 2.1 fusion
  160.9 1.0 slice.117
  162.0 5.3 %collective-permute-start.22 = (bf16[4,6,4,1408]{3,1,2,0:T(8,128)(2,1)S(1)}, bf16[4,6,4,1408]{3,1,2,0:T(8,128)(2,1)S(1)}, u32[]{:S(2)}, u32[]{:S(2)}) collective-permute-start(bf16[4,6,4,1408]{3,1,2,0:T(8,128)(2,1)S(1)} %copy.130), channel_id=1, source_target_pairs={{0,7},{1,0},{2,1},{3,2},{4,3},{5,4},{6,5},{7,6},{8,15},{9,8},{10,9... | collective-permute-start | bytes 811016 | tf_op jit(solution)/shard_map/ppermute | solution.py:24
  167.3 1.0 slice.116
  168.4 1.9 collective-permute-start.21
  170.3 1.7 fusion.38
  172.0 1.7 fusion.36
  174.5 4.1 %collective-permute-done.21 = bf16[4,6,4,1280]{3,1,2,0:T(8,128)(2,1)S(1)} collective-permute-done((bf16[4,6,4,1280]{3,1,2,0:T(8,128)(2,1)S(1)}, bf16[4,6,4,1280]{3,1,2,0:T(8,128)(2,1)S(1)}, u32[]{:S(2)}, u32[]{:S(2)}) %collective-permute-start.21) | collective-permute-done | bytes 245792 | tf_op jit(solution)/shard_map/ppermute | solution.py:23
  178.6 1.4 fusion.24
  182.5 24.8 %gather_fusion.2 = bf16[2304]{0:T(1024)(128)(2,1)S(1)} fusion(bf16[4,8,6,4]{2,3,1,0:T(4,128)(2,1)S(1)} %pad_maximum_fusion.1, s32[2304]{0:T(1024)S(1)} %get-tuple-element.19), kind=kCustom, calls=%fused_computation.2 | custom fusion | bytes 46080 | tf_op jit(solution)/shard_map/gather | solution.py:99
  207.6 1.2 copy.84
  208.8 1.3 fusion.21
  210.1 1.7 fusion.8
  212.1 15.9 %gather_fusion.3 = f32[2304,128]{1,0:T(8,128)S(1)} fusion(f32[8,4,6,4,3,128]{5,3,4,2,1,0:T(4,128)S(1)} %copy.87, s32[2304]{0:T(1024)S(1)} %get-tuple-element.20), kind=kCustom, calls=%fused_computation.3 | custom fusion | bytes 2405376 | tf_op jit(solution)/shard_map/gather | solution.py:98
  228.1 1.2 select_convert_fusion
  (84 shorter events, 8.4 us)
Async XLA Ops:
  3.8 11.7 %copy-start.6 = (s32[16,6]{0,1:T(8,128)S(1)}, s32[16,6]{0,1:T(8,128)}, u32[]{:S(2)}) copy-start(s32[16,6]{0,1:T(8,128)} %param.11) | copy-start | bytes 1156
  5.1 29.6 %all-to-all-start = ((bf16[16,4,5504]{2,1,0:T(4,128)(2,1)}), bf16[16,4,5504]{2,1,0:T(4,128)(2,1)S(1)}, u32[]{:S(2)}, u32[]{:S(2)}) async-start(bf16[16,4,5504]{2,1,0:T(4,128)(2,1)} %broadcast_select_fusion), calls=%async_computation | async-start | bytes 1409024 | tf_op jit(solution)/shard_map/all_to_all | solution.py:52
  15.7 2.5 %copy-start.7 = (s32[1,1,18,2]{2,3,1,0:T(2,128)S(1)}, s32[1,1,18,2]{2,3,1,0:T(2,128)}, u32[]{:S(2)}) copy-start(s32[1,1,18,2]{2,3,1,0:T(2,128)} %param.12) | copy-start | bytes 436
  35.5 29.4 %copy-start = (bf16[1,1,3,5376,128]{4,3,2,1,0:T(8,128)(2,1)S(1)}, bf16[1,1,3,5376,128]{4,3,2,1,0:T(8,128)(2,1)}, u32[]{:S(2)}) copy-start(bf16[1,1,3,5376,128]{4,3,2,1,0:T(8,128)(2,1)} %param.10) | copy-start | bytes 12386308
  35.7 14.7 %collective-permute-start.11 = (bf16[6,4,2688]{2,0,1:T(8,128)(2,1)S(1)}, bf16[6,4,2688]{2,0,1:T(8,128)(2,1)S(1)}, u32[]{:S(2)}, u32[]{:S(2)}) collective-permute-start(bf16[6,4,2688]{2,0,1:T(8,128)(2,1)S(1)} %get-tuple-element.18), channel_id=1, source_target_pairs={{0,24},{8,0},{16,8},{24,16},{1,25},{9,1},{17,9},{25,17},{2,26},{10... | collective-permute-start | bytes 387080 | tf_op jit(solution)/shard_map/ppermute | solution.py:28
  38.7 13.6 %collective-permute-start.12 = (bf16[6,4,2688]{2,0,1:T(8,128)(2,1)S(1)}, bf16[6,4,2688]{2,0,1:T(8,128)(2,1)S(1)}, u32[]{:S(2)}, u32[]{:S(2)}) collective-permute-start(bf16[6,4,2688]{2,0,1:T(8,128)(2,1)S(1)} %get-tuple-element.18), channel_id=1, source_target_pairs={{0,8},{8,16},{16,24},{24,0},{1,9},{9,17},{17,25},{25,1},{2,10},{10... | collective-permute-start | bytes 387080 | tf_op jit(solution)/shard_map/ppermute | solution.py:27
  43.0 14.5 %collective-permute-start = (bf16[6,4,2816]{2,0,1:T(8,128)(2,1)S(1)}, bf16[6,4,2816]{2,0,1:T(8,128)(2,1)S(1)}, u32[]{:S(2)}, u32[]{:S(2)}) collective-permute-start(bf16[6,4,2816]{2,0,1:T(8,128)(2,1)S(1)} %slice.104), channel_id=1, source_target_pairs={{0,7},{1,0},{2,1},{3,2},{4,3},{5,4},{6,5},{7,6},{8,15},{9,8},{10,9... | collective-permute-start | bytes 405512 | tf_op jit(solution)/shard_map/ppermute | solution.py:28
  48.4 14.2 %collective-permute-start.3 = (bf16[6,4,2816]{2,0,1:T(8,128)(2,1)S(1)}, bf16[6,4,2816]{2,0,1:T(8,128)(2,1)S(1)}, u32[]{:S(2)}, u32[]{:S(2)}) collective-permute-start(bf16[6,4,2816]{2,0,1:T(8,128)(2,1)S(1)} %slice.104), channel_id=1, source_target_pairs={{0,1},{1,2},{2,3},{3,4},{4,5},{5,6},{6,7},{7,0},{8,9},{9,10},{10,1... | collective-permute-start | bytes 405512 | tf_op jit(solution)/shard_map/ppermute | solution.py:27
  50.3 14.2 %collective-permute-start.14 = (bf16[6,4,1408]{2,0,1:T(8,128)(2,1)S(1)}, bf16[6,4,1408]{2,0,1:T(8,128)(2,1)S(1)}, u32[]{:S(2)}, u32[]{:S(2)}) collective-permute-start(bf16[6,4,1408]{2,0,1:T(8,128)(2,1)S(1)} %slice.114), channel_id=1, source_target_pairs={{0,24},{8,0},{16,8},{24,16},{1,25},{9,1},{17,9},{25,17},{2,26},{10... | collective-permute-start | bytes 202760 | tf_op jit(solution)/shard_map/ppermute | solution.py:24
  52.3 12.3 %collective-permute-start.13 = (bf16[6,4,1280]{2,0,1:T(8,128)(2,1)S(1)}, bf16[6,4,1280]{2,0,1:T(8,128)(2,1)S(1)}, u32[]{:S(2)}, u32[]{:S(2)}) collective-permute-start(bf16[6,4,1280]{2,0,1:T(8,128)(2,1)S(1)} %slice.113), channel_id=1, source_target_pairs={{0,8},{8,16},{16,24},{24,0},{1,9},{9,17},{17,25},{25,1},{2,10},{10... | collective-permute-start | bytes 184328 | tf_op jit(solution)/shard_map/ppermute | solution.py:23
  57.5 16.9 %collective-permute-start.1 = (bf16[6,4,2816]{2,0,1:T(8,128)(2,1)S(1)}, bf16[6,4,2816]{2,0,1:T(8,128)(2,1)S(1)}, u32[]{:S(2)}, u32[]{:S(2)}) collective-permute-start(bf16[6,4,2816]{2,0,1:T(8,128)(2,1)S(1)} %collective-permute-done), channel_id=1, source_target_pairs={{0,7},{1,0},{2,1},{3,2},{4,3},{5,4},{6,5},{7,6},{8,15},{9,8},{10,9... | collective-permute-start | bytes 405512 | tf_op jit(solution)/shard_map/ppermute | solution.py:28
  62.6 16.8 %collective-permute-start.4 = (bf16[6,4,2816]{2,0,1:T(8,128)(2,1)S(1)}, bf16[6,4,2816]{2,0,1:T(8,128)(2,1)S(1)}, u32[]{:S(2)}, u32[]{:S(2)}) collective-permute-start(bf16[6,4,2816]{2,0,1:T(8,128)(2,1)S(1)} %collective-permute-done.3), channel_id=1, source_target_pairs={{0,1},{1,2},{2,3},{3,4},{4,5},{5,6},{6,7},{7,0},{8,9},{9,10},{10,1... | collective-permute-start | bytes 405512 | tf_op jit(solution)/shard_map/ppermute | solution.py:27
  67.2 47.5 %collective-permute-start.15 = (bf16[4,6,4,2688]{3,2,1,0:T(4,128)(2,1)}, bf16[4,6,4,2688]{3,2,1,0:T(4,128)(2,1)}, u32[]{:S(2)}, u32[]{:S(2)}) collective-permute-start(bf16[4,6,4,2688]{3,2,1,0:T(4,128)(2,1)} %copy.73), channel_id=1, source_target_pairs={{0,7},{1,0},{2,1},{3,2},{4,3},{5,4},{6,5},{7,6},{8,15},{9,8},{10,9... | collective-permute-start | bytes 1548296 | tf_op jit(solution)/shard_map/ppermute | solution.py:28
  72.4 50.6 %collective-permute-start.18 = (bf16[4,6,4,2688]{3,2,1,0:T(4,128)(2,1)}, bf16[4,6,4,2688]{3,2,1,0:T(4,128)(2,1)}, u32[]{:S(2)}, u32[]{:S(2)}) collective-permute-start(bf16[4,6,4,2688]{3,2,1,0:T(4,128)(2,1)} %copy.73), channel_id=1, source_target_pairs={{0,1},{1,2},{2,3},{3,4},{4,5},{5,6},{6,7},{7,0},{8,9},{9,10},{10,1... | collective-permute-start | bytes 1548296 | tf_op jit(solution)/shard_map/ppermute | solution.py:27
  74.3 20.6 %collective-permute-start.2 = (bf16[6,4,2816]{2,0,1:T(8,128)(2,1)S(1)}, bf16[6,4,2816]{2,0,1:T(8,128)(2,1)S(1)}, u32[]{:S(2)}, u32[]{:S(2)}) collective-permute-start(bf16[6,4,2816]{2,0,1:T(8,128)(2,1)S(1)} %collective-permute-done.1), channel_id=1, source_target_pairs={{0,7},{1,0},{2,1},{3,2},{4,3},{5,4},{6,5},{7,6},{8,15},{9,8},{10,9... | collective-permute-start | bytes 405512 | tf_op jit(solution)/shard_map/ppermute | solution.py:28
  79.5 13.5 %collective-permute-start.5 = (bf16[6,4,2816]{2,0,1:T(8,128)(2,1)S(1)}, bf16[6,4,2816]{2,0,1:T(8,128)(2,1)S(1)}, u32[]{:S(2)}, u32[]{:S(2)}) collective-permute-start(bf16[6,4,2816]{2,0,1:T(8,128)(2,1)S(1)} %collective-permute-done.4), channel_id=1, source_target_pairs={{0,1},{1,2},{2,3},{3,4},{4,5},{5,6},{6,7},{7,0},{8,9},{9,10},{10,1... | collective-permute-start | bytes 405512 | tf_op jit(solution)/shard_map/ppermute | solution.py:27
  93.0 7.6 %collective-permute-start.6 = (bf16[6,4,1408]{2,0,1:T(8,128)(2,1)S(1)}, bf16[6,4,1408]{2,0,1:T(8,128)(2,1)S(1)}, u32[]{:S(2)}, u32[]{:S(2)}) collective-permute-start(bf16[6,4,1408]{2,0,1:T(8,128)(2,1)S(1)} %slice.105), channel_id=1, source_target_pairs={{0,1},{1,2},{2,3},{3,4},{4,5},{5,6},{6,7},{7,0},{8,9},{9,10},{10,1... | collective-permute-start | bytes 202760 | tf_op jit(solution)/shard_map/ppermute | solution.py:23
  94.9 7.3 %collective-permute-start.7 = (bf16[6,4,1408]{2,0,1:T(8,128)(2,1)S(1)}, bf16[6,4,1408]{2,0,1:T(8,128)(2,1)S(1)}, u32[]{:S(2)}, u32[]{:S(2)}) collective-permute-start(bf16[6,4,1408]{2,0,1:T(8,128)(2,1)S(1)} %slice.106), channel_id=1, source_target_pairs={{0,7},{1,0},{2,1},{3,2},{4,3},{5,4},{6,5},{7,6},{8,15},{9,8},{10,9... | collective-permute-start | bytes 202760 | tf_op jit(solution)/shard_map/ppermute | solution.py:24
  103.8 39.5 %collective-permute-start.8 = (bf16[8,6,4,2816]{3,0,2,1:T(8,128)(2,1)}, bf16[8,6,4,2816]{3,0,2,1:T(8,128)(2,1)}, u32[]{:S(2)}, u32[]{:S(2)}) collective-permute-start(bf16[8,6,4,2816]{3,0,2,1:T(8,128)(2,1)} %copy.67), channel_id=1, source_target_pairs={{0,24},{8,0},{16,8},{24,16},{1,25},{9,1},{17,9},{25,17},{2,26},{10... | collective-permute-start | bytes 3244040 | tf_op jit(solution)/shard_map/ppermute | solution.py:28
  105.8 42.5 %collective-permute-start.10 = (bf16[8,6,4,2816]{3,0,2,1:T(8,128)(2,1)}, bf16[8,6,4,2816]{3,0,2,1:T(8,128)(2,1)}, u32[]{:S(2)}, u32[]{:S(2)}) collective-permute-start(bf16[8,6,4,2816]{3,0,2,1:T(8,128)(2,1)} %copy.67), channel_id=1, source_target_pairs={{0,8},{8,16},{16,24},{24,0},{1,9},{9,17},{17,25},{25,1},{2,10},{10... | collective-permute-start | bytes 3244040 | tf_op jit(solution)/shard_map/ppermute | solution.py:27
  114.8 10.1 %copy-start.1 = (bf16[1,1,3,5376,128]{4,3,2,1,0:T(8,128)(2,1)S(1)}, bf16[1,1,3,5376,128]{4,3,2,1,0:T(8,128)(2,1)}, u32[]{:S(2)}) copy-start(bf16[1,1,3,5376,128]{4,3,2,1,0:T(8,128)(2,1)} %param.10) | copy-start | bytes 12386308
  114.8 14.1 %collective-permute-start.16 = (bf16[4,6,4,2688]{3,2,1,0:T(4,128)(2,1)}, bf16[4,6,4,2688]{3,2,1,0:T(4,128)(2,1)}, u32[]{:S(2)}, u32[]{:S(2)}) collective-permute-start(bf16[4,6,4,2688]{3,2,1,0:T(4,128)(2,1)} %collective-permute-done.15), channel_id=1, source_target_pairs={{0,7},{1,0},{2,1},{3,2},{4,3},{5,4},{6,5},{7,6},{8,15},{9,8},{10,9... | collective-permute-start | bytes 1548296 | tf_op jit(solution)/shard_map/ppermute | solution.py:28
  122.9 13.7 %collective-permute-start.19 = (bf16[4,6,4,2688]{3,2,1,0:T(4,128)(2,1)}, bf16[4,6,4,2688]{3,2,1,0:T(4,128)(2,1)}, u32[]{:S(2)}, u32[]{:S(2)}) collective-permute-start(bf16[4,6,4,2688]{3,2,1,0:T(4,128)(2,1)} %collective-permute-done.18), channel_id=1, source_target_pairs={{0,1},{1,2},{2,3},{3,4},{4,5},{5,6},{6,7},{7,0},{8,9},{9,10},{10,1... | collective-permute-start | bytes 1548296 | tf_op jit(solution)/shard_map/ppermute | solution.py:27
  128.9 32.0 %collective-permute-start.17 = (bf16[4,6,4,2688]{3,2,1,0:T(4,128)(2,1)}, bf16[4,6,4,2688]{3,2,1,0:T(4,128)(2,1)}, u32[]{:S(2)}, u32[]{:S(2)}) collective-permute-start(bf16[4,6,4,2688]{3,2,1,0:T(4,128)(2,1)} %collective-permute-done.16), channel_id=1, source_target_pairs={{0,7},{1,0},{2,1},{3,2},{4,3},{5,4},{6,5},{7,6},{8,15},{9,8},{10,9... | collective-permute-start | bytes 1548296 | tf_op jit(solution)/shard_map/ppermute | solution.py:28
  136.6 30.7 %collective-permute-start.20 = (bf16[4,6,4,2688]{3,2,1,0:T(4,128)(2,1)}, bf16[4,6,4,2688]{3,2,1,0:T(4,128)(2,1)}, u32[]{:S(2)}, u32[]{:S(2)}) collective-permute-start(bf16[4,6,4,2688]{3,2,1,0:T(4,128)(2,1)} %collective-permute-done.19), channel_id=1, source_target_pairs={{0,1},{1,2},{2,3},{3,4},{4,5},{5,6},{6,7},{7,0},{8,9},{9,10},{10,1... | collective-permute-start | bytes 1548296 | tf_op jit(solution)/shard_map/ppermute | solution.py:27
  145.2 36.9 %collective-permute-start.9 = (bf16[8,6,4,1408]{3,0,2,1:T(8,128)(2,1)}, bf16[8,6,4,1408]{3,0,2,1:T(8,128)(2,1)S(1)}, u32[]{:S(2)}, u32[]{:S(2)}) collective-permute-start(bf16[8,6,4,1408]{3,0,2,1:T(8,128)(2,1)} %slice.109), channel_id=1, source_target_pairs={{0,24},{8,0},{16,8},{24,16},{1,25},{9,1},{17,9},{25,17},{2,26},{10... | collective-permute-start | bytes 1622024 | tf_op jit(solution)/shard_map/ppermute | solution.py:24
  151.3 56.3 %collective-permute-start.23 = (bf16[8,6,4,1408]{3,0,2,1:T(8,128)(2,1)}, bf16[8,6,4,1408]{3,0,2,1:T(8,128)(2,1)}, u32[]{:S(2)}, u32[]{:S(2)}) collective-permute-start(bf16[8,6,4,1408]{3,0,2,1:T(8,128)(2,1)} %slice.119), channel_id=1, source_target_pairs={{0,8},{8,16},{16,24},{24,0},{1,9},{9,17},{17,25},{25,1},{2,10},{10... | collective-permute-start | bytes 1622024 | tf_op jit(solution)/shard_map/ppermute | solution.py:23
  158.6 11.8 %copy-start.2 = (bf16[1,1,3,5376,128]{4,3,2,1,0:T(8,128)(2,1)S(1)}, bf16[1,1,3,5376,128]{4,3,2,1,0:T(8,128)(2,1)}, u32[]{:S(2)}) copy-start(bf16[1,1,3,5376,128]{4,3,2,1,0:T(8,128)(2,1)} %param.10) | copy-start | bytes 12386308
  162.0 16.6 %collective-permute-start.22 = (bf16[4,6,4,1408]{3,1,2,0:T(8,128)(2,1)S(1)}, bf16[4,6,4,1408]{3,1,2,0:T(8,128)(2,1)S(1)}, u32[]{:S(2)}, u32[]{:S(2)}) collective-permute-start(bf16[4,6,4,1408]{3,1,2,0:T(8,128)(2,1)S(1)} %copy.130), channel_id=1, source_target_pairs={{0,7},{1,0},{2,1},{3,2},{4,3},{5,4},{6,5},{7,6},{8,15},{9,8},{10,9... | collective-permute-start | bytes 811016 | tf_op jit(solution)/shard_map/ppermute | solution.py:24
  168.4 10.2 %collective-permute-start.21 = (bf16[4,6,4,1280]{3,1,2,0:T(8,128)(2,1)S(1)}, bf16[4,6,4,1280]{3,1,2,0:T(8,128)(2,1)S(1)}, u32[]{:S(2)}, u32[]{:S(2)}) collective-permute-start(bf16[4,6,4,1280]{3,1,2,0:T(8,128)(2,1)S(1)} %copy.129), channel_id=1, source_target_pairs={{0,1},{1,2},{2,3},{3,4},{4,5},{5,6},{6,7},{7,0},{8,9},{9,10},{10,1... | collective-permute-start | bytes 737288 | tf_op jit(solution)/shard_map/ppermute | solution.py:23
  174.5 6.3 %copy-start.5 = (f32[4,6,4,3,128]{4,2,3,1,0:T(4,128)S(1)}, f32[4,6,4,3,128]{4,2,3,1,0:T(4,128)}, u32[]{:S(2)}) copy-start(f32[4,6,4,3,128]{4,2,3,1,0:T(4,128)} %fusion.34) | copy-start | bytes 442372
  174.5 7.0 %copy-start.4 = (f32[4,6,4,3,128]{4,2,3,1,0:T(4,128)S(1)}, f32[4,6,4,3,128]{4,2,3,1,0:T(4,128)}, u32[]{:S(2)}) copy-start(f32[4,6,4,3,128]{4,2,3,1,0:T(4,128)} %fusion.32) | copy-start | bytes 442372
  208.8 1.3 copy-start.3

commit v3 on v2

--- a/solution.py
+++ b/solution.py
@@ -71,32 +71,29 @@
         flat = block.reshape(-1, block.shape[-1])
         return jnp.einsum("rd,edc->rec", flat, enc, preferred_element_type=jnp.float32)
 
-    a_x = jnp.stack(ring_parts(part_a, "x", n_x), axis=0)
-    prod_a = [mm(blk, enc_a) for blk in ring_parts(a_x, "y", n_y)]
-    prod_a = jnp.stack(prod_a, axis=0).reshape(n_y, n_x, slots, rows_dev, enc_count, tile_cols)
+    a_x = lax.all_gather(part_a, "x", axis=0, tiled=False)
+    a_all = lax.all_gather(a_x, "y", axis=1, tiled=False)
+    prod_a = mm(a_all, enc_a).reshape(n_x, n_y, slots, rows_dev, enc_count, tile_cols)
 
     b_y = jnp.stack(ring_parts(part_b, "y", n_y), axis=0)
     b_parts = ring_parts(b_y, "x", n_x)
-    prod_b = [mm(blk, enc_b) for blk in b_parts]
-    prod_b = jnp.stack(prod_b, axis=0).reshape(n_x, n_y, slots, rows_dev, enc_count, tile_cols)
+    prod_b = jnp.stack([mm(blk, enc_b) for blk in b_parts], axis=0)
+    prod_b = prod_b.reshape(n_x, n_y, slots, rows_dev, enc_count, tile_cols)
+    prod_b = jnp.roll(jnp.roll(prod_b, my_x, axis=0), my_y, axis=1)
     scale_b = jnp.stack([blk[..., width - split] for blk in b_parts], axis=0)
+    scale_b = jnp.roll(jnp.roll(scale_b, my_x, axis=0), my_y, axis=1)
 
-    products = prod_a + jnp.transpose(prod_b, (1, 0, 2, 3, 4, 5))
+    products = prod_a + prod_b
+    tiles = jnp.transpose(products, (2, 4, 0, 1, 3, 5)).reshape(slots * enc_count, -1, tile_cols)
+    scale_rows = jnp.transpose(scale_b, (2, 0, 1, 3)).reshape(slots, -1)
 
     dev_pairs = pair_list[0, 0]
     slot_ids = dev_pairs[:, 0]
     block_ids = dev_pairs[:, 1]
     amount = pair_count[0, 0]
     pair_total = dev_pairs.shape[0]
-
-    rows_all = jnp.arange(n_x * n_y * rows_dev)
-    rr = rows_all % rows_dev
-    shard_abs = rows_all // rows_dev
-    kx = (shard_abs // n_y - my_x) % n_x
-    ky = (shard_abs % n_y - my_y) % n_y
-
-    chosen = products[ky[None, :], kx[None, :], slot_ids[:, None], rr[None, :], block_ids[:, None], :]
-    scales = scale_b[kx[None, :], ky[None, :], slot_ids[:, None], rr[None, :]].astype(jnp.float32)
+    chosen = jnp.take(tiles, slot_ids * enc_count + block_ids, axis=0)
+    scales = jnp.take(scale_rows, slot_ids, axis=0).astype(jnp.float32)
     is_live = jnp.arange(pair_total) < amount
     result = jnp.where(
         is_live[:, None, None], scales[:, :, None] * chosen, jnp.zeros((), jnp.float32)

time: 231 us -> 175 us (0.76)
  the two profiles are of different devices: /device:TPU:6 before, /device:TPU:24 now
where the time goes in v3:
time: 175 us; the launch traced here: 174 us
  starting transfers between devices  53.4 us (31%)
  waiting for transfers between devices  51.1 us (29%)
  local copies, waits for them, and re-layouts  21.9 us (13%)
  blocking collectives  14.6 us (8%)
  between operations  14.6 us (8%)
  matrix products  13.2 us (8%)
  other arithmetic  5.66 us (3%)
    all_to_all x1, waiting for transfers between devices, local(): recv = lax.all_to_all(send, GRP, 0, 0, tiled=True)  18.8 us
    ppermute x4, starting transfers between devices, ring_parts(): left = lax.ppermute(left, axis, up)  17.8 us
    all_gather x1, blocking collectives, local(): a_x = lax.all_gather(part_a, 'x', axis=0, tiled=False)  14.6 us
    ppermute x4, waiting for transfers between devices, ring_parts(): right = lax.ppermute(right, axis, down)  14.4 us
    dot_general x5, matrix products, mm(): jnp.einsum('rd,edc->rec', flat, enc, preferred_element_type=jnp.float32)  13.2 us
    all_to_all x1, starting transfers between devices, local(): recv = lax.all_to_all(send, GRP, 0, 0, tiled=True)  10.4 us
    ppermute x4, starting transfers between devices, ring_parts(): right = lax.ppermute(right, axis, down)  10.1 us
    ppermute x4, waiting for transfers between devices, ring_parts(): left = lax.ppermute(left, axis, up)  9.49 us
  transfers between devices with their start and end apart: 14, of which 7 were waited for; matrix products, arithmetic and copies ran while one was open for 14% of the time, Pallas kernels for 0%

profile of v3, /device:TPU:24, one launch (start us, length us, event | category | flops | bytes accessed | tf_op | source)
XLA Modules:
  0.0 174.3 jit_solution(18195211012103880978)
XLA Ops:
  6.5 0.7 fusion.29
  7.3 0.8 and_bitcast_fusion
  8.0 0.8 copy.155
  8.8 1.1 fusion.25
  10.0 1.2 gather_fusion
  11.2 1.2 broadcast_select_fusion
  12.4 10.4 %all-to-all-start = ((bf16[16,4,5504]{2,1,0:T(4,128)(2,1)}), bf16[16,4,5504]{2,1,0:T(4,128)(2,1)S(1)}, u32[]{:S(2)}, u32[]{:S(2)}) async-start(bf16[16,4,5504]{2,1,0:T(4,128)(2,1)} %broadcast_select_fusion), calls=%async_computation | async-start | bytes 1409024 | tf_op jit(solution)/shard_map/all_to_all | solution.py:52
  22.9 0.2 dynamic-slice_reduce_fusion
  23.1 18.8 %all-to-all-done = bf16[16,4,5504]{2,1,0:T(4,128)(2,1)S(1)} async-done(((bf16[16,4,5504]{2,1,0:T(4,128)(2,1)}), bf16[16,4,5504]{2,1,0:T(4,128)(2,1)S(1)}, u32[]{:S(2)}, u32[]{:S(2)}) %all-to-all-start) | async-done | bytes 704544 | tf_op jit(solution)/shard_map/all_to_all | solution.py:52
  42.0 0.8 gather_fusion.1
  42.8 0.2 select_select_fusion
  43.0 14.6 %all-gather = bf16[24,4,2688]{2,1,0:T(4,128)(2,1)} all-gather(bf16[6,4,2688]{2,1,0:T(4,128)(2,1)S(1)} %slice.91), channel_id=2, replica_groups=mesh['z'=8,'c'=2,'x'=4,'y'=8] {'x'}, dimensions={0}, use_global_device_ids=true | all-gather | bytes 645120 | tf_op jit(solution)/shard_map/all_gather | solution.py:74
  57.7 4.7 %collective-permute-start.3 = (bf16[6,4,2816]{2,1,0:T(4,128)(2,1)S(1)}, bf16[6,4,2816]{2,1,0:T(4,128)(2,1)S(1)}, u32[]{:S(2)}, u32[]{:S(2)}) collective-permute-start(bf16[6,4,2816]{2,1,0:T(4,128)(2,1)S(1)} %get-tuple-element.19), channel_id=1, source_target_pairs={{0,1},{1,2},{2,3},{3,4},{4,5},{5,6},{6,7},{7,0},{8,9},{9,10},{10,1... | collective-permute-start | bytes 405512 | tf_op jit(solution)/shard_map/ppermute | solution.py:27
  62.4 1.9 %collective-permute-start = (bf16[6,4,2816]{2,1,0:T(4,128)(2,1)S(1)}, bf16[6,4,2816]{2,1,0:T(4,128)(2,1)S(1)}, u32[]{:S(2)}, u32[]{:S(2)}) collective-permute-start(bf16[6,4,2816]{2,1,0:T(4,128)(2,1)S(1)} %get-tuple-element.19), channel_id=1, source_target_pairs={{0,7},{1,0},{2,1},{3,2},{4,3},{5,4},{6,5},{7,6},{8,15},{9,8},{10,9... | collective-permute-start | bytes 405512 | tf_op jit(solution)/shard_map/ppermute | solution.py:28
  64.3 1.2 collective-permute-done.3
  65.5 5.6 %collective-permute-start.4 = (bf16[6,4,2816]{2,1,0:T(4,128)(2,1)S(1)}, bf16[6,4,2816]{2,1,0:T(4,128)(2,1)S(1)}, u32[]{:S(2)}, u32[]{:S(2)}) collective-permute-start(bf16[6,4,2816]{2,1,0:T(4,128)(2,1)S(1)} %collective-permute-done.3), channel_id=1, source_target_pairs={{0,1},{1,2},{2,3},{3,4},{4,5},{5,6},{6,7},{7,0},{8,9},{9,10},{10,1... | collective-permute-start | bytes 405512 | tf_op jit(solution)/shard_map/ppermute | solution.py:27
  71.1 1.9 %collective-permute-start.1 = (bf16[6,4,2816]{2,1,0:T(4,128)(2,1)S(1)}, bf16[6,4,2816]{2,1,0:T(4,128)(2,1)S(1)}, u32[]{:S(2)}, u32[]{:S(2)}) collective-permute-start(bf16[6,4,2816]{2,1,0:T(4,128)(2,1)S(1)} %collective-permute-done), channel_id=1, source_target_pairs={{0,7},{1,0},{2,1},{3,2},{4,3},{5,4},{6,5},{7,6},{8,15},{9,8},{10,9... | collective-permute-start | bytes 405512 | tf_op jit(solution)/shard_map/ppermute | solution.py:28
  73.0 4.3 %collective-permute-done.4 = bf16[6,4,2816]{2,1,0:T(4,128)(2,1)S(1)} collective-permute-done((bf16[6,4,2816]{2,1,0:T(4,128)(2,1)S(1)}, bf16[6,4,2816]{2,1,0:T(4,128)(2,1)S(1)}, u32[]{:S(2)}, u32[]{:S(2)}) %collective-permute-start.4) | collective-permute-done | bytes 135200 | tf_op jit(solution)/shard_map/ppermute | solution.py:27
  77.3 5.6 %collective-permute-start.5 = (bf16[6,4,2816]{2,1,0:T(4,128)(2,1)S(1)}, bf16[6,4,2816]{2,1,0:T(4,128)(2,1)S(1)}, u32[]{:S(2)}, u32[]{:S(2)}) collective-permute-start(bf16[6,4,2816]{2,1,0:T(4,128)(2,1)S(1)} %collective-permute-done.4), channel_id=1, source_target_pairs={{0,1},{1,2},{2,3},{3,4},{4,5},{5,6},{6,7},{7,0},{8,9},{9,10},{10,1... | collective-permute-start | bytes 405512 | tf_op jit(solution)/shard_map/ppermute | solution.py:27
  82.9 1.9 %collective-permute-start.2 = (bf16[6,4,2816]{2,1,0:T(4,128)(2,1)S(1)}, bf16[6,4,2816]{2,1,0:T(4,128)(2,1)S(1)}, u32[]{:S(2)}, u32[]{:S(2)}) collective-permute-start(bf16[6,4,2816]{2,1,0:T(4,128)(2,1)S(1)} %collective-permute-done.1), channel_id=1, source_target_pairs={{0,7},{1,0},{2,1},{3,2},{4,3},{5,4},{6,5},{7,6},{8,15},{9,8},{10,9... | collective-permute-start | bytes 405512 | tf_op jit(solution)/shard_map/ppermute | solution.py:28
  84.9 4.0 %collective-permute-done.5 = bf16[6,4,2816]{2,1,0:T(4,128)(2,1)S(1)} collective-permute-done((bf16[6,4,2816]{2,1,0:T(4,128)(2,1)S(1)}, bf16[6,4,2816]{2,1,0:T(4,128)(2,1)S(1)}, u32[]{:S(2)}, u32[]{:S(2)}) %collective-permute-start.5) | collective-permute-done | bytes 135200 | tf_op jit(solution)/shard_map/ppermute | solution.py:27
  88.9 5.6 %collective-permute-start.6 = (bf16[6,4,1408]{2,1,0:T(4,128)(2,1)S(1)}, bf16[6,4,1408]{2,1,0:T(4,128)(2,1)S(1)}, u32[]{:S(2)}, u32[]{:S(2)}) collective-permute-start(bf16[6,4,1408]{2,1,0:T(4,128)(2,1)S(1)} %slice.84), channel_id=1, source_target_pairs={{0,1},{1,2},{2,3},{3,4},{4,5},{5,6},{6,7},{7,0},{8,9},{9,10},{10,1... | collective-permute-start | bytes 202760 | tf_op jit(solution)/shard_map/ppermute | solution.py:23
  94.6 1.9 %collective-permute-start.7 = (bf16[6,4,1408]{2,1,0:T(4,128)(2,1)S(1)}, bf16[6,4,1408]{2,1,0:T(4,128)(2,1)S(1)}, u32[]{:S(2)}, u32[]{:S(2)}) collective-permute-start(bf16[6,4,1408]{2,1,0:T(4,128)(2,1)S(1)} %slice.85), channel_id=1, source_target_pairs={{0,7},{1,0},{2,1},{3,2},{4,3},{5,4},{6,5},{7,6},{8,15},{9,8},{10,9... | collective-permute-start | bytes 202760 | tf_op jit(solution)/shard_map/ppermute | solution.py:24
  96.5 0.2 copy.134
  96.7 0.2 copy.135
  97.0 0.2 copy.141
  97.2 0.2 copy.136
  97.4 0.2 copy.140
  97.6 0.2 copy.137
  97.8 0.2 copy.139
  98.1 5.5 %collective-permute-done.7 = bf16[6,4,1408]{2,1,0:T(4,128)(2,1)S(1)} collective-permute-done((bf16[6,4,1408]{2,1,0:T(4,128)(2,1)S(1)}, bf16[6,4,1408]{2,1,0:T(4,128)(2,1)S(1)}, u32[]{:S(2)}, u32[]{:S(2)}) %collective-permute-start.7) | collective-permute-done | bytes 67616 | tf_op jit(solution)/shard_map/ppermute | solution.py:24
  103.6 0.2 copy.138
  103.8 5.3 %stack.41 = bf16[8,6,4,2816]{3,0,2,1:T(8,128)(2,1)S(1)} concatenate(bf16[1,6,4,2816]{3,0,2,1:T(2,128)(2,1)S(1)} %copy.134, bf16[1,6,4,2816]{3,0,2,1:T(2,128)(2,1)S(1)} %copy.135, bf16[1,6,4,2816]{3,0,2,1:T(2,128)(2,1)S(1)} %copy.136, bf16[1,6,4,2816]{3,0,2,1:T(2,128)(2,1)S(1)} %copy.137, bf16[1,6,4,2816]{3,0,2,1:T(2,128)(2,1)S(1)} %copy.138, bf16[1,6,4,2816]{3,0,2,1:T(2,128)(2,1)S(1)} %copy.139, ...), dimensions={0} | concatenate | bytes 2162688 | tf_op jit(solution)/shard_map/stack | solution.py:78
  109.2 4.3 %collective-permute-start.8 = (bf16[8,6,4,2816]{3,0,2,1:T(8,128)(2,1)S(1)}, bf16[8,6,4,2816]{3,0,2,1:T(8,128)(2,1)}, u32[]{:S(2)}, u32[]{:S(2)}) collective-permute-start(bf16[8,6,4,2816]{3,0,2,1:T(8,128)(2,1)S(1)} %stack.41), channel_id=1, source_target_pairs={{0,24},{8,0},{16,8},{24,16},{1,25},{9,1},{17,9},{25,17},{2,26},{10... | collective-permute-start | bytes 3244040 | tf_op jit(solution)/shard_map/ppermute | solution.py:28
  113.5 1.9 %collective-permute-start.10 = (bf16[8,6,4,2816]{3,0,2,1:T(8,128)(2,1)S(1)}, bf16[8,6,4,2816]{3,0,2,1:T(8,128)(2,1)}, u32[]{:S(2)}, u32[]{:S(2)}) collective-permute-start(bf16[8,6,4,2816]{3,0,2,1:T(8,128)(2,1)S(1)} %stack.41), channel_id=1, source_target_pairs={{0,8},{8,16},{16,24},{24,0},{1,9},{9,17},{17,25},{25,1},{2,10},{10... | collective-permute-start | bytes 3244040 | tf_op jit(solution)/shard_map/ppermute | solution.py:27
  115.5 1.7 slice.93
  117.9 0.1 slice_reduce_fusion.3
  118.0 0.7 fusion.6
  118.7 0.8 bitcast_dynamic-update-slice_fusion.6
  119.5 14.4 %collective-permute-done.8 = bf16[8,6,4,2816]{3,0,2,1:T(8,128)(2,1)} collective-permute-done((bf16[8,6,4,2816]{3,0,2,1:T(8,128)(2,1)S(1)}, bf16[8,6,4,2816]{3,0,2,1:T(8,128)(2,1)}, u32[]{:S(2)}, u32[]{:S(2)}) %collective-permute-start.8) | collective-permute-done | bytes 1081376 | tf_op jit(solution)/shard_map/ppermute | solution.py:28
  133.9 1.1 slice.88
  135.0 5.5 %collective-permute-start.9 = (bf16[8,6,4,1408]{3,0,2,1:T(8,128)(2,1)S(1)}, bf16[8,6,4,1408]{3,0,2,1:T(8,128)(2,1)S(1)}, u32[]{:S(2)}, u32[]{:S(2)}) collective-permute-start(bf16[8,6,4,1408]{3,0,2,1:T(8,128)(2,1)S(1)} %slice.88), channel_id=1, source_target_pairs={{0,24},{8,0},{16,8},{24,16},{1,25},{9,1},{17,9},{25,17},{2,26},{10... | collective-permute-start | bytes 1622024 | tf_op jit(solution)/shard_map/ppermute | solution.py:24
  140.5 2.0 %slice.94 = bf16[8,6,4,1408]{3,0,2,1:T(8,128)(2,1)} slice(bf16[8,6,4,2816]{3,0,2,1:T(8,128)(2,1)} %collective-permute-done.10), slice={[0:8], [0:6], [0:4], [0:1408]} | slice | bytes 1081344 | tf_op jit(solution)/shard_map/slice | solution.py:23
  142.4 2.1 %collective-permute-start.11 = (bf16[8,6,4,1408]{3,0,2,1:T(8,128)(2,1)}, bf16[8,6,4,1408]{3,0,2,1:T(8,128)(2,1)}, u32[]{:S(2)}, u32[]{:S(2)}) collective-permute-start(bf16[8,6,4,1408]{3,0,2,1:T(8,128)(2,1)} %slice.94), channel_id=1, source_target_pairs={{0,8},{8,16},{16,24},{24,0},{1,9},{9,17},{17,25},{25,1},{2,10},{10... | collective-permute-start | bytes 1622024 | tf_op jit(solution)/shard_map/ppermute | solution.py:23
  144.5 0.9 slice_reduce_fusion.2
  145.5 2.0 %fusion.4 = f32[8,6,4,3,128]{4,0,3,2,1:T(8,128)S(1)} fusion(bf16[3,2688,128]{2,1,0:T(8,128)(2,1)S(1)} %slice.93, bf16[8,6,4,2816]{3,0,2,1:T(8,128)(2,1)} %collective-permute-done.8), kind=kOutput, calls=%fused_computation.10 | convolution fusion | flops 415236096 | bytes 3440640 | tf_op jit(solution)/shard_map/rd,edc->rec/dot_general | solution.py:72
  147.4 0.9 slice_reduce_fusion
  148.4 0.8 bitcast_dynamic-update-slice_fusion.4
  149.2 2.0 %fusion = f32[8,6,4,3,128]{4,0,3,2,1:T(8,128)S(1)} fusion(bf16[3,2688,128]{2,1,0:T(8,128)(2,1)S(1)} %slice.93, bf16[8,6,4,2816]{3,0,2,1:T(8,128)(2,1)} %collective-permute-done.10), kind=kOutput, calls=%fused_computation.6 | convolution fusion | flops 415236096 | bytes 3440640 | tf_op jit(solution)/shard_map/rd,edc->rec/dot_general | solution.py:72
  151.2 0.1 slice_reduce_fusion.1
  151.4 0.6 copy-done.2
  152.0 0.1 fusion.26
  152.1 0.2 copy.142
  152.3 0.1 reshape.246
  152.4 0.6 gather_fusion.2
  153.0 2.8 %collective-permute-done.11 = bf16[8,6,4,1408]{3,0,2,1:T(8,128)(2,1)} collective-permute-done((bf16[8,6,4,1408]{3,0,2,1:T(8,128)(2,1)}, bf16[8,6,4,1408]{3,0,2,1:T(8,128)(2,1)}, u32[]{:S(2)}, u32[]{:S(2)}) %collective-permute-start.11) | collective-permute-done | bytes 540704 | tf_op jit(solution)/shard_map/ppermute | solution.py:23
  155.8 1.9 %fusion.2 = f32[8,6,4,3,128]{4,0,3,2,1:T(8,128)S(1)} fusion(bf16[3,2688,128]{2,1,0:T(8,128)(2,1)S(1)} %slice.93, bf16[8,6,4,1408]{3,0,2,1:T(8,128)(2,1)} %copy-done.2, bf16[8,6,4,1408]{3,0,2,1:T(8,128)(2,1)} %collective-permute-done.11), kind=kOutput, calls=%fused_computation.8 | convolution fusion | flops 417398784 | bytes 3440640 | tf_op jit(solution)/shard_map/rd,edc->rec/dot_general | solution.py:72
  157.8 0.1 bitcast_dynamic-update-slice_fusion.2
  157.9 0.1 bitcast_dynamic-update-slice_fusion
  158.4 0.2 constant_dynamic-slice_fusion
  158.7 6.5 %fusion.14 = f32[6,3,4,8,4,128]{5,4,1,0,3,2:T(4,128)S(1)} fusion(bf16[4,8,6,4,2688,1]{4,3,5,2,1,0:T(4,128)(2,1)} %bitcast.138, bf16[3,5376,128]{2,1,0:T(8,128)(2,1)} %bitcast.127, s32[]{:T(128)S(6)} %select_n.190, f32[4,8,6,4,3,128]{5,3,4,2,1,0:T(4,128)S(1)} %constant_dynamic-slice_fusion), kind=kOutput, calls=%fused_computation.21 | convolution fusion | flops 1586036736 | bytes 8552452 | tf_op jit(solution)/shard_map/rd,edc->rec/dot_general | solution.py:72
  165.3 0.3 copy.147
  165.6 0.6 gather_fusion.3
  166.2 1.2 fusion.18
  (43 shorter events, 1.0 us)
Async XLA Ops:
  10.0 12.9 %copy-start.1 = (s32[16,6]{0,1:T(8,128)S(1)}, s32[16,6]{0,1:T(8,128)}, u32[]{:S(2)}) copy-start(s32[16,6]{0,1:T(8,128)} %param.11) | copy-start | bytes 1156
  10.0 13.1 %copy-start.3 = (s32[1,1,18,2]{2,3,1,0:T(2,128)S(1)}, s32[1,1,18,2]{2,3,1,0:T(2,128)}, u32[]{:S(2)}) copy-start(s32[1,1,18,2]{2,3,1,0:T(2,128)} %param.12) | copy-start | bytes 436
  12.4 29.6 %all-to-all-start = ((bf16[16,4,5504]{2,1,0:T(4,128)(2,1)}), bf16[16,4,5504]{2,1,0:T(4,128)(2,1)S(1)}, u32[]{:S(2)}, u32[]{:S(2)}) async-start(bf16[16,4,5504]{2,1,0:T(4,128)(2,1)} %broadcast_select_fusion), calls=%async_computation | async-start | bytes 1409024 | tf_op jit(solution)/shard_map/all_to_all | solution.py:52
  22.8 135.9 %all-gather.4.cloned.1.call-start = ((), (), s32[]{:S(2)}) async-start(), calls=%async_computation.1 | async-start | bytes 4644864 | tf_op jit(solution)/shard_map/all_gather | solution.py:75
  57.7 7.8 %collective-permute-start.3 = (bf16[6,4,2816]{2,1,0:T(4,128)(2,1)S(1)}, bf16[6,4,2816]{2,1,0:T(4,128)(2,1)S(1)}, u32[]{:S(2)}, u32[]{:S(2)}) collective-permute-start(bf16[6,4,2816]{2,1,0:T(4,128)(2,1)S(1)} %get-tuple-element.19), channel_id=1, source_target_pairs={{0,1},{1,2},{2,3},{3,4},{4,5},{5,6},{6,7},{7,0},{8,9},{9,10},{10,1... | collective-permute-start | bytes 405512 | tf_op jit(solution)/shard_map/ppermute | solution.py:27
  62.4 8.7 %collective-permute-start = (bf16[6,4,2816]{2,1,0:T(4,128)(2,1)S(1)}, bf16[6,4,2816]{2,1,0:T(4,128)(2,1)S(1)}, u32[]{:S(2)}, u32[]{:S(2)}) collective-permute-start(bf16[6,4,2816]{2,1,0:T(4,128)(2,1)S(1)} %get-tuple-element.19), channel_id=1, source_target_pairs={{0,7},{1,0},{2,1},{3,2},{4,3},{5,4},{6,5},{7,6},{8,15},{9,8},{10,9... | collective-permute-start | bytes 405512 | tf_op jit(solution)/shard_map/ppermute | solution.py:28
  65.5 11.8 %collective-permute-start.4 = (bf16[6,4,2816]{2,1,0:T(4,128)(2,1)S(1)}, bf16[6,4,2816]{2,1,0:T(4,128)(2,1)S(1)}, u32[]{:S(2)}, u32[]{:S(2)}) collective-permute-start(bf16[6,4,2816]{2,1,0:T(4,128)(2,1)S(1)} %collective-permute-done.3), channel_id=1, source_target_pairs={{0,1},{1,2},{2,3},{3,4},{4,5},{5,6},{6,7},{7,0},{8,9},{9,10},{10,1... | collective-permute-start | bytes 405512 | tf_op jit(solution)/shard_map/ppermute | solution.py:27
  71.1 11.8 %collective-permute-start.1 = (bf16[6,4,2816]{2,1,0:T(4,128)(2,1)S(1)}, bf16[6,4,2816]{2,1,0:T(4,128)(2,1)S(1)}, u32[]{:S(2)}, u32[]{:S(2)}) collective-permute-start(bf16[6,4,2816]{2,1,0:T(4,128)(2,1)S(1)} %collective-permute-done), channel_id=1, source_target_pairs={{0,7},{1,0},{2,1},{3,2},{4,3},{5,4},{6,5},{7,6},{8,15},{9,8},{10,9... | collective-permute-start | bytes 405512 | tf_op jit(solution)/shard_map/ppermute | solution.py:28
  77.3 11.6 %collective-permute-start.5 = (bf16[6,4,2816]{2,1,0:T(4,128)(2,1)S(1)}, bf16[6,4,2816]{2,1,0:T(4,128)(2,1)S(1)}, u32[]{:S(2)}, u32[]{:S(2)}) collective-permute-start(bf16[6,4,2816]{2,1,0:T(4,128)(2,1)S(1)} %collective-permute-done.4), channel_id=1, source_target_pairs={{0,1},{1,2},{2,3},{3,4},{4,5},{5,6},{6,7},{7,0},{8,9},{9,10},{10,1... | collective-permute-start | bytes 405512 | tf_op jit(solution)/shard_map/ppermute | solution.py:27
  82.9 11.6 %collective-permute-start.2 = (bf16[6,4,2816]{2,1,0:T(4,128)(2,1)S(1)}, bf16[6,4,2816]{2,1,0:T(4,128)(2,1)S(1)}, u32[]{:S(2)}, u32[]{:S(2)}) collective-permute-start(bf16[6,4,2816]{2,1,0:T(4,128)(2,1)S(1)} %collective-permute-done.1), channel_id=1, source_target_pairs={{0,7},{1,0},{2,1},{3,2},{4,3},{5,4},{6,5},{7,6},{8,15},{9,8},{10,9... | collective-permute-start | bytes 405512 | tf_op jit(solution)/shard_map/ppermute | solution.py:28
  88.9 9.1 %collective-permute-start.6 = (bf16[6,4,1408]{2,1,0:T(4,128)(2,1)S(1)}, bf16[6,4,1408]{2,1,0:T(4,128)(2,1)S(1)}, u32[]{:S(2)}, u32[]{:S(2)}) collective-permute-start(bf16[6,4,1408]{2,1,0:T(4,128)(2,1)S(1)} %slice.84), channel_id=1, source_target_pairs={{0,1},{1,2},{2,3},{3,4},{4,5},{5,6},{6,7},{7,0},{8,9},{9,10},{10,1... | collective-permute-start | bytes 202760 | tf_op jit(solution)/shard_map/ppermute | solution.py:23
  94.6 9.0 %collective-permute-start.7 = (bf16[6,4,1408]{2,1,0:T(4,128)(2,1)S(1)}, bf16[6,4,1408]{2,1,0:T(4,128)(2,1)S(1)}, u32[]{:S(2)}, u32[]{:S(2)}) collective-permute-start(bf16[6,4,1408]{2,1,0:T(4,128)(2,1)S(1)} %slice.85), channel_id=1, source_target_pairs={{0,7},{1,0},{2,1},{3,2},{4,3},{5,4},{6,5},{7,6},{8,15},{9,8},{10,9... | collective-permute-start | bytes 202760 | tf_op jit(solution)/shard_map/ppermute | solution.py:24
  109.2 24.8 %collective-permute-start.8 = (bf16[8,6,4,2816]{3,0,2,1:T(8,128)(2,1)S(1)}, bf16[8,6,4,2816]{3,0,2,1:T(8,128)(2,1)}, u32[]{:S(2)}, u32[]{:S(2)}) collective-permute-start(bf16[8,6,4,2816]{3,0,2,1:T(8,128)(2,1)S(1)} %stack.41), channel_id=1, source_target_pairs={{0,24},{8,0},{16,8},{24,16},{1,25},{9,1},{17,9},{25,17},{2,26},{10... | collective-permute-start | bytes 3244040 | tf_op jit(solution)/shard_map/ppermute | solution.py:28
  113.5 27.0 %collective-permute-start.10 = (bf16[8,6,4,2816]{3,0,2,1:T(8,128)(2,1)S(1)}, bf16[8,6,4,2816]{3,0,2,1:T(8,128)(2,1)}, u32[]{:S(2)}, u32[]{:S(2)}) collective-permute-start(bf16[8,6,4,2816]{3,0,2,1:T(8,128)(2,1)S(1)} %stack.41), channel_id=1, source_target_pairs={{0,8},{8,16},{16,24},{24,0},{1,9},{9,17},{17,25},{25,1},{2,10},{10... | collective-permute-start | bytes 3244040 | tf_op jit(solution)/shard_map/ppermute | solution.py:27
  135.0 16.1 %collective-permute-start.9 = (bf16[8,6,4,1408]{3,0,2,1:T(8,128)(2,1)S(1)}, bf16[8,6,4,1408]{3,0,2,1:T(8,128)(2,1)S(1)}, u32[]{:S(2)}, u32[]{:S(2)}) collective-permute-start(bf16[8,6,4,1408]{3,0,2,1:T(8,128)(2,1)S(1)} %slice.88), channel_id=1, source_target_pairs={{0,24},{8,0},{16,8},{24,16},{1,25},{9,1},{17,9},{25,17},{2,26},{10... | collective-permute-start | bytes 1622024 | tf_op jit(solution)/shard_map/ppermute | solution.py:24
  142.4 13.4 %collective-permute-start.11 = (bf16[8,6,4,1408]{3,0,2,1:T(8,128)(2,1)}, bf16[8,6,4,1408]{3,0,2,1:T(8,128)(2,1)}, u32[]{:S(2)}, u32[]{:S(2)}) collective-permute-start(bf16[8,6,4,1408]{3,0,2,1:T(8,128)(2,1)} %slice.94), channel_id=1, source_target_pairs={{0,8},{8,16},{16,24},{24,0},{1,9},{9,17},{17,25},{25,1},{2,10},{10... | collective-permute-start | bytes 1622024 | tf_op jit(solution)/shard_map/ppermute | solution.py:23
  151.2 0.8 copy-start.2
  153.0 4.7 %copy-start = (f32[8,8,6,4,3,128]{5,3,4,2,1,0:T(4,128)S(1)}, f32[8,8,6,4,3,128]{5,3,4,2,1,0:T(4,128)}, u32[]{:S(2)}) copy-start(f32[8,8,6,4,3,128]{5,3,4,2,1,0:T(4,128)} %bitcast_dynamic-update-slice_fusion.4) | copy-start | bytes 7077892
Sparse Core Ops, SparseCore 0:
  57.7 61.6 all-gather.3

commit v4 on v3

--- a/solution.py
+++ b/solution.py
@@ -58,7 +58,7 @@
     slot_rows = jnp.where(my_valid[:, None, None], slot_rows, jnp.zeros((), slot_rows.dtype))
     slots, rows_dev, _ = slot_rows.shape
 
-    split = (ext_width // 2) // LANES * LANES
+    split = (ext_width * 3 // 5) // LANES * LANES
     part_a = slot_rows[..., :split]
     part_b = slot_rows[..., split:]
 
@@ -71,8 +71,7 @@
         flat = block.reshape(-1, block.shape[-1])
         return jnp.einsum("rd,edc->rec", flat, enc, preferred_element_type=jnp.float32)
 
-    a_x = lax.all_gather(part_a, "x", axis=0, tiled=False)
-    a_all = lax.all_gather(a_x, "y", axis=1, tiled=False)
+    a_all = lax.all_gather(part_a, SHARD, axis=0, tiled=False)
     prod_a = mm(a_all, enc_a).reshape(n_x, n_y, slots, rows_dev, enc_count, tile_cols)
 
     b_y = jnp.stack(ring_parts(part_b, "y", n_y), axis=0)

time: 175 us -> 163 us (0.931)
  blocking collectives: 14.6 us -> 0 us
  waiting for transfers between devices: 51.1 us -> 56 us
  local copies, waits for them, and re-layouts: 21.9 us -> 18.6 us
    all_gather x1 -> x0, blocking collectives: 14.6 us -> none  [local(): a_x = lax.all_gather(part_a, 'x', axis=0, tiled=False)]
    ppermute x4, waiting for transfers between devices: 14.4 us -> 25.2 us  [ring_parts(): right = lax.ppermute(right, axis, down)]
    ppermute x4, waiting for transfers between devices: 9.49 us -> 5.81 us  [ring_parts(): left = lax.ppermute(left, axis, up)]
    another operation x9, local copies, waits for them, and re-layouts: 6.99 us -> 4.14 us  [local(): b_y = jnp.stack(ring_parts(part_b, 'y', n_y), axis=0)]
    ppermute x2, waiting for transfers between devices: 5.5 us -> 3.42 us  [ring_parts(): got_right = lax.ppermute(right[..., half:], axis, down)]
  transfers between devices with their start and end apart: 14 -> 14, of which waited for: 7 -> 9; matrix products, arithmetic and copies ran while one was open for 14% -> 12% of each run, Pallas kernels for 0% -> 0%
where the time goes in v4:
time: 163 us; the launch traced here: 162 us
  waiting for transfers between devices  56 us (34%)
  starting transfers between devices  53.9 us (33%)
  local copies, waits for them, and re-layouts  18.6 us (11%)
  between operations  14.6 us (9%)
  matrix products  13.4 us (8%)
  other arithmetic  5.65 us (3%)
    ppermute x4, waiting for transfers between devices, ring_parts(): right = lax.ppermute(right, axis, down)  25.2 us
    all_to_all x1, waiting for transfers between devices, local(): recv = lax.all_to_all(send, GRP, 0, 0, tiled=True)  18.8 us
    ppermute x4, starting transfers between devices, ring_parts(): left = lax.ppermute(left, axis, up)  17.7 us
    dot_general x5, matrix products, mm(): jnp.einsum('rd,edc->rec', flat, enc, preferred_element_type=jnp.float32)  13.4 us
    all_to_all x1, starting transfers between devices, local(): recv = lax.all_to_all(send, GRP, 0, 0, tiled=True)  10.4 us
    ppermute x4, starting transfers between devices, ring_parts(): right = lax.ppermute(right, axis, down)  10.4 us
    ppermute x2, starting transfers between devices, ring_parts(): got_left = lax.ppermute(left[..., :half], axis, up)  7.7 us
    ppermute x2, starting transfers between devices, ring_parts(): got_right = lax.ppermute(right[..., half:], axis, down)  7.63 us
  transfers between devices with their start and end apart: 14, of which 9 were waited for; matrix products, arithmetic and copies ran while one was open for 12% of the time, Pallas kernels for 0%

profile of v4, /device:TPU:24, one launch (start us, length us, event | category | flops | bytes accessed | tf_op | source)
XLA Modules:
  0.0 162.2 jit_solution(6226606397206782654)
XLA Ops:
  6.5 0.7 fusion.29
  7.3 0.8 and_bitcast_fusion
  8.0 0.8 copy.155
  8.8 1.1 fusion.25
  10.0 1.2 gather_fusion
  11.2 1.2 broadcast_select_fusion
  12.4 10.4 %all-to-all-start = ((bf16[16,4,5504]{2,1,0:T(4,128)(2,1)}), bf16[16,4,5504]{2,1,0:T(4,128)(2,1)S(1)}, u32[]{:S(2)}, u32[]{:S(2)}) async-start(bf16[16,4,5504]{2,1,0:T(4,128)(2,1)} %broadcast_select_fusion), calls=%async_computation | async-start | bytes 1409024 | tf_op jit(solution)/shard_map/all_to_all | solution.py:52
  22.9 0.2 dynamic-slice_reduce_fusion
  23.1 18.8 %all-to-all-done = bf16[16,4,5504]{2,1,0:T(4,128)(2,1)S(1)} async-done(((bf16[16,4,5504]{2,1,0:T(4,128)(2,1)}), bf16[16,4,5504]{2,1,0:T(4,128)(2,1)S(1)}, u32[]{:S(2)}, u32[]{:S(2)}) %all-to-all-start) | async-done | bytes 704544 | tf_op jit(solution)/shard_map/all_to_all | solution.py:52
  42.0 0.8 gather_fusion.1
  42.8 0.2 select_select_fusion
  43.0 0.7 slice.91
  43.8 4.7 %collective-permute-start.3 = (bf16[6,4,2304]{2,1,0:T(4,128)(2,1)S(1)}, bf16[6,4,2304]{2,1,0:T(4,128)(2,1)S(1)}, u32[]{:S(2)}, u32[]{:S(2)}) collective-permute-start(bf16[6,4,2304]{2,1,0:T(4,128)(2,1)S(1)} %get-tuple-element.19), channel_id=1, source_target_pairs={{0,1},{1,2},{2,3},{3,4},{4,5},{5,6},{6,7},{7,0},{8,9},{9,10},{10,1... | collective-permute-start | bytes 331784 | tf_op jit(solution)/shard_map/ppermute | solution.py:27
  48.5 1.9 %collective-permute-start = (bf16[6,4,2304]{2,1,0:T(4,128)(2,1)S(1)}, bf16[6,4,2304]{2,1,0:T(4,128)(2,1)S(1)}, u32[]{:S(2)}, u32[]{:S(2)}) collective-permute-start(bf16[6,4,2304]{2,1,0:T(4,128)(2,1)S(1)} %get-tuple-element.19), channel_id=1, source_target_pairs={{0,7},{1,0},{2,1},{3,2},{4,3},{5,4},{6,5},{7,6},{8,15},{9,8},{10,9... | collective-permute-start | bytes 331784 | tf_op jit(solution)/shard_map/ppermute | solution.py:28
  50.4 0.4 collective-permute-done.3
  50.8 5.5 %collective-permute-start.4 = (bf16[6,4,2304]{2,1,0:T(4,128)(2,1)S(1)}, bf16[6,4,2304]{2,1,0:T(4,128)(2,1)S(1)}, u32[]{:S(2)}, u32[]{:S(2)}) collective-permute-start(bf16[6,4,2304]{2,1,0:T(4,128)(2,1)S(1)} %collective-permute-done.3), channel_id=1, source_target_pairs={{0,1},{1,2},{2,3},{3,4},{4,5},{5,6},{6,7},{7,0},{8,9},{9,10},{10,1... | collective-permute-start | bytes 331784 | tf_op jit(solution)/shard_map/ppermute | solution.py:27
  56.3 0.2 collective-permute-done
  56.5 1.9 %collective-permute-start.1 = (bf16[6,4,2304]{2,1,0:T(4,128)(2,1)S(1)}, bf16[6,4,2304]{2,1,0:T(4,128)(2,1)S(1)}, u32[]{:S(2)}, u32[]{:S(2)}) collective-permute-start(bf16[6,4,2304]{2,1,0:T(4,128)(2,1)S(1)} %collective-permute-done), channel_id=1, source_target_pairs={{0,7},{1,0},{2,1},{3,2},{4,3},{5,4},{6,5},{7,6},{8,15},{9,8},{10,9... | collective-permute-start | bytes 331784 | tf_op jit(solution)/shard_map/ppermute | solution.py:28
  58.4 2.0 %collective-permute-done.4 = bf16[6,4,2304]{2,1,0:T(4,128)(2,1)S(1)} collective-permute-done((bf16[6,4,2304]{2,1,0:T(4,128)(2,1)S(1)}, bf16[6,4,2304]{2,1,0:T(4,128)(2,1)S(1)}, u32[]{:S(2)}, u32[]{:S(2)}) %collective-permute-start.4) | collective-permute-done | bytes 110624 | tf_op jit(solution)/shard_map/ppermute | solution.py:27
  60.4 5.6 %collective-permute-start.5 = (bf16[6,4,2304]{2,1,0:T(4,128)(2,1)S(1)}, bf16[6,4,2304]{2,1,0:T(4,128)(2,1)S(1)}, u32[]{:S(2)}, u32[]{:S(2)}) collective-permute-start(bf16[6,4,2304]{2,1,0:T(4,128)(2,1)S(1)} %collective-permute-done.4), channel_id=1, source_target_pairs={{0,1},{1,2},{2,3},{3,4},{4,5},{5,6},{6,7},{7,0},{8,9},{9,10},{10,1... | collective-permute-start | bytes 331784 | tf_op jit(solution)/shard_map/ppermute | solution.py:27
  66.0 1.9 %collective-permute-start.2 = (bf16[6,4,2304]{2,1,0:T(4,128)(2,1)S(1)}, bf16[6,4,2304]{2,1,0:T(4,128)(2,1)S(1)}, u32[]{:S(2)}, u32[]{:S(2)}) collective-permute-start(bf16[6,4,2304]{2,1,0:T(4,128)(2,1)S(1)} %collective-permute-done.1), channel_id=1, source_target_pairs={{0,7},{1,0},{2,1},{3,2},{4,3},{5,4},{6,5},{7,6},{8,15},{9,8},{10,9... | collective-permute-start | bytes 331784 | tf_op jit(solution)/shard_map/ppermute | solution.py:28
  67.9 2.1 %collective-permute-done.5 = bf16[6,4,2304]{2,1,0:T(4,128)(2,1)S(1)} collective-permute-done((bf16[6,4,2304]{2,1,0:T(4,128)(2,1)S(1)}, bf16[6,4,2304]{2,1,0:T(4,128)(2,1)S(1)}, u32[]{:S(2)}, u32[]{:S(2)}) %collective-permute-start.5) | collective-permute-done | bytes 110624 | tf_op jit(solution)/shard_map/ppermute | solution.py:27
  70.0 5.6 %collective-permute-start.6 = (bf16[6,4,1152]{2,1,0:T(4,128)(2,1)S(1)}, bf16[6,4,1152]{2,1,0:T(4,128)(2,1)S(1)}, u32[]{:S(2)}, u32[]{:S(2)}) collective-permute-start(bf16[6,4,1152]{2,1,0:T(4,128)(2,1)S(1)} %slice.84), channel_id=1, source_target_pairs={{0,1},{1,2},{2,3},{3,4},{4,5},{5,6},{6,7},{7,0},{8,9},{9,10},{10,1... | collective-permute-start | bytes 165896 | tf_op jit(solution)/shard_map/ppermute | solution.py:23
  75.7 1.9 %collective-permute-start.7 = (bf16[6,4,1152]{2,1,0:T(4,128)(2,1)S(1)}, bf16[6,4,1152]{2,1,0:T(4,128)(2,1)S(1)}, u32[]{:S(2)}, u32[]{:S(2)}) collective-permute-start(bf16[6,4,1152]{2,1,0:T(4,128)(2,1)S(1)} %slice.85), channel_id=1, source_target_pairs={{0,7},{1,0},{2,1},{3,2},{4,3},{5,4},{6,5},{7,6},{8,15},{9,8},{10,9... | collective-permute-start | bytes 165896 | tf_op jit(solution)/shard_map/ppermute | solution.py:24
  78.2 0.2 copy.134
  78.4 0.2 copy.135
  78.6 0.2 copy.141
  78.8 0.2 copy.136
  79.0 0.2 copy.140
  79.1 0.2 copy.137
  79.3 0.2 copy.139
  79.5 3.4 %collective-permute-done.7 = bf16[6,4,1152]{2,1,0:T(4,128)(2,1)S(1)} collective-permute-done((bf16[6,4,1152]{2,1,0:T(4,128)(2,1)S(1)}, bf16[6,4,1152]{2,1,0:T(4,128)(2,1)S(1)}, u32[]{:S(2)}, u32[]{:S(2)}) %collective-permute-start.7) | collective-permute-done | bytes 55328 | tf_op jit(solution)/shard_map/ppermute | solution.py:24
  83.0 0.2 copy.138
  83.2 2.8 %stack.41 = bf16[8,6,4,2304]{3,0,2,1:T(8,128)(2,1)S(1)} concatenate(bf16[1,6,4,2304]{3,0,2,1:T(2,128)(2,1)S(1)} %copy.134, bf16[1,6,4,2304]{3,0,2,1:T(2,128)(2,1)S(1)} %copy.135, bf16[1,6,4,2304]{3,0,2,1:T(2,128)(2,1)S(1)} %copy.136, bf16[1,6,4,2304]{3,0,2,1:T(2,128)(2,1)S(1)} %copy.137, bf16[1,6,4,2304]{3,0,2,1:T(2,128)(2,1)S(1)} %copy.138, bf16[1,6,4,2304]{3,0,2,1:T(2,128)(2,1)S(1)} %copy.139, ...), dimensions={0} | concatenate | bytes 1769472 | tf_op jit(solution)/shard_map/stack | solution.py:77
  85.9 4.6 %collective-permute-start.8 = (bf16[8,6,4,2304]{3,0,2,1:T(8,128)(2,1)S(1)}, bf16[8,6,4,2304]{3,0,2,1:T(8,128)(2,1)}, u32[]{:S(2)}, u32[]{:S(2)}) collective-permute-start(bf16[8,6,4,2304]{3,0,2,1:T(8,128)(2,1)S(1)} %stack.41), channel_id=1, source_target_pairs={{0,24},{8,0},{16,8},{24,16},{1,25},{9,1},{17,9},{25,17},{2,26},{10... | collective-permute-start | bytes 2654216 | tf_op jit(solution)/shard_map/ppermute | solution.py:28
  90.6 1.9 %collective-permute-start.10 = (bf16[8,6,4,2304]{3,0,2,1:T(8,128)(2,1)S(1)}, bf16[8,6,4,2304]{3,0,2,1:T(8,128)(2,1)}, u32[]{:S(2)}, u32[]{:S(2)}) collective-permute-start(bf16[8,6,4,2304]{3,0,2,1:T(8,128)(2,1)S(1)} %stack.41), channel_id=1, source_target_pairs={{0,8},{8,16},{16,24},{24,0},{1,9},{9,17},{17,25},{25,1},{2,10},{10... | collective-permute-start | bytes 2654216 | tf_op jit(solution)/shard_map/ppermute | solution.py:27
  92.5 1.6 slice.93
  94.1 0.1 slice_reduce_fusion.3
  94.3 0.6 fusion.7
  94.9 0.8 bitcast_dynamic-update-slice_fusion.6
  95.7 25.0 %collective-permute-done.8 = bf16[8,6,4,2304]{3,0,2,1:T(8,128)(2,1)} collective-permute-done((bf16[8,6,4,2304]{3,0,2,1:T(8,128)(2,1)S(1)}, bf16[8,6,4,2304]{3,0,2,1:T(8,128)(2,1)}, u32[]{:S(2)}, u32[]{:S(2)}) %collective-permute-start.8) | collective-permute-done | bytes 884768 | tf_op jit(solution)/shard_map/ppermute | solution.py:28
  120.7 1.1 slice.88
  121.8 5.7 %collective-permute-start.9 = (bf16[8,6,4,1152]{3,0,2,1:T(8,128)(2,1)S(1)}, bf16[8,6,4,1152]{3,0,2,1:T(8,128)(2,1)S(1)}, u32[]{:S(2)}, u32[]{:S(2)}) collective-permute-start(bf16[8,6,4,1152]{3,0,2,1:T(8,128)(2,1)S(1)} %slice.88), channel_id=1, source_target_pairs={{0,24},{8,0},{16,8},{24,16},{1,25},{9,1},{17,9},{25,17},{2,26},{10... | collective-permute-start | bytes 1327112 | tf_op jit(solution)/shard_map/ppermute | solution.py:24
  127.5 1.4 collective-permute-done.10
  128.9 1.0 slice.94
  129.9 2.1 %collective-permute-start.11 = (bf16[8,6,4,1152]{3,0,2,1:T(8,128)(2,1)S(1)}, bf16[8,6,4,1152]{3,0,2,1:T(8,128)(2,1)}, u32[]{:S(2)}, u32[]{:S(2)}) collective-permute-start(bf16[8,6,4,1152]{3,0,2,1:T(8,128)(2,1)S(1)} %slice.94), channel_id=1, source_target_pairs={{0,8},{8,16},{16,24},{24,0},{1,9},{9,17},{17,25},{25,1},{2,10},{10... | collective-permute-start | bytes 1327112 | tf_op jit(solution)/shard_map/ppermute | solution.py:23
  132.0 0.9 slice_reduce_fusion.2
  132.9 0.9 slice_reduce_fusion
  133.9 1.8 %fusion.5 = f32[8,6,4,3,128]{4,0,3,2,1:T(8,128)S(1)} fusion(bf16[3,2176,128]{2,1,0:T(8,128)(2,1)S(1)} %slice.93, bf16[8,6,4,2304]{3,0,2,1:T(8,128)(2,1)} %collective-permute-done.8), kind=kOutput, calls=%fused_computation.12 | convolution fusion | flops 339738624 | bytes 2850816 | tf_op jit(solution)/shard_map/rd,edc->rec/dot_general | solution.py:72
  135.7 0.8 bitcast_dynamic-update-slice_fusion.4
  136.5 1.8 %fusion.1 = f32[8,6,4,3,128]{4,0,3,2,1:T(8,128)S(1)} fusion(bf16[3,2176,128]{2,1,0:T(8,128)(2,1)S(1)} %slice.93, bf16[8,6,4,2304]{3,0,2,1:T(8,128)(2,1)} %collective-permute-done.10), kind=kOutput, calls=%fused_computation.8 | convolution fusion | flops 339738624 | bytes 2850816 | tf_op jit(solution)/shard_map/rd,edc->rec/dot_general | solution.py:72
  138.3 0.1 slice_reduce_fusion.1
  138.6 0.5 copy-done.2
  139.1 0.1 fusion.26
  139.2 0.2 copy.142
  139.5 0.1 reshape.246
  139.6 0.6 gather_fusion.2
  140.2 2.8 %collective-permute-done.11 = bf16[8,6,4,1152]{3,0,2,1:T(8,128)(2,1)} collective-permute-done((bf16[8,6,4,1152]{3,0,2,1:T(8,128)(2,1)S(1)}, bf16[8,6,4,1152]{3,0,2,1:T(8,128)(2,1)}, u32[]{:S(2)}, u32[]{:S(2)}) %collective-permute-start.11) | collective-permute-done | bytes 442400 | tf_op jit(solution)/shard_map/ppermute | solution.py:23
  143.0 1.8 %fusion.3 = f32[8,6,4,3,128]{4,0,3,2,1:T(8,128)S(1)} fusion(bf16[3,2176,128]{2,1,0:T(8,128)(2,1)S(1)} %slice.93, bf16[8,6,4,1152]{3,0,2,1:T(8,128)(2,1)} %copy-done.2, bf16[8,6,4,1152]{3,0,2,1:T(8,128)(2,1)} %collective-permute-done.11), kind=kOutput, calls=%fused_computation.10 | convolution fusion | flops 341508096 | bytes 2850816 | tf_op jit(solution)/shard_map/rd,edc->rec/dot_general | solution.py:72
  145.4 0.2 constant_dynamic-slice_fusion
  145.7 7.4 %fusion.10 = f32[6,3,4,8,4,128]{5,4,1,0,3,2:T(4,128)S(1)} fusion(bf16[4,8,6,4,3200,1]{4,3,5,2,1,0:T(4,128)(2,1)} %bitcast.136, bf16[3,5376,128]{2,1,0:T(8,128)(2,1)} %bitcast.125, s32[]{:T(128)S(6)} %select_n.190, f32[4,8,6,4,3,128]{5,3,4,2,1,0:T(4,128)S(1)} %constant_dynamic-slice_fusion), kind=kOutput, calls=%fused_computation.17 | convolution fusion | flops 1888026624 | bytes 9732100 | tf_op jit(solution)/shard_map/rd,edc->rec/dot_general | solution.py:72
  153.1 0.3 copy.147
  153.5 0.6 gather_fusion.3
  154.1 1.2 fusion.18
  (42 shorter events, 1.1 us)
Async XLA Ops:
  10.0 12.9 %copy-start.1 = (s32[16,6]{0,1:T(8,128)S(1)}, s32[16,6]{0,1:T(8,128)}, u32[]{:S(2)}) copy-start(s32[16,6]{0,1:T(8,128)} %param.11) | copy-start | bytes 1156
  10.0 13.1 %copy-start.3 = (s32[1,1,18,2]{2,3,1,0:T(2,128)S(1)}, s32[1,1,18,2]{2,3,1,0:T(2,128)}, u32[]{:S(2)}) copy-start(s32[1,1,18,2]{2,3,1,0:T(2,128)} %param.12) | copy-start | bytes 436
  12.4 29.6 %all-to-all-start = ((bf16[16,4,5504]{2,1,0:T(4,128)(2,1)}), bf16[16,4,5504]{2,1,0:T(4,128)(2,1)S(1)}, u32[]{:S(2)}, u32[]{:S(2)}) async-start(bf16[16,4,5504]{2,1,0:T(4,128)(2,1)} %broadcast_select_fusion), calls=%async_computation | async-start | bytes 1409024 | tf_op jit(solution)/shard_map/all_to_all | solution.py:52
  22.8 122.9 %all-gather.3.cloned.1.call-start = ((), (), s32[]{:S(2)}) async-start(), calls=%async_computation.1 | async-start | bytes 5068800 | tf_op jit(solution)/shard_map/all_gather | solution.py:74
  43.8 7.0 %collective-permute-start.3 = (bf16[6,4,2304]{2,1,0:T(4,128)(2,1)S(1)}, bf16[6,4,2304]{2,1,0:T(4,128)(2,1)S(1)}, u32[]{:S(2)}, u32[]{:S(2)}) collective-permute-start(bf16[6,4,2304]{2,1,0:T(4,128)(2,1)S(1)} %get-tuple-element.19), channel_id=1, source_target_pairs={{0,1},{1,2},{2,3},{3,4},{4,5},{5,6},{6,7},{7,0},{8,9},{9,10},{10,1... | collective-permute-start | bytes 331784 | tf_op jit(solution)/shard_map/ppermute | solution.py:27
  48.5 8.0 %collective-permute-start = (bf16[6,4,2304]{2,1,0:T(4,128)(2,1)S(1)}, bf16[6,4,2304]{2,1,0:T(4,128)(2,1)S(1)}, u32[]{:S(2)}, u32[]{:S(2)}) collective-permute-start(bf16[6,4,2304]{2,1,0:T(4,128)(2,1)S(1)} %get-tuple-element.19), channel_id=1, source_target_pairs={{0,7},{1,0},{2,1},{3,2},{4,3},{5,4},{6,5},{7,6},{8,15},{9,8},{10,9... | collective-permute-start | bytes 331784 | tf_op jit(solution)/shard_map/ppermute | solution.py:28
  50.8 9.6 %collective-permute-start.4 = (bf16[6,4,2304]{2,1,0:T(4,128)(2,1)S(1)}, bf16[6,4,2304]{2,1,0:T(4,128)(2,1)S(1)}, u32[]{:S(2)}, u32[]{:S(2)}) collective-permute-start(bf16[6,4,2304]{2,1,0:T(4,128)(2,1)S(1)} %collective-permute-done.3), channel_id=1, source_target_pairs={{0,1},{1,2},{2,3},{3,4},{4,5},{5,6},{6,7},{7,0},{8,9},{9,10},{10,1... | collective-permute-start | bytes 331784 | tf_op jit(solution)/shard_map/ppermute | solution.py:27
  56.5 9.5 %collective-permute-start.1 = (bf16[6,4,2304]{2,1,0:T(4,128)(2,1)S(1)}, bf16[6,4,2304]{2,1,0:T(4,128)(2,1)S(1)}, u32[]{:S(2)}, u32[]{:S(2)}) collective-permute-start(bf16[6,4,2304]{2,1,0:T(4,128)(2,1)S(1)} %collective-permute-done), channel_id=1, source_target_pairs={{0,7},{1,0},{2,1},{3,2},{4,3},{5,4},{6,5},{7,6},{8,15},{9,8},{10,9... | collective-permute-start | bytes 331784 | tf_op jit(solution)/shard_map/ppermute | solution.py:28
  60.4 9.6 %collective-permute-start.5 = (bf16[6,4,2304]{2,1,0:T(4,128)(2,1)S(1)}, bf16[6,4,2304]{2,1,0:T(4,128)(2,1)S(1)}, u32[]{:S(2)}, u32[]{:S(2)}) collective-permute-start(bf16[6,4,2304]{2,1,0:T(4,128)(2,1)S(1)} %collective-permute-done.4), channel_id=1, source_target_pairs={{0,1},{1,2},{2,3},{3,4},{4,5},{5,6},{6,7},{7,0},{8,9},{9,10},{10,1... | collective-permute-start | bytes 331784 | tf_op jit(solution)/shard_map/ppermute | solution.py:27
  66.0 9.6 %collective-permute-start.2 = (bf16[6,4,2304]{2,1,0:T(4,128)(2,1)S(1)}, bf16[6,4,2304]{2,1,0:T(4,128)(2,1)S(1)}, u32[]{:S(2)}, u32[]{:S(2)}) collective-permute-start(bf16[6,4,2304]{2,1,0:T(4,128)(2,1)S(1)} %collective-permute-done.1), channel_id=1, source_target_pairs={{0,7},{1,0},{2,1},{3,2},{4,3},{5,4},{6,5},{7,6},{8,15},{9,8},{10,9... | collective-permute-start | bytes 331784 | tf_op jit(solution)/shard_map/ppermute | solution.py:28
  70.0 9.5 %collective-permute-start.6 = (bf16[6,4,1152]{2,1,0:T(4,128)(2,1)S(1)}, bf16[6,4,1152]{2,1,0:T(4,128)(2,1)S(1)}, u32[]{:S(2)}, u32[]{:S(2)}) collective-permute-start(bf16[6,4,1152]{2,1,0:T(4,128)(2,1)S(1)} %slice.84), channel_id=1, source_target_pairs={{0,1},{1,2},{2,3},{3,4},{4,5},{5,6},{6,7},{7,0},{8,9},{9,10},{10,1... | collective-permute-start | bytes 165896 | tf_op jit(solution)/shard_map/ppermute | solution.py:23
  75.7 7.3 %collective-permute-start.7 = (bf16[6,4,1152]{2,1,0:T(4,128)(2,1)S(1)}, bf16[6,4,1152]{2,1,0:T(4,128)(2,1)S(1)}, u32[]{:S(2)}, u32[]{:S(2)}) collective-permute-start(bf16[6,4,1152]{2,1,0:T(4,128)(2,1)S(1)} %slice.85), channel_id=1, source_target_pairs={{0,7},{1,0},{2,1},{3,2},{4,3},{5,4},{6,5},{7,6},{8,15},{9,8},{10,9... | collective-permute-start | bytes 165896 | tf_op jit(solution)/shard_map/ppermute | solution.py:24
  85.9 34.8 %collective-permute-start.8 = (bf16[8,6,4,2304]{3,0,2,1:T(8,128)(2,1)S(1)}, bf16[8,6,4,2304]{3,0,2,1:T(8,128)(2,1)}, u32[]{:S(2)}, u32[]{:S(2)}) collective-permute-start(bf16[8,6,4,2304]{3,0,2,1:T(8,128)(2,1)S(1)} %stack.41), channel_id=1, source_target_pairs={{0,24},{8,0},{16,8},{24,16},{1,25},{9,1},{17,9},{25,17},{2,26},{10... | collective-permute-start | bytes 2654216 | tf_op jit(solution)/shard_map/ppermute | solution.py:28
  90.6 38.3 %collective-permute-start.10 = (bf16[8,6,4,2304]{3,0,2,1:T(8,128)(2,1)S(1)}, bf16[8,6,4,2304]{3,0,2,1:T(8,128)(2,1)}, u32[]{:S(2)}, u32[]{:S(2)}) collective-permute-start(bf16[8,6,4,2304]{3,0,2,1:T(8,128)(2,1)S(1)} %stack.41), channel_id=1, source_target_pairs={{0,8},{8,16},{16,24},{24,0},{1,9},{9,17},{17,25},{25,1},{2,10},{10... | collective-permute-start | bytes 2654216 | tf_op jit(solution)/shard_map/ppermute | solution.py:27
  121.8 16.6 %collective-permute-start.9 = (bf16[8,6,4,1152]{3,0,2,1:T(8,128)(2,1)S(1)}, bf16[8,6,4,1152]{3,0,2,1:T(8,128)(2,1)S(1)}, u32[]{:S(2)}, u32[]{:S(2)}) collective-permute-start(bf16[8,6,4,1152]{3,0,2,1:T(8,128)(2,1)S(1)} %slice.88), channel_id=1, source_target_pairs={{0,24},{8,0},{16,8},{24,16},{1,25},{9,1},{17,9},{25,17},{2,26},{10... | collective-permute-start | bytes 1327112 | tf_op jit(solution)/shard_map/ppermute | solution.py:24
  129.9 13.0 %collective-permute-start.11 = (bf16[8,6,4,1152]{3,0,2,1:T(8,128)(2,1)S(1)}, bf16[8,6,4,1152]{3,0,2,1:T(8,128)(2,1)}, u32[]{:S(2)}, u32[]{:S(2)}) collective-permute-start(bf16[8,6,4,1152]{3,0,2,1:T(8,128)(2,1)S(1)} %slice.94), channel_id=1, source_target_pairs={{0,8},{8,16},{16,24},{24,0},{1,9},{9,17},{17,25},{25,1},{2,10},{10... | collective-permute-start | bytes 1327112 | tf_op jit(solution)/shard_map/ppermute | solution.py:23
  138.3 0.8 copy-start.2
  140.2 4.6 %copy-start = (f32[8,8,6,4,3,128]{5,3,4,2,1,0:T(4,128)S(1)}, f32[8,8,6,4,3,128]{5,3,4,2,1,0:T(4,128)}, u32[]{:S(2)}) copy-start(f32[8,8,6,4,3,128]{5,3,4,2,1,0:T(4,128)} %bitcast_dynamic-update-slice_fusion.4) | copy-start | bytes 7077892
Sparse Core Ops, SparseCore 0:
  43.8 99.9 all-gather.2

commit v5 on v4

--- a/solution.py
+++ b/solution.py
@@ -18,11 +18,10 @@
     down = [(i, (i - 1) % n) for i in range(n)]
     for step in range(1, n // 2 + 1):
         if 2 * step == n:
-            cols = block.shape[-1]
-            half = (cols // 2) // LANES * LANES
-            got_left = lax.ppermute(left[..., :half], axis, up)
-            got_right = lax.ppermute(right[..., half:], axis, down)
-            parts[step] = jnp.concatenate([got_left, got_right], axis=-1)
+            half = block.shape[0] // 2
+            got_left = lax.ppermute(left[:half], axis, up)
+            got_right = lax.ppermute(right[half:], axis, down)
+            parts[step] = jnp.concatenate([got_left, got_right], axis=0)
         else:
             left = lax.ppermute(left, axis, up)
             right = lax.ppermute(right, axis, down)

time: 163 us -> 163 us (level)
  the two profiles are of different devices: /device:TPU:24 before, /device:TPU:26 now
where the time goes in v5:
time: 163 us; the launch traced here: 162 us
  waiting for transfers between devices  57 us (35%)
  starting transfers between devices  51.6 us (32%)
  local copies, waits for them, and re-layouts  19.4 us (12%)
  between operations  14.6 us (9%)
  matrix products  13.5 us (8%)
  other arithmetic  5.81 us (4%)
    ppermute x4, waiting for transfers between devices, ring_parts(): left = lax.ppermute(left, axis, up)  28.6 us
    ppermute x4, starting transfers between devices, ring_parts(): left = lax.ppermute(left, axis, up)  19.1 us
    all_to_all x1, waiting for transfers between devices, local(): recv = lax.all_to_all(send, GRP, 0, 0, tiled=True)  18.8 us
    dot_general x5, matrix products, mm(): jnp.einsum('rd,edc->rec', flat, enc, preferred_element_type=jnp.float32)  13.5 us
    all_to_all x1, starting transfers between devices, local(): recv = lax.all_to_all(send, GRP, 0, 0, tiled=True)  10.4 us
    ppermute x2, starting transfers between devices, ring_parts(): got_left = lax.ppermute(left[:half], axis, up)  8.91 us
    ppermute x4, starting transfers between devices, ring_parts(): right = lax.ppermute(right, axis, down)  8.31 us
    ppermute x2, waiting for transfers between devices, ring_parts(): got_right = lax.ppermute(right[half:], axis, down)  6.97 us
  transfers between devices with their start and end apart: 14, of which 10 were waited for; matrix products, arithmetic and copies ran while one was open for 13% of the time, Pallas kernels for 0%

profile of v5, /device:TPU:26, one launch (start us, length us, event | category | flops | bytes accessed | tf_op | source)
XLA Modules:
  0.0 161.8 jit_solution(8411761208465744015)
XLA Ops:
  6.5 0.7 fusion.31
  7.3 0.8 and_bitcast_fusion
  8.0 0.8 copy.157
  8.8 1.1 fusion.25
  10.0 1.2 gather_fusion
  11.2 1.2 broadcast_select_fusion
  12.4 10.4 %all-to-all-start = ((bf16[16,4,5504]{2,1,0:T(4,128)(2,1)}), bf16[16,4,5504]{2,1,0:T(4,128)(2,1)S(1)}, u32[]{:S(2)}, u32[]{:S(2)}) async-start(bf16[16,4,5504]{2,1,0:T(4,128)(2,1)} %broadcast_select_fusion), calls=%async_computation | async-start | bytes 1409024 | tf_op jit(solution)/shard_map/all_to_all | solution.py:51
  22.9 0.2 dynamic-slice_reduce_fusion
  23.1 18.8 %all-to-all-done = bf16[16,4,5504]{2,1,0:T(4,128)(2,1)S(1)} async-done(((bf16[16,4,5504]{2,1,0:T(4,128)(2,1)}), bf16[16,4,5504]{2,1,0:T(4,128)(2,1)S(1)}, u32[]{:S(2)}, u32[]{:S(2)}) %all-to-all-start) | async-done | bytes 704544 | tf_op jit(solution)/shard_map/all_to_all | solution.py:51
  42.0 0.8 gather_fusion.1
  42.8 0.2 select_select_fusion
  43.0 0.7 slice.93
  43.8 4.7 %collective-permute-start.3 = (bf16[6,4,2304]{2,1,0:T(4,128)(2,1)S(1)}, bf16[6,4,2304]{2,1,0:T(4,128)(2,1)S(1)}, u32[]{:S(2)}, u32[]{:S(2)}) collective-permute-start(bf16[6,4,2304]{2,1,0:T(4,128)(2,1)S(1)} %get-tuple-element.19), channel_id=1, source_target_pairs={{0,1},{1,2},{2,3},{3,4},{4,5},{5,6},{6,7},{7,0},{8,9},{9,10},{10,1... | collective-permute-start | bytes 331784 | tf_op jit(solution)/shard_map/ppermute | solution.py:26
  48.5 1.9 %collective-permute-start = (bf16[6,4,2304]{2,1,0:T(4,128)(2,1)S(1)}, bf16[6,4,2304]{2,1,0:T(4,128)(2,1)S(1)}, u32[]{:S(2)}, u32[]{:S(2)}) collective-permute-start(bf16[6,4,2304]{2,1,0:T(4,128)(2,1)S(1)} %get-tuple-element.19), channel_id=1, source_target_pairs={{0,7},{1,0},{2,1},{3,2},{4,3},{5,4},{6,5},{7,6},{8,15},{9,8},{10,9... | collective-permute-start | bytes 331784 | tf_op jit(solution)/shard_map/ppermute | solution.py:27
  50.4 0.4 collective-permute-done.3
  50.8 5.5 %collective-permute-start.4 = (bf16[6,4,2304]{2,1,0:T(4,128)(2,1)S(1)}, bf16[6,4,2304]{2,1,0:T(4,128)(2,1)S(1)}, u32[]{:S(2)}, u32[]{:S(2)}) collective-permute-start(bf16[6,4,2304]{2,1,0:T(4,128)(2,1)S(1)} %collective-permute-done.3), channel_id=1, source_target_pairs={{0,1},{1,2},{2,3},{3,4},{4,5},{5,6},{6,7},{7,0},{8,9},{9,10},{10,1... | collective-permute-start | bytes 331784 | tf_op jit(solution)/shard_map/ppermute | solution.py:26
  56.3 0.2 collective-permute-done
  56.5 1.9 %collective-permute-start.1 = (bf16[6,4,2304]{2,1,0:T(4,128)(2,1)S(1)}, bf16[6,4,2304]{2,1,0:T(4,128)(2,1)S(1)}, u32[]{:S(2)}, u32[]{:S(2)}) collective-permute-start(bf16[6,4,2304]{2,1,0:T(4,128)(2,1)S(1)} %collective-permute-done), channel_id=1, source_target_pairs={{0,7},{1,0},{2,1},{3,2},{4,3},{5,4},{6,5},{7,6},{8,15},{9,8},{10,9... | collective-permute-start | bytes 331784 | tf_op jit(solution)/shard_map/ppermute | solution.py:27
  58.4 2.0 %collective-permute-done.4 = bf16[6,4,2304]{2,1,0:T(4,128)(2,1)S(1)} collective-permute-done((bf16[6,4,2304]{2,1,0:T(4,128)(2,1)S(1)}, bf16[6,4,2304]{2,1,0:T(4,128)(2,1)S(1)}, u32[]{:S(2)}, u32[]{:S(2)}) %collective-permute-start.4) | collective-permute-done | bytes 110624 | tf_op jit(solution)/shard_map/ppermute | solution.py:26
  60.4 5.6 %collective-permute-start.5 = (bf16[6,4,2304]{2,1,0:T(4,128)(2,1)S(1)}, bf16[6,4,2304]{2,1,0:T(4,128)(2,1)S(1)}, u32[]{:S(2)}, u32[]{:S(2)}) collective-permute-start(bf16[6,4,2304]{2,1,0:T(4,128)(2,1)S(1)} %collective-permute-done.4), channel_id=1, source_target_pairs={{0,1},{1,2},{2,3},{3,4},{4,5},{5,6},{6,7},{7,0},{8,9},{9,10},{10,1... | collective-permute-start | bytes 331784 | tf_op jit(solution)/shard_map/ppermute | solution.py:26
  66.0 1.9 %collective-permute-start.2 = (bf16[6,4,2304]{2,1,0:T(4,128)(2,1)S(1)}, bf16[6,4,2304]{2,1,0:T(4,128)(2,1)S(1)}, u32[]{:S(2)}, u32[]{:S(2)}) collective-permute-start(bf16[6,4,2304]{2,1,0:T(4,128)(2,1)S(1)} %collective-permute-done.1), channel_id=1, source_target_pairs={{0,7},{1,0},{2,1},{3,2},{4,3},{5,4},{6,5},{7,6},{8,15},{9,8},{10,9... | collective-permute-start | bytes 331784 | tf_op jit(solution)/shard_map/ppermute | solution.py:27
  68.0 1.8 %collective-permute-done.5 = bf16[6,4,2304]{2,1,0:T(4,128)(2,1)S(1)} collective-permute-done((bf16[6,4,2304]{2,1,0:T(4,128)(2,1)S(1)}, bf16[6,4,2304]{2,1,0:T(4,128)(2,1)S(1)}, u32[]{:S(2)}, u32[]{:S(2)}) %collective-permute-start.5) | collective-permute-done | bytes 110624 | tf_op jit(solution)/shard_map/ppermute | solution.py:26
  69.8 5.6 %collective-permute-start.6 = (bf16[3,4,2304]{2,1,0:T(4,128)(2,1)S(1)}, bf16[3,4,2304]{2,1,0:T(4,128)(2,1)S(1)}, u32[]{:S(2)}, u32[]{:S(2)}) collective-permute-start(bf16[3,4,2304]{2,1,0:T(4,128)(2,1)S(1)} %slice.84), channel_id=1, source_target_pairs={{0,1},{1,2},{2,3},{3,4},{4,5},{5,6},{6,7},{7,0},{8,9},{9,10},{10,1... | collective-permute-start | bytes 165896 | tf_op jit(solution)/shard_map/ppermute | solution.py:22
  75.5 1.9 %collective-permute-start.7 = (bf16[3,4,2304]{2,1,0:T(4,128)(2,1)S(1)}, bf16[3,4,2304]{2,1,0:T(4,128)(2,1)S(1)}, u32[]{:S(2)}, u32[]{:S(2)}) collective-permute-start(bf16[3,4,2304]{2,1,0:T(4,128)(2,1)S(1)} %slice.85), channel_id=1, source_target_pairs={{0,7},{1,0},{2,1},{3,2},{4,3},{5,4},{6,5},{7,6},{8,15},{9,8},{10,9... | collective-permute-start | bytes 165896 | tf_op jit(solution)/shard_map/ppermute | solution.py:23
  78.0 0.2 copy.136
  78.2 0.2 copy.137
  78.4 0.2 copy.143
  78.6 0.2 copy.138
  78.8 0.2 copy.142
  78.9 0.2 copy.139
  79.1 0.2 copy.141
  79.3 3.5 %collective-permute-done.7 = bf16[3,4,2304]{2,1,0:T(4,128)(2,1)S(1)} collective-permute-done((bf16[3,4,2304]{2,1,0:T(4,128)(2,1)S(1)}, bf16[3,4,2304]{2,1,0:T(4,128)(2,1)S(1)}, u32[]{:S(2)}, u32[]{:S(2)}) %collective-permute-start.7) | collective-permute-done | bytes 55328 | tf_op jit(solution)/shard_map/ppermute | solution.py:23
  82.9 0.2 copy.140
  83.1 2.8 %stack.41 = bf16[8,6,4,2304]{3,0,2,1:T(8,128)(2,1)S(1)} concatenate(bf16[1,6,4,2304]{3,0,2,1:T(2,128)(2,1)S(1)} %copy.136, bf16[1,6,4,2304]{3,0,2,1:T(2,128)(2,1)S(1)} %copy.137, bf16[1,6,4,2304]{3,0,2,1:T(2,128)(2,1)S(1)} %copy.138, bf16[1,6,4,2304]{3,0,2,1:T(2,128)(2,1)S(1)} %copy.139, bf16[1,6,4,2304]{3,0,2,1:T(2,128)(2,1)S(1)} %copy.140, bf16[1,6,4,2304]{3,0,2,1:T(2,128)(2,1)S(1)} %copy.141, ...), dimensions={0} | concatenate | bytes 1769472 | tf_op jit(solution)/shard_map/stack | solution.py:76
  85.9 3.3 %collective-permute-start.9 = (bf16[8,6,4,2304]{3,0,2,1:T(8,128)(2,1)S(1)}, bf16[8,6,4,2304]{3,0,2,1:T(8,128)(2,1)}, u32[]{:S(2)}, u32[]{:S(2)}) collective-permute-start(bf16[8,6,4,2304]{3,0,2,1:T(8,128)(2,1)S(1)} %stack.41), channel_id=1, source_target_pairs={{0,8},{8,16},{16,24},{24,0},{1,9},{9,17},{17,25},{25,1},{2,10},{10... | collective-permute-start | bytes 2654216 | tf_op jit(solution)/shard_map/ppermute | solution.py:26
  89.1 2.6 %collective-permute-start.8 = (bf16[8,6,4,2304]{3,0,2,1:T(8,128)(2,1)S(1)}, bf16[8,6,4,2304]{3,0,2,1:T(8,128)(2,1)}, u32[]{:S(2)}, u32[]{:S(2)}) collective-permute-start(bf16[8,6,4,2304]{3,0,2,1:T(8,128)(2,1)S(1)} %stack.41), channel_id=1, source_target_pairs={{0,24},{8,0},{16,8},{24,16},{1,25},{9,1},{17,9},{25,17},{2,26},{10... | collective-permute-start | bytes 2654216 | tf_op jit(solution)/shard_map/ppermute | solution.py:27
  91.8 1.6 slice.95
  93.5 0.6 fusion.7
  94.1 0.8 bitcast_dynamic-update-slice_fusion.6
  94.9 24.4 %collective-permute-done.9 = bf16[8,6,4,2304]{3,0,2,1:T(8,128)(2,1)} collective-permute-done((bf16[8,6,4,2304]{3,0,2,1:T(8,128)(2,1)S(1)}, bf16[8,6,4,2304]{3,0,2,1:T(8,128)(2,1)}, u32[]{:S(2)}, u32[]{:S(2)}) %collective-permute-start.9) | collective-permute-done | bytes 884768 | tf_op jit(solution)/shard_map/ppermute | solution.py:26
  119.3 1.3 slice.88
  120.6 3.3 %collective-permute-start.10 = (bf16[4,6,4,2304]{3,0,2,1:T(4,128)(2,1)S(1)}, bf16[4,6,4,2304]{3,0,2,1:T(4,128)(2,1)S(1)}, u32[]{:S(2)}, u32[]{:S(2)}) collective-permute-start(bf16[4,6,4,2304]{3,0,2,1:T(4,128)(2,1)S(1)} %slice.88), channel_id=1, source_target_pairs={{0,8},{8,16},{16,24},{24,0},{1,9},{9,17},{17,25},{25,1},{2,10},{10... | collective-permute-start | bytes 1327112 | tf_op jit(solution)/shard_map/ppermute | solution.py:22
  124.0 1.1 collective-permute-done.8
  125.1 1.5 slice.89
  126.6 2.9 %collective-permute-start.11 = (bf16[4,6,4,2304]{3,0,2,1:T(4,128)(2,1)S(1)}, bf16[4,6,4,2304]{3,0,2,1:T(4,128)(2,1)S(1)}, u32[]{:S(2)}, u32[]{:S(2)}) collective-permute-start(bf16[4,6,4,2304]{3,0,2,1:T(4,128)(2,1)S(1)} %slice.89), channel_id=1, source_target_pairs={{0,24},{8,0},{16,8},{24,16},{1,25},{9,1},{17,9},{25,17},{2,26},{10... | collective-permute-start | bytes 1327112 | tf_op jit(solution)/shard_map/ppermute | solution.py:23
  129.5 0.9 slice_reduce_fusion.1
  130.4 0.9 slice_reduce_fusion
  131.3 1.8 %fusion.5 = f32[8,6,4,3,128]{4,0,3,2,1:T(8,128)S(1)} fusion(bf16[3,2176,128]{2,1,0:T(8,128)(2,1)S(1)} %slice.95, bf16[8,6,4,2304]{3,0,2,1:T(8,128)(2,1)} %collective-permute-done.8), kind=kOutput, calls=%fused_computation.12 | convolution fusion | flops 339738624 | bytes 2850816 | tf_op jit(solution)/shard_map/rd,edc->rec/dot_general | solution.py:71
  133.1 0.8 bitcast_dynamic-update-slice_fusion.4
  134.0 1.8 %fusion.1 = f32[8,6,4,3,128]{4,0,3,2,1:T(8,128)S(1)} fusion(bf16[3,2176,128]{2,1,0:T(8,128)(2,1)S(1)} %slice.95, bf16[8,6,4,2304]{3,0,2,1:T(8,128)(2,1)} %collective-permute-done.9), kind=kOutput, calls=%fused_computation.8 | convolution fusion | flops 339738624 | bytes 2850816 | tf_op jit(solution)/shard_map/rd,edc->rec/dot_general | solution.py:71
  135.8 1.3 collective-permute-done.10
  137.0 3.5 %collective-permute-done.11 = bf16[4,6,4,2304]{3,0,2,1:T(4,128)(2,1)S(1)} collective-permute-done((bf16[4,6,4,2304]{3,0,2,1:T(4,128)(2,1)S(1)}, bf16[4,6,4,2304]{3,0,2,1:T(4,128)(2,1)S(1)}, u32[]{:S(2)}, u32[]{:S(2)}) %collective-permute-start.11) | collective-permute-done | bytes 442400 | tf_op jit(solution)/shard_map/ppermute | solution.py:23
  140.5 0.8 copy-done.1
  141.2 0.1 fusion.27
  141.5 0.1 fusion.28
  141.6 0.2 copy.144
  141.9 0.1 reshape.246
  142.0 0.6 gather_fusion.2
  142.6 1.8 %fusion.3 = f32[8,6,4,3,128]{4,0,3,2,1:T(8,128)S(1)} fusion(bf16[3,2176,128]{2,1,0:T(8,128)(2,1)S(1)} %slice.95, bf16[4,6,4,2304]{3,0,2,1:T(4,128)(2,1)} %copy-done.1, bf16[4,6,4,2304]{3,0,2,1:T(4,128)(2,1)S(1)} %collective-permute-done.10), kind=kOutput, calls=%fused_computation.10 | convolution fusion | flops 341508096 | bytes 2850816 | tf_op jit(solution)/shard_map/rd,edc->rec/dot_general | solution.py:71
  145.1 0.2 constant_dynamic-slice_fusion
  145.4 7.4 %fusion.10 = f32[6,3,4,8,4,128]{5,4,1,0,3,2:T(4,128)S(1)} fusion(bf16[4,8,6,4,3200,1]{4,3,5,2,1,0:T(4,128)(2,1)} %bitcast.136, bf16[3,5376,128]{2,1,0:T(8,128)(2,1)} %bitcast.125, s32[]{:T(128)S(6)} %select_n.190, f32[4,8,6,4,3,128]{5,3,4,2,1,0:T(4,128)S(1)} %constant_dynamic-slice_fusion), kind=kOutput, calls=%fused_computation.17 | convolution fusion | flops 1888026624 | bytes 9732100 | tf_op jit(solution)/shard_map/rd,edc->rec/dot_general | solution.py:71
  152.8 0.3 copy.149
  153.1 0.6 gather_fusion.3
  153.8 1.2 fusion.18
  (42 shorter events, 1.3 us)
Async XLA Ops:
  10.0 12.9 %copy-start.2 = (s32[16,6]{0,1:T(8,128)S(1)}, s32[16,6]{0,1:T(8,128)}, u32[]{:S(2)}) copy-start(s32[16,6]{0,1:T(8,128)} %param.11) | copy-start | bytes 1156
  10.0 13.1 %copy-start.3 = (s32[1,1,18,2]{2,3,1,0:T(2,128)S(1)}, s32[1,1,18,2]{2,3,1,0:T(2,128)}, u32[]{:S(2)}) copy-start(s32[1,1,18,2]{2,3,1,0:T(2,128)} %param.12) | copy-start | bytes 436
  12.4 29.6 %all-to-all-start = ((bf16[16,4,5504]{2,1,0:T(4,128)(2,1)}), bf16[16,4,5504]{2,1,0:T(4,128)(2,1)S(1)}, u32[]{:S(2)}, u32[]{:S(2)}) async-start(bf16[16,4,5504]{2,1,0:T(4,128)(2,1)} %broadcast_select_fusion), calls=%async_computation | async-start | bytes 1409024 | tf_op jit(solution)/shard_map/all_to_all | solution.py:51
  22.8 122.5 %all-gather.3.cloned.1.call-start = ((), (), s32[]{:S(2)}) async-start(), calls=%async_computation.1 | async-start | bytes 5068800 | tf_op jit(solution)/shard_map/all_gather | solution.py:73
  43.8 7.0 %collective-permute-start.3 = (bf16[6,4,2304]{2,1,0:T(4,128)(2,1)S(1)}, bf16[6,4,2304]{2,1,0:T(4,128)(2,1)S(1)}, u32[]{:S(2)}, u32[]{:S(2)}) collective-permute-start(bf16[6,4,2304]{2,1,0:T(4,128)(2,1)S(1)} %get-tuple-element.19), channel_id=1, source_target_pairs={{0,1},{1,2},{2,3},{3,4},{4,5},{5,6},{6,7},{7,0},{8,9},{9,10},{10,1... | collective-permute-start | bytes 331784 | tf_op jit(solution)/shard_map/ppermute | solution.py:26
  48.5 8.0 %collective-permute-start = (bf16[6,4,2304]{2,1,0:T(4,128)(2,1)S(1)}, bf16[6,4,2304]{2,1,0:T(4,128)(2,1)S(1)}, u32[]{:S(2)}, u32[]{:S(2)}) collective-permute-start(bf16[6,4,2304]{2,1,0:T(4,128)(2,1)S(1)} %get-tuple-element.19), channel_id=1, source_target_pairs={{0,7},{1,0},{2,1},{3,2},{4,3},{5,4},{6,5},{7,6},{8,15},{9,8},{10,9... | collective-permute-start | bytes 331784 | tf_op jit(solution)/shard_map/ppermute | solution.py:27
  50.8 9.6 %collective-permute-start.4 = (bf16[6,4,2304]{2,1,0:T(4,128)(2,1)S(1)}, bf16[6,4,2304]{2,1,0:T(4,128)(2,1)S(1)}, u32[]{:S(2)}, u32[]{:S(2)}) collective-permute-start(bf16[6,4,2304]{2,1,0:T(4,128)(2,1)S(1)} %collective-permute-done.3), channel_id=1, source_target_pairs={{0,1},{1,2},{2,3},{3,4},{4,5},{5,6},{6,7},{7,0},{8,9},{9,10},{10,1... | collective-permute-start | bytes 331784 | tf_op jit(solution)/shard_map/ppermute | solution.py:26
  56.5 9.5 %collective-permute-start.1 = (bf16[6,4,2304]{2,1,0:T(4,128)(2,1)S(1)}, bf16[6,4,2304]{2,1,0:T(4,128)(2,1)S(1)}, u32[]{:S(2)}, u32[]{:S(2)}) collective-permute-start(bf16[6,4,2304]{2,1,0:T(4,128)(2,1)S(1)} %collective-permute-done), channel_id=1, source_target_pairs={{0,7},{1,0},{2,1},{3,2},{4,3},{5,4},{6,5},{7,6},{8,15},{9,8},{10,9... | collective-permute-start | bytes 331784 | tf_op jit(solution)/shard_map/ppermute | solution.py:27
  60.4 9.4 %collective-permute-start.5 = (bf16[6,4,2304]{2,1,0:T(4,128)(2,1)S(1)}, bf16[6,4,2304]{2,1,0:T(4,128)(2,1)S(1)}, u32[]{:S(2)}, u32[]{:S(2)}) collective-permute-start(bf16[6,4,2304]{2,1,0:T(4,128)(2,1)S(1)} %collective-permute-done.4), channel_id=1, source_target_pairs={{0,1},{1,2},{2,3},{3,4},{4,5},{5,6},{6,7},{7,0},{8,9},{9,10},{10,1... | collective-permute-start | bytes 331784 | tf_op jit(solution)/shard_map/ppermute | solution.py:26
  66.0 9.4 %collective-permute-start.2 = (bf16[6,4,2304]{2,1,0:T(4,128)(2,1)S(1)}, bf16[6,4,2304]{2,1,0:T(4,128)(2,1)S(1)}, u32[]{:S(2)}, u32[]{:S(2)}) collective-permute-start(bf16[6,4,2304]{2,1,0:T(4,128)(2,1)S(1)} %collective-permute-done.1), channel_id=1, source_target_pairs={{0,7},{1,0},{2,1},{3,2},{4,3},{5,4},{6,5},{7,6},{8,15},{9,8},{10,9... | collective-permute-start | bytes 331784 | tf_op jit(solution)/shard_map/ppermute | solution.py:27
  69.8 9.5 %collective-permute-start.6 = (bf16[3,4,2304]{2,1,0:T(4,128)(2,1)S(1)}, bf16[3,4,2304]{2,1,0:T(4,128)(2,1)S(1)}, u32[]{:S(2)}, u32[]{:S(2)}) collective-permute-start(bf16[3,4,2304]{2,1,0:T(4,128)(2,1)S(1)} %slice.84), channel_id=1, source_target_pairs={{0,1},{1,2},{2,3},{3,4},{4,5},{5,6},{6,7},{7,0},{8,9},{9,10},{10,1... | collective-permute-start | bytes 165896 | tf_op jit(solution)/shard_map/ppermute | solution.py:22
  75.5 7.4 %collective-permute-start.7 = (bf16[3,4,2304]{2,1,0:T(4,128)(2,1)S(1)}, bf16[3,4,2304]{2,1,0:T(4,128)(2,1)S(1)}, u32[]{:S(2)}, u32[]{:S(2)}) collective-permute-start(bf16[3,4,2304]{2,1,0:T(4,128)(2,1)S(1)} %slice.85), channel_id=1, source_target_pairs={{0,7},{1,0},{2,1},{3,2},{4,3},{5,4},{6,5},{7,6},{8,15},{9,8},{10,9... | collective-permute-start | bytes 165896 | tf_op jit(solution)/shard_map/ppermute | solution.py:23
  85.9 33.5 %collective-permute-start.9 = (bf16[8,6,4,2304]{3,0,2,1:T(8,128)(2,1)S(1)}, bf16[8,6,4,2304]{3,0,2,1:T(8,128)(2,1)}, u32[]{:S(2)}, u32[]{:S(2)}) collective-permute-start(bf16[8,6,4,2304]{3,0,2,1:T(8,128)(2,1)S(1)} %stack.41), channel_id=1, source_target_pairs={{0,8},{8,16},{16,24},{24,0},{1,9},{9,17},{17,25},{25,1},{2,10},{10... | collective-permute-start | bytes 2654216 | tf_op jit(solution)/shard_map/ppermute | solution.py:26
  89.1 35.9 %collective-permute-start.8 = (bf16[8,6,4,2304]{3,0,2,1:T(8,128)(2,1)S(1)}, bf16[8,6,4,2304]{3,0,2,1:T(8,128)(2,1)}, u32[]{:S(2)}, u32[]{:S(2)}) collective-permute-start(bf16[8,6,4,2304]{3,0,2,1:T(8,128)(2,1)S(1)} %stack.41), channel_id=1, source_target_pairs={{0,24},{8,0},{16,8},{24,16},{1,25},{9,1},{17,9},{25,17},{2,26},{10... | collective-permute-start | bytes 2654216 | tf_op jit(solution)/shard_map/ppermute | solution.py:27
  120.6 16.4 %collective-permute-start.10 = (bf16[4,6,4,2304]{3,0,2,1:T(4,128)(2,1)S(1)}, bf16[4,6,4,2304]{3,0,2,1:T(4,128)(2,1)S(1)}, u32[]{:S(2)}, u32[]{:S(2)}) collective-permute-start(bf16[4,6,4,2304]{3,0,2,1:T(4,128)(2,1)S(1)} %slice.88), channel_id=1, source_target_pairs={{0,8},{8,16},{16,24},{24,0},{1,9},{9,17},{17,25},{25,1},{2,10},{10... | collective-permute-start | bytes 1327112 | tf_op jit(solution)/shard_map/ppermute | solution.py:22
  126.6 13.9 %collective-permute-start.11 = (bf16[4,6,4,2304]{3,0,2,1:T(4,128)(2,1)S(1)}, bf16[4,6,4,2304]{3,0,2,1:T(4,128)(2,1)S(1)}, u32[]{:S(2)}, u32[]{:S(2)}) collective-permute-start(bf16[4,6,4,2304]{3,0,2,1:T(4,128)(2,1)S(1)} %slice.89), channel_id=1, source_target_pairs={{0,24},{8,0},{16,8},{24,16},{1,25},{9,1},{17,9},{25,17},{2,26},{10... | collective-permute-start | bytes 1327112 | tf_op jit(solution)/shard_map/ppermute | solution.py:23
  140.5 0.8 copy-start.1
  142.6 1.8 %copy-start = (f32[8,8,6,4,3,128]{5,3,4,2,1,0:T(4,128)S(1)}, f32[8,8,6,4,3,128]{5,3,4,2,1,0:T(4,128)}, u32[]{:S(2)}) copy-start(f32[8,8,6,4,3,128]{5,3,4,2,1,0:T(4,128)} %bitcast_dynamic-update-slice_fusion.4) | copy-start | bytes 7077892
Sparse Core Ops, SparseCore 0:
  43.8 99.2 all-gather.2

commit v6 on v5

--- a/solution.py
+++ b/solution.py
@@ -57,7 +57,7 @@
     slot_rows = jnp.where(my_valid[:, None, None], slot_rows, jnp.zeros((), slot_rows.dtype))
     slots, rows_dev, _ = slot_rows.shape
 
-    split = (ext_width * 3 // 5) // LANES * LANES
+    split = (ext_width * 5 // 9 + LANES - 1) // LANES * LANES
     part_a = slot_rows[..., :split]
     part_b = slot_rows[..., split:]
 

time: 163 us -> 170 us (1.043)
  the two profiles are of different devices: /device:TPU:26 before, /device:TPU:6 now
where the time goes in v6:
time: 170 us; the launch traced here: 168 us
  waiting for transfers between devices  65.5 us (39%)
  starting transfers between devices  51.1 us (30%)
  local copies, waits for them, and re-layouts  20.4 us (12%)
  between operations  14.5 us (9%)
  matrix products  10.9 us (6%)
  other arithmetic  5.8 us (3%)
    ppermute x4, waiting for transfers between devices, ring_parts(): left = lax.ppermute(left, axis, up)  35.5 us
    all_to_all x1, waiting for transfers between devices, local(): recv = lax.all_to_all(send, GRP, 0, 0, tiled=True)  18.8 us
    ppermute x4, starting transfers between devices, ring_parts(): right = lax.ppermute(right, axis, down)  16.5 us
    dot_general x5, matrix products, mm(): jnp.einsum('rd,edc->rec', flat, enc, preferred_element_type=jnp.float32)  10.9 us
    ppermute x4, starting transfers between devices, ring_parts(): left = lax.ppermute(left, axis, up)  10.5 us
    all_to_all x1, starting transfers between devices, local(): recv = lax.all_to_all(send, GRP, 0, 0, tiled=True)  10.4 us
    another operation x9, local copies, waits for them, and re-layouts, local(): b_y = jnp.stack(ring_parts(part_b, 'y', n_y), axis=0)  9.95 us
    ppermute x2, starting transfers between devices, ring_parts(): got_right = lax.ppermute(right[half:], axis, down)  7.42 us
  transfers between devices with their start and end apart: 14, of which 10 were waited for; matrix products, arithmetic and copies ran while one was open for 12% of the time, Pallas kernels for 0%

profile of v6, /device:TPU:6, one launch (start us, length us, event | category | flops | bytes accessed | tf_op | source)
XLA Modules:
  0.0 168.2 jit_solution(13114118014369070061)
XLA Ops:
  6.5 0.7 fusion.31
  7.3 0.8 and_bitcast_fusion
  8.0 0.8 copy.157
  8.8 1.1 fusion.25
  10.0 1.2 gather_fusion
  11.2 1.2 broadcast_select_fusion
  12.4 10.4 %all-to-all-start = ((bf16[16,4,5504]{2,1,0:T(4,128)(2,1)}), bf16[16,4,5504]{2,1,0:T(4,128)(2,1)S(1)}, u32[]{:S(2)}, u32[]{:S(2)}) async-start(bf16[16,4,5504]{2,1,0:T(4,128)(2,1)} %broadcast_select_fusion), calls=%async_computation | async-start | bytes 1409024 | tf_op jit(solution)/shard_map/all_to_all | solution.py:51
  22.9 0.2 dynamic-slice_reduce_fusion
  23.1 18.8 %all-to-all-done = bf16[16,4,5504]{2,1,0:T(4,128)(2,1)S(1)} async-done(((bf16[16,4,5504]{2,1,0:T(4,128)(2,1)}), bf16[16,4,5504]{2,1,0:T(4,128)(2,1)S(1)}, u32[]{:S(2)}, u32[]{:S(2)}) %all-to-all-start) | async-done | bytes 704544 | tf_op jit(solution)/shard_map/all_to_all | solution.py:51
  42.0 0.8 gather_fusion.1
  42.8 0.2 select_select_fusion
  43.0 0.7 slice.93
  43.8 3.5 %collective-permute-start.3 = (bf16[6,4,2432]{2,1,0:T(4,128)(2,1)S(1)}, bf16[6,4,2432]{2,1,0:T(4,128)(2,1)S(1)}, u32[]{:S(2)}, u32[]{:S(2)}) collective-permute-start(bf16[6,4,2432]{2,1,0:T(4,128)(2,1)S(1)} %get-tuple-element.19), channel_id=1, source_target_pairs={{0,1},{1,2},{2,3},{3,4},{4,5},{5,6},{6,7},{7,0},{8,9},{9,10},{10,1... | collective-permute-start | bytes 350216 | tf_op jit(solution)/shard_map/ppermute | solution.py:26
  47.3 3.8 %collective-permute-start = (bf16[6,4,2432]{2,1,0:T(4,128)(2,1)S(1)}, bf16[6,4,2432]{2,1,0:T(4,128)(2,1)S(1)}, u32[]{:S(2)}, u32[]{:S(2)}) collective-permute-start(bf16[6,4,2432]{2,1,0:T(4,128)(2,1)S(1)} %get-tuple-element.19), channel_id=1, source_target_pairs={{0,7},{1,0},{2,1},{3,2},{4,3},{5,4},{6,5},{7,6},{8,15},{9,8},{10,9... | collective-permute-start | bytes 350216 | tf_op jit(solution)/shard_map/ppermute | solution.py:27
  51.1 0.8 collective-permute-done.3
  51.9 2.0 %collective-permute-start.4 = (bf16[6,4,2432]{2,1,0:T(4,128)(2,1)S(1)}, bf16[6,4,2432]{2,1,0:T(4,128)(2,1)S(1)}, u32[]{:S(2)}, u32[]{:S(2)}) collective-permute-start(bf16[6,4,2432]{2,1,0:T(4,128)(2,1)S(1)} %collective-permute-done.3), channel_id=1, source_target_pairs={{0,1},{1,2},{2,3},{3,4},{4,5},{5,6},{6,7},{7,0},{8,9},{9,10},{10,1... | collective-permute-start | bytes 350216 | tf_op jit(solution)/shard_map/ppermute | solution.py:26
  54.0 0.3 collective-permute-done
  54.2 4.8 %collective-permute-start.1 = (bf16[6,4,2432]{2,1,0:T(4,128)(2,1)S(1)}, bf16[6,4,2432]{2,1,0:T(4,128)(2,1)S(1)}, u32[]{:S(2)}, u32[]{:S(2)}) collective-permute-start(bf16[6,4,2432]{2,1,0:T(4,128)(2,1)S(1)} %collective-permute-done), channel_id=1, source_target_pairs={{0,7},{1,0},{2,1},{3,2},{4,3},{5,4},{6,5},{7,6},{8,15},{9,8},{10,9... | collective-permute-start | bytes 350216 | tf_op jit(solution)/shard_map/ppermute | solution.py:27
  59.0 1.7 collective-permute-done.4
  60.7 1.9 %collective-permute-start.5 = (bf16[6,4,2432]{2,1,0:T(4,128)(2,1)S(1)}, bf16[6,4,2432]{2,1,0:T(4,128)(2,1)S(1)}, u32[]{:S(2)}, u32[]{:S(2)}) collective-permute-start(bf16[6,4,2432]{2,1,0:T(4,128)(2,1)S(1)} %collective-permute-done.4), channel_id=1, source_target_pairs={{0,1},{1,2},{2,3},{3,4},{4,5},{5,6},{6,7},{7,0},{8,9},{9,10},{10,1... | collective-permute-start | bytes 350216 | tf_op jit(solution)/shard_map/ppermute | solution.py:26
  62.6 0.3 collective-permute-done.1
  62.9 5.1 %collective-permute-start.2 = (bf16[6,4,2432]{2,1,0:T(4,128)(2,1)S(1)}, bf16[6,4,2432]{2,1,0:T(4,128)(2,1)S(1)}, u32[]{:S(2)}, u32[]{:S(2)}) collective-permute-start(bf16[6,4,2432]{2,1,0:T(4,128)(2,1)S(1)} %collective-permute-done.1), channel_id=1, source_target_pairs={{0,7},{1,0},{2,1},{3,2},{4,3},{5,4},{6,5},{7,6},{8,15},{9,8},{10,9... | collective-permute-start | bytes 350216 | tf_op jit(solution)/shard_map/ppermute | solution.py:27
  68.0 1.5 collective-permute-done.5
  69.5 1.9 %collective-permute-start.6 = (bf16[3,4,2432]{2,1,0:T(4,128)(2,1)S(1)}, bf16[3,4,2432]{2,1,0:T(4,128)(2,1)S(1)}, u32[]{:S(2)}, u32[]{:S(2)}) collective-permute-start(bf16[3,4,2432]{2,1,0:T(4,128)(2,1)S(1)} %slice.84), channel_id=1, source_target_pairs={{0,1},{1,2},{2,3},{3,4},{4,5},{5,6},{6,7},{7,0},{8,9},{9,10},{10,1... | collective-permute-start | bytes 175112 | tf_op jit(solution)/shard_map/ppermute | solution.py:22
  71.5 5.3 %collective-permute-start.7 = (bf16[3,4,2432]{2,1,0:T(4,128)(2,1)S(1)}, bf16[3,4,2432]{2,1,0:T(4,128)(2,1)S(1)}, u32[]{:S(2)}, u32[]{:S(2)}) collective-permute-start(bf16[3,4,2432]{2,1,0:T(4,128)(2,1)S(1)} %slice.85), channel_id=1, source_target_pairs={{0,7},{1,0},{2,1},{3,2},{4,3},{5,4},{6,5},{7,6},{8,15},{9,8},{10,9... | collective-permute-start | bytes 175112 | tf_op jit(solution)/shard_map/ppermute | solution.py:23
  76.9 1.6 slice.95
  79.1 0.2 copy.136
  79.3 0.2 copy.137
  79.5 0.2 copy.143
  79.7 0.9 copy.138
  80.6 0.9 copy.142
  81.4 0.9 copy.139
  82.3 0.9 copy.141
  83.3 0.9 copy.140
  84.2 5.0 %stack.41 = bf16[8,6,4,2432]{3,0,2,1:T(8,128)(2,1)S(1)} concatenate(bf16[1,6,4,2432]{3,0,2,1:T(2,128)(2,1)S(1)} %copy.136, bf16[1,6,4,2432]{3,0,2,1:T(2,128)(2,1)S(1)} %copy.137, bf16[1,6,4,2432]{3,0,2,1:T(2,128)(2,1)} %copy.138, bf16[1,6,4,2432]{3,0,2,1:T(2,128)(2,1)} %copy.139, bf16[1,6,4,2432]{3,0,2,1:T(2,128)(2,1)} %copy.140, bf16[1,6,4,2432]{3,0,2,1:T(2,128)(2,1)} %copy.141, ...), dimensions={0} | concatenate | bytes 1867776 | tf_op jit(solution)/shard_map/stack | solution.py:76
  89.2 3.1 %collective-permute-start.9 = (bf16[8,6,4,2432]{3,0,2,1:T(8,128)(2,1)S(1)}, bf16[8,6,4,2432]{3,0,2,1:T(8,128)(2,1)S(1)}, u32[]{:S(2)}, u32[]{:S(2)}) collective-permute-start(bf16[8,6,4,2432]{3,0,2,1:T(8,128)(2,1)S(1)} %stack.41), channel_id=1, source_target_pairs={{0,8},{8,16},{16,24},{24,0},{1,9},{9,17},{17,25},{25,1},{2,10},{10... | collective-permute-start | bytes 2801672 | tf_op jit(solution)/shard_map/ppermute | solution.py:26
  92.3 2.7 %collective-permute-start.8 = (bf16[8,6,4,2432]{3,0,2,1:T(8,128)(2,1)S(1)}, bf16[8,6,4,2432]{3,0,2,1:T(8,128)(2,1)S(1)}, u32[]{:S(2)}, u32[]{:S(2)}) collective-permute-start(bf16[8,6,4,2432]{3,0,2,1:T(8,128)(2,1)S(1)} %stack.41), channel_id=1, source_target_pairs={{0,24},{8,0},{16,8},{24,16},{1,25},{9,1},{17,9},{25,17},{2,26},{10... | collective-permute-start | bytes 2801672 | tf_op jit(solution)/shard_map/ppermute | solution.py:27
  95.1 0.1 slice_reduce_fusion.2
  95.2 0.6 fusion.7
  95.8 0.8 bitcast_dynamic-update-slice_fusion.6
  96.6 31.5 %collective-permute-done.9 = bf16[8,6,4,2432]{3,0,2,1:T(8,128)(2,1)S(1)} collective-permute-done((bf16[8,6,4,2432]{3,0,2,1:T(8,128)(2,1)S(1)}, bf16[8,6,4,2432]{3,0,2,1:T(8,128)(2,1)S(1)}, u32[]{:S(2)}, u32[]{:S(2)}) %collective-permute-start.9) | collective-permute-done | bytes 933920 | tf_op jit(solution)/shard_map/ppermute | solution.py:26
  128.1 0.1 slice.88
  128.2 4.3 %collective-permute-start.10 = (bf16[4,6,4,2432]{3,0,2,1:T(4,128)(2,1)S(1)}, bf16[4,6,4,2432]{3,0,2,1:T(4,128)(2,1)S(1)}, u32[]{:S(2)}, u32[]{:S(2)}) collective-permute-start(bf16[4,6,4,2432]{3,0,2,1:T(4,128)(2,1)S(1)} %slice.88), channel_id=1, source_target_pairs={{0,8},{8,16},{16,24},{24,0},{1,9},{9,17},{17,25},{25,1},{2,10},{10... | collective-permute-start | bytes 1400840 | tf_op jit(solution)/shard_map/ppermute | solution.py:22
  132.5 3.4 %collective-permute-done.8 = bf16[8,6,4,2432]{3,0,2,1:T(8,128)(2,1)S(1)} collective-permute-done((bf16[8,6,4,2432]{3,0,2,1:T(8,128)(2,1)S(1)}, bf16[8,6,4,2432]{3,0,2,1:T(8,128)(2,1)S(1)}, u32[]{:S(2)}, u32[]{:S(2)}) %collective-permute-start.8) | collective-permute-done | bytes 933920 | tf_op jit(solution)/shard_map/ppermute | solution.py:27
  135.9 0.2 slice.89
  136.2 2.1 %collective-permute-start.11 = (bf16[4,6,4,2432]{3,0,2,1:T(4,128)(2,1)S(1)}, bf16[4,6,4,2432]{3,0,2,1:T(4,128)(2,1)S(1)}, u32[]{:S(2)}, u32[]{:S(2)}) collective-permute-start(bf16[4,6,4,2432]{3,0,2,1:T(4,128)(2,1)S(1)} %slice.89), channel_id=1, source_target_pairs={{0,24},{8,0},{16,8},{24,16},{1,25},{9,1},{17,9},{25,17},{2,26},{10... | collective-permute-start | bytes 1400840 | tf_op jit(solution)/shard_map/ppermute | solution.py:23
  138.3 0.1 slice_reduce_fusion.1
  138.4 0.1 slice_reduce_fusion
  138.5 0.6 fusion.5
  139.1 0.8 bitcast_dynamic-update-slice_fusion.4
  139.9 0.6 fusion.1
  140.6 1.3 collective-permute-done.10
  141.8 6.0 %collective-permute-done.11 = bf16[4,6,4,2432]{3,0,2,1:T(4,128)(2,1)S(1)} collective-permute-done((bf16[4,6,4,2432]{3,0,2,1:T(4,128)(2,1)S(1)}, bf16[4,6,4,2432]{3,0,2,1:T(4,128)(2,1)S(1)}, u32[]{:S(2)}, u32[]{:S(2)}) %collective-permute-start.11) | collective-permute-done | bytes 466976 | tf_op jit(solution)/shard_map/ppermute | solution.py:23
  147.8 0.1 fusion.27
  148.1 0.1 fusion.28
  148.2 0.2 copy.144
  148.5 0.1 reshape.246
  148.6 0.6 gather_fusion.2
  149.2 1.8 %fusion.3 = f32[8,6,4,3,128]{4,0,3,2,1:T(8,128)S(1)} fusion(bf16[3,2304,128]{2,1,0:T(8,128)(2,1)S(1)} %slice.95, bf16[4,6,4,2432]{3,0,2,1:T(4,128)(2,1)S(1)} %collective-permute-done.11, bf16[4,6,4,2432]{3,0,2,1:T(4,128)(2,1)} %copy-done.1), kind=kOutput, calls=%fused_computation.10 | convolution fusion | flops 360480768 | bytes 2998272 | tf_op jit(solution)/shard_map/rd,edc->rec/dot_general | solution.py:71
  151.7 0.2 constant_dynamic-slice_fusion
  152.0 7.2 %fusion.10 = f32[6,3,4,8,4,128]{5,4,1,0,3,2:T(4,128)S(1)} fusion(bf16[4,8,6,4,3072,1]{4,3,5,2,1,0:T(4,128)(2,1)} %bitcast.136, bf16[3,5376,128]{2,1,0:T(8,128)(2,1)} %bitcast.125, s32[]{:T(128)S(6)} %select_n.190, f32[4,8,6,4,3,128]{5,3,4,2,1,0:T(4,128)S(1)} %constant_dynamic-slice_fusion), kind=kOutput, calls=%fused_computation.17 | convolution fusion | flops 1812529152 | bytes 9437188 | tf_op jit(solution)/shard_map/rd,edc->rec/dot_general | solution.py:71
  159.2 0.3 copy.149
  159.5 0.6 gather_fusion.3
  160.1 1.2 fusion.18
  (42 shorter events, 1.2 us)
Async XLA Ops:
  10.0 12.9 %copy-start.2 = (s32[16,6]{0,1:T(8,128)S(1)}, s32[16,6]{0,1:T(8,128)}, u32[]{:S(2)}) copy-start(s32[16,6]{0,1:T(8,128)} %param.11) | copy-start | bytes 1156
  10.0 13.1 %copy-start.3 = (s32[1,1,18,2]{2,3,1,0:T(2,128)S(1)}, s32[1,1,18,2]{2,3,1,0:T(2,128)}, u32[]{:S(2)}) copy-start(s32[1,1,18,2]{2,3,1,0:T(2,128)} %param.12) | copy-start | bytes 436
  12.4 29.6 %all-to-all-start = ((bf16[16,4,5504]{2,1,0:T(4,128)(2,1)}), bf16[16,4,5504]{2,1,0:T(4,128)(2,1)S(1)}, u32[]{:S(2)}, u32[]{:S(2)}) async-start(bf16[16,4,5504]{2,1,0:T(4,128)(2,1)} %broadcast_select_fusion), calls=%async_computation | async-start | bytes 1409024 | tf_op jit(solution)/shard_map/all_to_all | solution.py:51
  22.8 129.1 %all-gather.3.cloned.1.call-start = ((), (), s32[]{:S(2)}) async-start(), calls=%async_computation.1 | async-start | bytes 4866048 | tf_op jit(solution)/shard_map/all_gather | solution.py:73
  43.8 8.2 %collective-permute-start.3 = (bf16[6,4,2432]{2,1,0:T(4,128)(2,1)S(1)}, bf16[6,4,2432]{2,1,0:T(4,128)(2,1)S(1)}, u32[]{:S(2)}, u32[]{:S(2)}) collective-permute-start(bf16[6,4,2432]{2,1,0:T(4,128)(2,1)S(1)} %get-tuple-element.19), channel_id=1, source_target_pairs={{0,1},{1,2},{2,3},{3,4},{4,5},{5,6},{6,7},{7,0},{8,9},{9,10},{10,1... | collective-permute-start | bytes 350216 | tf_op jit(solution)/shard_map/ppermute | solution.py:26
  47.3 6.9 %collective-permute-start = (bf16[6,4,2432]{2,1,0:T(4,128)(2,1)S(1)}, bf16[6,4,2432]{2,1,0:T(4,128)(2,1)S(1)}, u32[]{:S(2)}, u32[]{:S(2)}) collective-permute-start(bf16[6,4,2432]{2,1,0:T(4,128)(2,1)S(1)} %get-tuple-element.19), channel_id=1, source_target_pairs={{0,7},{1,0},{2,1},{3,2},{4,3},{5,4},{6,5},{7,6},{8,15},{9,8},{10,9... | collective-permute-start | bytes 350216 | tf_op jit(solution)/shard_map/ppermute | solution.py:27
  51.9 8.7 %collective-permute-start.4 = (bf16[6,4,2432]{2,1,0:T(4,128)(2,1)S(1)}, bf16[6,4,2432]{2,1,0:T(4,128)(2,1)S(1)}, u32[]{:S(2)}, u32[]{:S(2)}) collective-permute-start(bf16[6,4,2432]{2,1,0:T(4,128)(2,1)S(1)} %collective-permute-done.3), channel_id=1, source_target_pairs={{0,1},{1,2},{2,3},{3,4},{4,5},{5,6},{6,7},{7,0},{8,9},{9,10},{10,1... | collective-permute-start | bytes 350216 | tf_op jit(solution)/shard_map/ppermute | solution.py:26
  54.2 8.7 %collective-permute-start.1 = (bf16[6,4,2432]{2,1,0:T(4,128)(2,1)S(1)}, bf16[6,4,2432]{2,1,0:T(4,128)(2,1)S(1)}, u32[]{:S(2)}, u32[]{:S(2)}) collective-permute-start(bf16[6,4,2432]{2,1,0:T(4,128)(2,1)S(1)} %collective-permute-done), channel_id=1, source_target_pairs={{0,7},{1,0},{2,1},{3,2},{4,3},{5,4},{6,5},{7,6},{8,15},{9,8},{10,9... | collective-permute-start | bytes 350216 | tf_op jit(solution)/shard_map/ppermute | solution.py:27
  60.7 8.8 %collective-permute-start.5 = (bf16[6,4,2432]{2,1,0:T(4,128)(2,1)S(1)}, bf16[6,4,2432]{2,1,0:T(4,128)(2,1)S(1)}, u32[]{:S(2)}, u32[]{:S(2)}) collective-permute-start(bf16[6,4,2432]{2,1,0:T(4,128)(2,1)S(1)} %collective-permute-done.4), channel_id=1, source_target_pairs={{0,1},{1,2},{2,3},{3,4},{4,5},{5,6},{6,7},{7,0},{8,9},{9,10},{10,1... | collective-permute-start | bytes 350216 | tf_op jit(solution)/shard_map/ppermute | solution.py:26
  62.9 8.6 %collective-permute-start.2 = (bf16[6,4,2432]{2,1,0:T(4,128)(2,1)S(1)}, bf16[6,4,2432]{2,1,0:T(4,128)(2,1)S(1)}, u32[]{:S(2)}, u32[]{:S(2)}) collective-permute-start(bf16[6,4,2432]{2,1,0:T(4,128)(2,1)S(1)} %collective-permute-done.1), channel_id=1, source_target_pairs={{0,7},{1,0},{2,1},{3,2},{4,3},{5,4},{6,5},{7,6},{8,15},{9,8},{10,9... | collective-permute-start | bytes 350216 | tf_op jit(solution)/shard_map/ppermute | solution.py:27
  69.5 13.7 %collective-permute-start.6 = (bf16[3,4,2432]{2,1,0:T(4,128)(2,1)S(1)}, bf16[3,4,2432]{2,1,0:T(4,128)(2,1)S(1)}, u32[]{:S(2)}, u32[]{:S(2)}) collective-permute-start(bf16[3,4,2432]{2,1,0:T(4,128)(2,1)S(1)} %slice.84), channel_id=1, source_target_pairs={{0,1},{1,2},{2,3},{3,4},{4,5},{5,6},{6,7},{7,0},{8,9},{9,10},{10,1... | collective-permute-start | bytes 175112 | tf_op jit(solution)/shard_map/ppermute | solution.py:22
  71.5 11.7 %collective-permute-start.7 = (bf16[3,4,2432]{2,1,0:T(4,128)(2,1)S(1)}, bf16[3,4,2432]{2,1,0:T(4,128)(2,1)S(1)}, u32[]{:S(2)}, u32[]{:S(2)}) collective-permute-start(bf16[3,4,2432]{2,1,0:T(4,128)(2,1)S(1)} %slice.85), channel_id=1, source_target_pairs={{0,7},{1,0},{2,1},{3,2},{4,3},{5,4},{6,5},{7,6},{8,15},{9,8},{10,9... | collective-permute-start | bytes 175112 | tf_op jit(solution)/shard_map/ppermute | solution.py:23
  89.2 38.9 %collective-permute-start.9 = (bf16[8,6,4,2432]{3,0,2,1:T(8,128)(2,1)S(1)}, bf16[8,6,4,2432]{3,0,2,1:T(8,128)(2,1)S(1)}, u32[]{:S(2)}, u32[]{:S(2)}) collective-permute-start(bf16[8,6,4,2432]{3,0,2,1:T(8,128)(2,1)S(1)} %stack.41), channel_id=1, source_target_pairs={{0,8},{8,16},{16,24},{24,0},{1,9},{9,17},{17,25},{25,1},{2,10},{10... | collective-permute-start | bytes 2801672 | tf_op jit(solution)/shard_map/ppermute | solution.py:26
  92.3 43.6 %collective-permute-start.8 = (bf16[8,6,4,2432]{3,0,2,1:T(8,128)(2,1)S(1)}, bf16[8,6,4,2432]{3,0,2,1:T(8,128)(2,1)S(1)}, u32[]{:S(2)}, u32[]{:S(2)}) collective-permute-start(bf16[8,6,4,2432]{3,0,2,1:T(8,128)(2,1)S(1)} %stack.41), channel_id=1, source_target_pairs={{0,24},{8,0},{16,8},{24,16},{1,25},{9,1},{17,9},{25,17},{2,26},{10... | collective-permute-start | bytes 2801672 | tf_op jit(solution)/shard_map/ppermute | solution.py:27
  128.2 13.6 %collective-permute-start.10 = (bf16[4,6,4,2432]{3,0,2,1:T(4,128)(2,1)S(1)}, bf16[4,6,4,2432]{3,0,2,1:T(4,128)(2,1)S(1)}, u32[]{:S(2)}, u32[]{:S(2)}) collective-permute-start(bf16[4,6,4,2432]{3,0,2,1:T(4,128)(2,1)S(1)} %slice.88), channel_id=1, source_target_pairs={{0,8},{8,16},{16,24},{24,0},{1,9},{9,17},{17,25},{25,1},{2,10},{10... | collective-permute-start | bytes 1400840 | tf_op jit(solution)/shard_map/ppermute | solution.py:22
  136.2 11.7 %collective-permute-start.11 = (bf16[4,6,4,2432]{3,0,2,1:T(4,128)(2,1)S(1)}, bf16[4,6,4,2432]{3,0,2,1:T(4,128)(2,1)S(1)}, u32[]{:S(2)}, u32[]{:S(2)}) collective-permute-start(bf16[4,6,4,2432]{3,0,2,1:T(4,128)(2,1)S(1)} %slice.89), channel_id=1, source_target_pairs={{0,24},{8,0},{16,8},{24,16},{1,25},{9,1},{17,9},{25,17},{2,26},{10... | collective-permute-start | bytes 1400840 | tf_op jit(solution)/shard_map/ppermute | solution.py:23
  141.8 6.0 %copy-start.1 = (bf16[4,6,4,2432]{3,0,2,1:T(4,128)(2,1)}, bf16[4,6,4,2432]{3,0,2,1:T(4,128)(2,1)S(1)}, u32[]{:S(2)}) copy-start(bf16[4,6,4,2432]{3,0,2,1:T(4,128)(2,1)S(1)} %collective-permute-done.10) | copy-start | bytes 1400836
  149.2 1.9 %copy-start = (f32[8,8,6,4,3,128]{5,3,4,2,1,0:T(4,128)S(1)}, f32[8,8,6,4,3,128]{5,3,4,2,1,0:T(4,128)}, u32[]{:S(2)}) copy-start(f32[8,8,6,4,3,128]{5,3,4,2,1,0:T(4,128)} %bitcast_dynamic-update-slice_fusion.4) | copy-start | bytes 7077892
Sparse Core Ops, SparseCore 0:
  43.8 98.1 all-gather.2

commit v7 on v5

--- a/solution.py
+++ b/solution.py
@@ -70,7 +70,8 @@
         flat = block.reshape(-1, block.shape[-1])
         return jnp.einsum("rd,edc->rec", flat, enc, preferred_element_type=jnp.float32)
 
-    a_all = lax.all_gather(part_a, SHARD, axis=0, tiled=False)
+    flat_a = part_a.reshape(slots * rows_dev, split)
+    a_all = lax.all_gather(flat_a, SHARD, axis=0, tiled=False)
     prod_a = mm(a_all, enc_a).reshape(n_x, n_y, slots, rows_dev, enc_count, tile_cols)
 
     b_y = jnp.stack(ring_parts(part_b, "y", n_y), axis=0)

time: 163 us -> 166 us (1.018)
  waiting for transfers between devices: 57 us -> 60.9 us
  matrix products: 13.5 us -> 10.6 us
  local copies, waits for them, and re-layouts: 19.4 us -> 22.2 us
    all_gather x0 -> x1, local copies, waits for them, and re-layouts: none -> 3.08 us  [local(): a_all = lax.all_gather(flat_a, SHARD, axis=0, tiled=False)]
    dot_general x5, matrix products: 13.5 us -> 10.6 us  [mm(): jnp.einsum('rd,edc->rec', flat, enc, preferred_element_type=jnp.float32)]
    ppermute x2, waiting for transfers between devices: 1.27 us -> 3.97 us  [ring_parts(): got_left = lax.ppermute(left[:half], axis, up)]
    unnamed x23 -> x21, local copies, waits for them, and re-layouts: 3.79 us -> 3.67 us
where the time goes in v7:
time: 166 us
  waiting for transfers between devices  60.9 us (37%)
  starting transfers between devices  51.6 us (31%)
  local copies, waits for them, and re-layouts  22.2 us (13%)
  between operations  14.5 us (9%)
  matrix products  10.6 us (6%)
  other arithmetic  5.8 us (3%)
    ppermute x4, waiting for transfers between devices, ring_parts(): left = lax.ppermute(left, axis, up)  28.2 us
    ppermute x4, starting transfers between devices, ring_parts(): left = lax.ppermute(left, axis, up)  19.1 us
    all_to_all x1, waiting for transfers between devices, local(): recv = lax.all_to_all(send, GRP, 0, 0, tiled=True)  18.8 us
    dot_general x5, matrix products, mm(): jnp.einsum('rd,edc->rec', flat, enc, preferred_element_type=jnp.float32)  10.6 us
    all_to_all x1, starting transfers between devices, local(): recv = lax.all_to_all(send, GRP, 0, 0, tiled=True)  10.4 us
    ppermute x2, starting transfers between devices, ring_parts(): got_left = lax.ppermute(left[:half], axis, up)  8.94 us
    ppermute x4, starting transfers between devices, ring_parts(): right = lax.ppermute(right, axis, down)  8.31 us
    ppermute x2, waiting for transfers between devices, ring_parts(): got_right = lax.ppermute(right[half:], axis, down)  7.61 us
  transfers between devices with their start and end apart: 14, of which 10 were waited for; matrix products, arithmetic and copies ran while one was open for 13% of the time, Pallas kernels for 0%

profile of v7, /device:TPU:26, one launch (start us, length us, event | category | flops | bytes accessed | tf_op | source)
XLA Modules:
  0.0 165.5 jit_solution(1171961099737586137)
XLA Ops:
  6.5 0.7 fusion.48
  7.3 0.8 and_bitcast_fusion
  8.0 0.8 copy.156
  8.8 1.1 fusion.42
  10.0 1.2 gather_fusion
  11.2 1.2 broadcast_select_fusion
  12.4 10.4 %all-to-all-start = ((bf16[16,4,5504]{2,1,0:T(4,128)(2,1)}), bf16[16,4,5504]{2,1,0:T(4,128)(2,1)S(1)}, u32[]{:S(2)}, u32[]{:S(2)}) async-start(bf16[16,4,5504]{2,1,0:T(4,128)(2,1)} %broadcast_select_fusion), calls=%async_computation | async-start | bytes 1409024 | tf_op jit(solution)/shard_map/all_to_all | solution.py:51
  22.9 0.2 dynamic-slice_reduce_fusion
  23.2 18.8 %all-to-all-done = bf16[16,4,5504]{2,1,0:T(4,128)(2,1)S(1)} async-done(((bf16[16,4,5504]{2,1,0:T(4,128)(2,1)}), bf16[16,4,5504]{2,1,0:T(4,128)(2,1)S(1)}, u32[]{:S(2)}, u32[]{:S(2)}) %all-to-all-start) | async-done | bytes 704544 | tf_op jit(solution)/shard_map/all_to_all | solution.py:51
  42.0 0.8 gather_fusion.1
  42.8 0.2 select_select_fusion
  43.0 0.7 all_gather_reshape.3
  43.8 4.7 %collective-permute-start.3 = (bf16[6,4,2304]{2,1,0:T(4,128)(2,1)S(1)}, bf16[6,4,2304]{2,1,0:T(4,128)(2,1)S(1)}, u32[]{:S(2)}, u32[]{:S(2)}) collective-permute-start(bf16[6,4,2304]{2,1,0:T(4,128)(2,1)S(1)} %get-tuple-element.19), channel_id=1, source_target_pairs={{0,1},{1,2},{2,3},{3,4},{4,5},{5,6},{6,7},{7,0},{8,9},{9,10},{10,1... | collective-permute-start | bytes 331784 | tf_op jit(solution)/shard_map/ppermute | solution.py:26
  48.5 1.9 %collective-permute-start = (bf16[6,4,2304]{2,1,0:T(4,128)(2,1)S(1)}, bf16[6,4,2304]{2,1,0:T(4,128)(2,1)S(1)}, u32[]{:S(2)}, u32[]{:S(2)}) collective-permute-start(bf16[6,4,2304]{2,1,0:T(4,128)(2,1)S(1)} %get-tuple-element.19), channel_id=1, source_target_pairs={{0,7},{1,0},{2,1},{3,2},{4,3},{5,4},{6,5},{7,6},{8,15},{9,8},{10,9... | collective-permute-start | bytes 331784 | tf_op jit(solution)/shard_map/ppermute | solution.py:27
  50.5 0.4 collective-permute-done.3
  50.8 5.5 %collective-permute-start.4 = (bf16[6,4,2304]{2,1,0:T(4,128)(2,1)S(1)}, bf16[6,4,2304]{2,1,0:T(4,128)(2,1)S(1)}, u32[]{:S(2)}, u32[]{:S(2)}) collective-permute-start(bf16[6,4,2304]{2,1,0:T(4,128)(2,1)S(1)} %collective-permute-done.3), channel_id=1, source_target_pairs={{0,1},{1,2},{2,3},{3,4},{4,5},{5,6},{6,7},{7,0},{8,9},{9,10},{10,1... | collective-permute-start | bytes 331784 | tf_op jit(solution)/shard_map/ppermute | solution.py:26
  56.4 0.2 collective-permute-done
  56.6 1.9 %collective-permute-start.1 = (bf16[6,4,2304]{2,1,0:T(4,128)(2,1)S(1)}, bf16[6,4,2304]{2,1,0:T(4,128)(2,1)S(1)}, u32[]{:S(2)}, u32[]{:S(2)}) collective-permute-start(bf16[6,4,2304]{2,1,0:T(4,128)(2,1)S(1)} %collective-permute-done), channel_id=1, source_target_pairs={{0,7},{1,0},{2,1},{3,2},{4,3},{5,4},{6,5},{7,6},{8,15},{9,8},{10,9... | collective-permute-start | bytes 331784 | tf_op jit(solution)/shard_map/ppermute | solution.py:27
  58.5 2.0 %collective-permute-done.4 = bf16[6,4,2304]{2,1,0:T(4,128)(2,1)S(1)} collective-permute-done((bf16[6,4,2304]{2,1,0:T(4,128)(2,1)S(1)}, bf16[6,4,2304]{2,1,0:T(4,128)(2,1)S(1)}, u32[]{:S(2)}, u32[]{:S(2)}) %collective-permute-start.4) | collective-permute-done | bytes 110624 | tf_op jit(solution)/shard_map/ppermute | solution.py:26
  60.5 5.6 %collective-permute-start.5 = (bf16[6,4,2304]{2,1,0:T(4,128)(2,1)S(1)}, bf16[6,4,2304]{2,1,0:T(4,128)(2,1)S(1)}, u32[]{:S(2)}, u32[]{:S(2)}) collective-permute-start(bf16[6,4,2304]{2,1,0:T(4,128)(2,1)S(1)} %collective-permute-done.4), channel_id=1, source_target_pairs={{0,1},{1,2},{2,3},{3,4},{4,5},{5,6},{6,7},{7,0},{8,9},{9,10},{10,1... | collective-permute-start | bytes 331784 | tf_op jit(solution)/shard_map/ppermute | solution.py:26
  66.1 1.9 %collective-permute-start.2 = (bf16[6,4,2304]{2,1,0:T(4,128)(2,1)S(1)}, bf16[6,4,2304]{2,1,0:T(4,128)(2,1)S(1)}, u32[]{:S(2)}, u32[]{:S(2)}) collective-permute-start(bf16[6,4,2304]{2,1,0:T(4,128)(2,1)S(1)} %collective-permute-done.1), channel_id=1, source_target_pairs={{0,7},{1,0},{2,1},{3,2},{4,3},{5,4},{6,5},{7,6},{8,15},{9,8},{10,9... | collective-permute-start | bytes 331784 | tf_op jit(solution)/shard_map/ppermute | solution.py:27
  68.0 1.8 %collective-permute-done.5 = bf16[6,4,2304]{2,1,0:T(4,128)(2,1)S(1)} collective-permute-done((bf16[6,4,2304]{2,1,0:T(4,128)(2,1)S(1)}, bf16[6,4,2304]{2,1,0:T(4,128)(2,1)S(1)}, u32[]{:S(2)}, u32[]{:S(2)}) %collective-permute-start.5) | collective-permute-done | bytes 110624 | tf_op jit(solution)/shard_map/ppermute | solution.py:26
  69.8 5.6 %collective-permute-start.6 = (bf16[3,4,2304]{2,1,0:T(4,128)(2,1)S(1)}, bf16[3,4,2304]{2,1,0:T(4,128)(2,1)S(1)}, u32[]{:S(2)}, u32[]{:S(2)}) collective-permute-start(bf16[3,4,2304]{2,1,0:T(4,128)(2,1)S(1)} %slice.84), channel_id=1, source_target_pairs={{0,1},{1,2},{2,3},{3,4},{4,5},{5,6},{6,7},{7,0},{8,9},{9,10},{10,1... | collective-permute-start | bytes 165896 | tf_op jit(solution)/shard_map/ppermute | solution.py:22
  75.5 1.9 %collective-permute-start.7 = (bf16[3,4,2304]{2,1,0:T(4,128)(2,1)S(1)}, bf16[3,4,2304]{2,1,0:T(4,128)(2,1)S(1)}, u32[]{:S(2)}, u32[]{:S(2)}) collective-permute-start(bf16[3,4,2304]{2,1,0:T(4,128)(2,1)S(1)} %slice.85), channel_id=1, source_target_pairs={{0,7},{1,0},{2,1},{3,2},{4,3},{5,4},{6,5},{7,6},{8,15},{9,8},{10,9... | collective-permute-start | bytes 165896 | tf_op jit(solution)/shard_map/ppermute | solution.py:23
  77.4 0.2 copy.135
  77.6 0.2 copy.136
  77.8 0.2 copy.142
  78.0 0.2 copy.137
  78.1 0.2 copy.141
  78.3 0.2 copy.138
  78.5 0.2 copy.140
  78.7 4.2 %collective-permute-done.7 = bf16[3,4,2304]{2,1,0:T(4,128)(2,1)S(1)} collective-permute-done((bf16[3,4,2304]{2,1,0:T(4,128)(2,1)S(1)}, bf16[3,4,2304]{2,1,0:T(4,128)(2,1)S(1)}, u32[]{:S(2)}, u32[]{:S(2)}) %collective-permute-start.7) | collective-permute-done | bytes 55328 | tf_op jit(solution)/shard_map/ppermute | solution.py:23
  82.9 0.2 copy.139
  83.1 2.8 %stack.41 = bf16[8,6,4,2304]{3,0,2,1:T(8,128)(2,1)S(1)} concatenate(bf16[1,6,4,2304]{3,0,2,1:T(2,128)(2,1)S(1)} %copy.135, bf16[1,6,4,2304]{3,0,2,1:T(2,128)(2,1)S(1)} %copy.136, bf16[1,6,4,2304]{3,0,2,1:T(2,128)(2,1)S(1)} %copy.137, bf16[1,6,4,2304]{3,0,2,1:T(2,128)(2,1)S(1)} %copy.138, bf16[1,6,4,2304]{3,0,2,1:T(2,128)(2,1)S(1)} %copy.139, bf16[1,6,4,2304]{3,0,2,1:T(2,128)(2,1)S(1)} %copy.140, ...), dimensions={0} | concatenate | bytes 1769472 | tf_op jit(solution)/shard_map/stack | solution.py:77
  85.9 3.3 %collective-permute-start.9 = (bf16[8,6,4,2304]{3,0,2,1:T(8,128)(2,1)S(1)}, bf16[8,6,4,2304]{3,0,2,1:T(8,128)(2,1)S(1)}, u32[]{:S(2)}, u32[]{:S(2)}) collective-permute-start(bf16[8,6,4,2304]{3,0,2,1:T(8,128)(2,1)S(1)} %stack.41), channel_id=1, source_target_pairs={{0,8},{8,16},{16,24},{24,0},{1,9},{9,17},{17,25},{25,1},{2,10},{10... | collective-permute-start | bytes 2654216 | tf_op jit(solution)/shard_map/ppermute | solution.py:26
  89.2 2.6 %collective-permute-start.8 = (bf16[8,6,4,2304]{3,0,2,1:T(8,128)(2,1)S(1)}, bf16[8,6,4,2304]{3,0,2,1:T(8,128)(2,1)}, u32[]{:S(2)}, u32[]{:S(2)}) collective-permute-start(bf16[8,6,4,2304]{3,0,2,1:T(8,128)(2,1)S(1)} %stack.41), channel_id=1, source_target_pairs={{0,24},{8,0},{16,8},{24,16},{1,25},{9,1},{17,9},{25,17},{2,26},{10... | collective-permute-start | bytes 2654216 | tf_op jit(solution)/shard_map/ppermute | solution.py:27
  91.8 1.6 slice.95
  94.1 1.5 constant_dynamic-update-slice_fusion.15
  95.6 24.0 %collective-permute-done.9 = bf16[8,6,4,2304]{3,0,2,1:T(8,128)(2,1)S(1)} collective-permute-done((bf16[8,6,4,2304]{3,0,2,1:T(8,128)(2,1)S(1)}, bf16[8,6,4,2304]{3,0,2,1:T(8,128)(2,1)S(1)}, u32[]{:S(2)}, u32[]{:S(2)}) %collective-permute-start.9) | collective-permute-done | bytes 884768 | tf_op jit(solution)/shard_map/ppermute | solution.py:26
  119.8 3.3 %collective-permute-start.10 = (bf16[4,6,4,2304]{3,0,2,1:T(4,128)(2,1)S(1)}, bf16[4,6,4,2304]{3,0,2,1:T(4,128)(2,1)S(1)}, u32[]{:S(2)}, u32[]{:S(2)}) collective-permute-start(bf16[4,6,4,2304]{3,0,2,1:T(4,128)(2,1)S(1)} %slice.88), channel_id=1, source_target_pairs={{0,8},{8,16},{16,24},{24,0},{1,9},{9,17},{17,25},{25,1},{2,10},{10... | collective-permute-start | bytes 1327112 | tf_op jit(solution)/shard_map/ppermute | solution.py:22
  123.1 2.0 %collective-permute-done.8 = bf16[8,6,4,2304]{3,0,2,1:T(8,128)(2,1)} collective-permute-done((bf16[8,6,4,2304]{3,0,2,1:T(8,128)(2,1)S(1)}, bf16[8,6,4,2304]{3,0,2,1:T(8,128)(2,1)}, u32[]{:S(2)}, u32[]{:S(2)}) %collective-permute-start.8) | collective-permute-done | bytes 884768 | tf_op jit(solution)/shard_map/ppermute | solution.py:27
  125.1 1.5 slice.89
  126.6 2.9 %collective-permute-start.11 = (bf16[4,6,4,2304]{3,0,2,1:T(4,128)(2,1)S(1)}, bf16[4,6,4,2304]{3,0,2,1:T(4,128)(2,1)S(1)}, u32[]{:S(2)}, u32[]{:S(2)}) collective-permute-start(bf16[4,6,4,2304]{3,0,2,1:T(4,128)(2,1)S(1)} %slice.89), channel_id=1, source_target_pairs={{0,24},{8,0},{16,8},{24,16},{1,25},{9,1},{17,9},{25,17},{2,26},{10... | collective-permute-start | bytes 1327112 | tf_op jit(solution)/shard_map/ppermute | solution.py:23
  129.5 0.9 slice_reduce_fusion.1
  130.6 2.5 %constant_dynamic-update-slice_fusion.14 = (f32[8,8,6,4,3,128]{5,1,4,3,2,0:T(8,128)}, f32[1,8,6,4,3,128]{5,1,4,3,2,0:T(8,128)S(1)}) fusion(f32[8,8,6,4,3,128]{5,1,4,3,2,0:T(8,128)} %get-tuple-element.24, bf16[3,2176,128]{2,1,0:T(8,128)(2,1)S(1)} %slice.95, bf16[8,6,4,2304]{3,0,2,1:T(8,128)(2,1)} %collective-permute-done.8), kind=kOutput, calls=%fused_computation.64 | convolution fusion | flops 339738624 | bytes 3145728 | tf_op jit(solution)/shard_map/rd,edc->rec/dot_general | solution.py:71
  133.1 4.0 %collective-permute-done.10 = bf16[4,6,4,2304]{3,0,2,1:T(4,128)(2,1)S(1)} collective-permute-done((bf16[4,6,4,2304]{3,0,2,1:T(4,128)(2,1)S(1)}, bf16[4,6,4,2304]{3,0,2,1:T(4,128)(2,1)S(1)}, u32[]{:S(2)}, u32[]{:S(2)}) %collective-permute-start.10) | collective-permute-done | bytes 442400 | tf_op jit(solution)/shard_map/ppermute | solution.py:22
  137.1 3.4 %collective-permute-done.11 = bf16[4,6,4,2304]{3,0,2,1:T(4,128)(2,1)S(1)} collective-permute-done((bf16[4,6,4,2304]{3,0,2,1:T(4,128)(2,1)S(1)}, bf16[4,6,4,2304]{3,0,2,1:T(4,128)(2,1)S(1)}, u32[]{:S(2)}, u32[]{:S(2)}) %collective-permute-start.11) | collective-permute-done | bytes 442400 | tf_op jit(solution)/shard_map/ppermute | solution.py:23
  140.5 0.1 fusion.44
  140.8 0.1 fusion.45
  140.9 0.2 copy.143
  141.3 0.6 gather_fusion.2
  141.8 2.4 %constant_dynamic-update-slice_fusion.13 = (f32[8,8,6,4,3,128]{5,1,4,3,2,0:T(8,128)}, f32[1,8,6,4,3,128]{5,1,4,3,2,0:T(8,128)S(1)}) fusion(f32[8,8,6,4,3,128]{5,1,4,3,2,0:T(8,128)} %get-tuple-element.26, bf16[3,2176,128]{2,1,0:T(8,128)(2,1)S(1)} %slice.95, bf16[4,6,4,2304]{3,0,2,1:T(4,128)(2,1)S(1)} %collective-permute-done.11, ...), kind=kOutput, calls=%fused_computation.63 | convolution fusion | flops 341508096 | bytes 3145728 | tf_op jit(solution)/shard_map/rd,edc->rec/dot_general | solution.py:71
  144.2 1.4 constant_dynamic-update-slice_fusion.12
  145.6 0.7 constant_dynamic-update-slice_fusion.11
  146.3 0.7 constant_dynamic-update-slice_fusion.10
  147.0 0.7 constant_dynamic-update-slice_fusion.9
  147.8 0.7 constant_dynamic-update-slice_fusion.8
  148.5 1.3 constant_dynamic-slice_fusion
  150.0 3.1 %copy.144 = bf16[32,24,3200]{2,0,1:T(8,128)(2,1)S(1)} copy(bf16[32,24,3200]{2,1,0:T(8,128)(2,1)} %all-gather.2.cloned.1.call-done) | data formatting | bytes 9830400 | tf_op jit(solution)/shard_map/all_gather | solution.py:74
  153.0 0.6 copy-done.1
  153.6 2.9 %fusion.13 = f32[6,3,4,8,4,128]{5,3,1,4,0,2:T(8,128)S(1)} fusion(bf16[3,5376,128]{2,1,0:T(8,128)(2,1)S(1)} %bitcast.143, bf16[4,8,6,4,3200,1]{4,1,0,3,2,5:T(8,128)(2,1)S(1)} %bitcast.140, s32[]{:T(128)S(6)} %select_n.190, f32[4,8,6,4,3,128]{5,1,4,3,2,0:T(8,128)S(1)} %constant_dynamic-slice_fusion), kind=kOutput, calls=%fused_computation.18 | convolution fusion | flops 1888026624 | bytes 9732100 | tf_op jit(solution)/shard_map/rd,edc->rec/dot_general | solution.py:71
  156.5 0.4 copy.146
  156.8 0.6 gather_fusion.3
  157.5 1.2 fusion.23
  (42 shorter events, 1.0 us)
Async XLA Ops:
  10.0 12.9 %copy-start.3 = (s32[16,6]{0,1:T(8,128)S(1)}, s32[16,6]{0,1:T(8,128)}, u32[]{:S(2)}) copy-start(s32[16,6]{0,1:T(8,128)} %param.11) | copy-start | bytes 1156
  10.0 13.1 %copy-start.4 = (s32[1,1,18,2]{2,3,1,0:T(2,128)S(1)}, s32[1,1,18,2]{2,3,1,0:T(2,128)}, u32[]{:S(2)}) copy-start(s32[1,1,18,2]{2,3,1,0:T(2,128)} %param.12) | copy-start | bytes 436
  12.4 29.6 %all-to-all-start = ((bf16[16,4,5504]{2,1,0:T(4,128)(2,1)}), bf16[16,4,5504]{2,1,0:T(4,128)(2,1)S(1)}, u32[]{:S(2)}, u32[]{:S(2)}) async-start(bf16[16,4,5504]{2,1,0:T(4,128)(2,1)} %broadcast_select_fusion), calls=%async_computation | async-start | bytes 1409024 | tf_op jit(solution)/shard_map/all_to_all | solution.py:51
  22.8 127.1 %all-gather.2.cloned.1.call-start = ((), (), s32[]{:S(2)}) async-start(), calls=%async_computation.1 | async-start | bytes 5068800 | tf_op jit(solution)/shard_map/all_gather | solution.py:74
  43.8 7.0 %collective-permute-start.3 = (bf16[6,4,2304]{2,1,0:T(4,128)(2,1)S(1)}, bf16[6,4,2304]{2,1,0:T(4,128)(2,1)S(1)}, u32[]{:S(2)}, u32[]{:S(2)}) collective-permute-start(bf16[6,4,2304]{2,1,0:T(4,128)(2,1)S(1)} %get-tuple-element.19), channel_id=1, source_target_pairs={{0,1},{1,2},{2,3},{3,4},{4,5},{5,6},{6,7},{7,0},{8,9},{9,10},{10,1... | collective-permute-start | bytes 331784 | tf_op jit(solution)/shard_map/ppermute | solution.py:26
  48.5 8.0 %collective-permute-start = (bf16[6,4,2304]{2,1,0:T(4,128)(2,1)S(1)}, bf16[6,4,2304]{2,1,0:T(4,128)(2,1)S(1)}, u32[]{:S(2)}, u32[]{:S(2)}) collective-permute-start(bf16[6,4,2304]{2,1,0:T(4,128)(2,1)S(1)} %get-tuple-element.19), channel_id=1, source_target_pairs={{0,7},{1,0},{2,1},{3,2},{4,3},{5,4},{6,5},{7,6},{8,15},{9,8},{10,9... | collective-permute-start | bytes 331784 | tf_op jit(solution)/shard_map/ppermute | solution.py:27
  50.8 9.6 %collective-permute-start.4 = (bf16[6,4,2304]{2,1,0:T(4,128)(2,1)S(1)}, bf16[6,4,2304]{2,1,0:T(4,128)(2,1)S(1)}, u32[]{:S(2)}, u32[]{:S(2)}) collective-permute-start(bf16[6,4,2304]{2,1,0:T(4,128)(2,1)S(1)} %collective-permute-done.3), channel_id=1, source_target_pairs={{0,1},{1,2},{2,3},{3,4},{4,5},{5,6},{6,7},{7,0},{8,9},{9,10},{10,1... | collective-permute-start | bytes 331784 | tf_op jit(solution)/shard_map/ppermute | solution.py:26
  56.6 9.5 %collective-permute-start.1 = (bf16[6,4,2304]{2,1,0:T(4,128)(2,1)S(1)}, bf16[6,4,2304]{2,1,0:T(4,128)(2,1)S(1)}, u32[]{:S(2)}, u32[]{:S(2)}) collective-permute-start(bf16[6,4,2304]{2,1,0:T(4,128)(2,1)S(1)} %collective-permute-done), channel_id=1, source_target_pairs={{0,7},{1,0},{2,1},{3,2},{4,3},{5,4},{6,5},{7,6},{8,15},{9,8},{10,9... | collective-permute-start | bytes 331784 | tf_op jit(solution)/shard_map/ppermute | solution.py:27
  60.5 9.4 %collective-permute-start.5 = (bf16[6,4,2304]{2,1,0:T(4,128)(2,1)S(1)}, bf16[6,4,2304]{2,1,0:T(4,128)(2,1)S(1)}, u32[]{:S(2)}, u32[]{:S(2)}) collective-permute-start(bf16[6,4,2304]{2,1,0:T(4,128)(2,1)S(1)} %collective-permute-done.4), channel_id=1, source_target_pairs={{0,1},{1,2},{2,3},{3,4},{4,5},{5,6},{6,7},{7,0},{8,9},{9,10},{10,1... | collective-permute-start | bytes 331784 | tf_op jit(solution)/shard_map/ppermute | solution.py:26
  66.1 9.4 %collective-permute-start.2 = (bf16[6,4,2304]{2,1,0:T(4,128)(2,1)S(1)}, bf16[6,4,2304]{2,1,0:T(4,128)(2,1)S(1)}, u32[]{:S(2)}, u32[]{:S(2)}) collective-permute-start(bf16[6,4,2304]{2,1,0:T(4,128)(2,1)S(1)} %collective-permute-done.1), channel_id=1, source_target_pairs={{0,7},{1,0},{2,1},{3,2},{4,3},{5,4},{6,5},{7,6},{8,15},{9,8},{10,9... | collective-permute-start | bytes 331784 | tf_op jit(solution)/shard_map/ppermute | solution.py:27
  69.8 8.8 %collective-permute-start.6 = (bf16[3,4,2304]{2,1,0:T(4,128)(2,1)S(1)}, bf16[3,4,2304]{2,1,0:T(4,128)(2,1)S(1)}, u32[]{:S(2)}, u32[]{:S(2)}) collective-permute-start(bf16[3,4,2304]{2,1,0:T(4,128)(2,1)S(1)} %slice.84), channel_id=1, source_target_pairs={{0,1},{1,2},{2,3},{3,4},{4,5},{5,6},{6,7},{7,0},{8,9},{9,10},{10,1... | collective-permute-start | bytes 165896 | tf_op jit(solution)/shard_map/ppermute | solution.py:22
  75.5 7.4 %collective-permute-start.7 = (bf16[3,4,2304]{2,1,0:T(4,128)(2,1)S(1)}, bf16[3,4,2304]{2,1,0:T(4,128)(2,1)S(1)}, u32[]{:S(2)}, u32[]{:S(2)}) collective-permute-start(bf16[3,4,2304]{2,1,0:T(4,128)(2,1)S(1)} %slice.85), channel_id=1, source_target_pairs={{0,7},{1,0},{2,1},{3,2},{4,3},{5,4},{6,5},{7,6},{8,15},{9,8},{10,9... | collective-permute-start | bytes 165896 | tf_op jit(solution)/shard_map/ppermute | solution.py:23
  85.9 33.7 %collective-permute-start.9 = (bf16[8,6,4,2304]{3,0,2,1:T(8,128)(2,1)S(1)}, bf16[8,6,4,2304]{3,0,2,1:T(8,128)(2,1)S(1)}, u32[]{:S(2)}, u32[]{:S(2)}) collective-permute-start(bf16[8,6,4,2304]{3,0,2,1:T(8,128)(2,1)S(1)} %stack.41), channel_id=1, source_target_pairs={{0,8},{8,16},{16,24},{24,0},{1,9},{9,17},{17,25},{25,1},{2,10},{10... | collective-permute-start | bytes 2654216 | tf_op jit(solution)/shard_map/ppermute | solution.py:26
  89.2 35.9 %collective-permute-start.8 = (bf16[8,6,4,2304]{3,0,2,1:T(8,128)(2,1)S(1)}, bf16[8,6,4,2304]{3,0,2,1:T(8,128)(2,1)}, u32[]{:S(2)}, u32[]{:S(2)}) collective-permute-start(bf16[8,6,4,2304]{3,0,2,1:T(8,128)(2,1)S(1)} %stack.41), channel_id=1, source_target_pairs={{0,24},{8,0},{16,8},{24,16},{1,25},{9,1},{17,9},{25,17},{2,26},{10... | collective-permute-start | bytes 2654216 | tf_op jit(solution)/shard_map/ppermute | solution.py:27
  119.8 17.3 %collective-permute-start.10 = (bf16[4,6,4,2304]{3,0,2,1:T(4,128)(2,1)S(1)}, bf16[4,6,4,2304]{3,0,2,1:T(4,128)(2,1)S(1)}, u32[]{:S(2)}, u32[]{:S(2)}) collective-permute-start(bf16[4,6,4,2304]{3,0,2,1:T(4,128)(2,1)S(1)} %slice.88), channel_id=1, source_target_pairs={{0,8},{8,16},{16,24},{24,0},{1,9},{9,17},{17,25},{25,1},{2,10},{10... | collective-permute-start | bytes 1327112 | tf_op jit(solution)/shard_map/ppermute | solution.py:22
  126.6 13.9 %collective-permute-start.11 = (bf16[4,6,4,2304]{3,0,2,1:T(4,128)(2,1)S(1)}, bf16[4,6,4,2304]{3,0,2,1:T(4,128)(2,1)S(1)}, u32[]{:S(2)}, u32[]{:S(2)}) collective-permute-start(bf16[4,6,4,2304]{3,0,2,1:T(4,128)(2,1)S(1)} %slice.89), channel_id=1, source_target_pairs={{0,24},{8,0},{16,8},{24,16},{1,25},{9,1},{17,9},{25,17},{2,26},{10... | collective-permute-start | bytes 1327112 | tf_op jit(solution)/shard_map/ppermute | solution.py:23
  137.1 3.5 %copy-start.2 = (bf16[4,6,4,2304]{3,0,2,1:T(4,128)(2,1)}, bf16[4,6,4,2304]{3,0,2,1:T(4,128)(2,1)S(1)}, u32[]{:S(2)}) copy-start(bf16[4,6,4,2304]{3,0,2,1:T(4,128)(2,1)S(1)} %collective-permute-done.10) | copy-start | bytes 1327108
  144.2 1.4 copy-start
  150.0 3.6 %copy-start.1 = (bf16[1,1,3,5376,128]{4,3,2,1,0:T(8,128)(2,1)S(1)}, bf16[1,1,3,5376,128]{4,3,2,1,0:T(8,128)(2,1)}, u32[]{:S(2)}) copy-start(bf16[1,1,3,5376,128]{4,3,2,1,0:T(8,128)(2,1)} %param.10) | copy-start | bytes 12386308
Sparse Core Ops, SparseCore 0:
  43.9 98.8 all-gather.1

commit v8 on v5

--- a/solution.py
+++ b/solution.py
@@ -39,21 +39,21 @@
     my_x = lax.axis_index("x")
     my_y = lax.axis_index("y")
 
-    act_block = jnp.zeros(src_act.shape + (LANES,), src_rows.dtype)
-    act_block = act_block.at[:, :, 0].set(src_act)
-    rows_ext = jnp.concatenate([src_rows, act_block], axis=-1)
-    ext_width = rows_ext.shape[-1]
+    ext_width = width + LANES
 
     is_valid = dest_list >= 0
     from_me = is_valid & (dest_list // nb_g == my_group)
     sel = jnp.sum(jnp.where(from_me, dest_list % nb_g, 0), axis=1)
-    send = jnp.take(rows_ext, sel, axis=0)
+    send_act = jnp.take(src_act, sel, axis=0, mode="clip")
+    act_block = jnp.zeros(send_act.shape + (LANES,), src_rows.dtype)
+    act_block = act_block.at[:, :, 0].set(send_act)
+    send = jnp.concatenate([jnp.take(src_rows, sel, axis=0, mode="clip"), act_block], axis=-1)
     recv = lax.all_to_all(send, GRP, 0, 0, tiled=True)
 
     my_list = lax.dynamic_index_in_dim(dest_list, my_group, 0, keepdims=False)
     my_valid = my_list >= 0
     source = jnp.where(my_valid, my_list // nb_g, 0)
-    slot_rows = jnp.take(recv, source, axis=0)
+    slot_rows = jnp.take(recv, source, axis=0, mode="clip")
     slot_rows = jnp.where(my_valid[:, None, None], slot_rows, jnp.zeros((), slot_rows.dtype))
     slots, rows_dev, _ = slot_rows.shape
 
@@ -90,8 +90,8 @@
     block_ids = dev_pairs[:, 1]
     amount = pair_count[0, 0]
     pair_total = dev_pairs.shape[0]
-    chosen = jnp.take(tiles, slot_ids * enc_count + block_ids, axis=0)
-    scales = jnp.take(scale_rows, slot_ids, axis=0).astype(jnp.float32)
+    chosen = jnp.take(tiles, slot_ids * enc_count + block_ids, axis=0, mode="clip")
+    scales = jnp.take(scale_rows, slot_ids, axis=0, mode="clip").astype(jnp.float32)
     is_live = jnp.arange(pair_total) < amount
     result = jnp.where(
         is_live[:, None, None], scales[:, :, None] * chosen, jnp.zeros((), jnp.float32)

time: 163 us -> 162 us (level)
  other arithmetic: 5.81 us -> 3.9 us
    gather x4 -> x6, local copies, waits for them, and re-layouts: 3.13 us -> 3.78 us  [the longest x1 1.14 us: local(): jnp.take(src_rows, sel, axis=0, mode='clip')]
    unnamed x23 -> x28, local copies, waits for them, and re-layouts: 3.79 us -> 3.73 us
where the time goes in v8:
time: 162 us; the launch traced here: 161 us
  waiting for transfers between devices  56.9 us (35%)
  starting transfers between devices  51.8 us (32%)
  local copies, waits for them, and re-layouts  20 us (12%)
  between operations  14.6 us (9%)
  matrix products  13.7 us (8%)
  other arithmetic  3.9 us (2%)
    ppermute x4, waiting for transfers between devices, ring_parts(): left = lax.ppermute(left, axis, up)  28.6 us
    ppermute x4, starting transfers between devices, ring_parts(): left = lax.ppermute(left, axis, up)  19.1 us
    all_to_all x1, waiting for transfers between devices, local(): recv = lax.all_to_all(send, GRP, 0, 0, tiled=True)  18.7 us
    dot_general x5, matrix products, mm(): jnp.einsum('rd,edc->rec', flat, enc, preferred_element_type=jnp.float32)  13.7 us
    all_to_all x1, starting transfers between devices, local(): recv = lax.all_to_all(send, GRP, 0, 0, tiled=True)  10.6 us
    ppermute x2, starting transfers between devices, ring_parts(): got_left = lax.ppermute(left[:half], axis, up)  8.92 us
    ppermute x4, starting transfers between devices, ring_parts(): right = lax.ppermute(right, axis, down)  8.31 us
    ppermute x2, waiting for transfers between devices, ring_parts(): got_right = lax.ppermute(right[half:], axis, down)  6.95 us
  transfers between devices with their start and end apart: 14, of which 10 were waited for; matrix products, arithmetic and copies ran while one was open for 13% of the time, Pallas kernels for 0%

profile of v8, /device:TPU:26, one launch (start us, length us, event | category | flops | bytes accessed | tf_op | source)
XLA Modules:
  0.0 160.8 jit_solution(6322489516725599008)
XLA Ops:
  6.5 0.8 fusion.30
  7.3 0.8 copy.153
  8.1 1.1 gather_fusion
  9.2 0.6 gather_fusion.1
  9.9 0.1 copy.177
  10.0 1.2 fusion.24
  11.2 10.6 %all-to-all-start = ((bf16[16,4,5504]{2,1,0:T(4,128)(2,1)}), bf16[16,4,5504]{2,1,0:T(4,128)(2,1)S(1)}, u32[]{:S(2)}, u32[]{:S(2)}) async-start(bf16[16,4,5504]{2,1,0:T(4,128)(2,1)} %fusion.24), calls=%async_computation | async-start | bytes 1409024 | tf_op jit(solution)/shard_map/all_to_all | solution.py:51
  21.8 0.2 dynamic-slice_reduce_fusion
  22.0 0.2 compare_reduce_fusion
  22.2 18.7 %all-to-all-done = bf16[16,4,5504]{2,1,0:T(4,128)(2,1)S(1)} async-done(((bf16[16,4,5504]{2,1,0:T(4,128)(2,1)}), bf16[16,4,5504]{2,1,0:T(4,128)(2,1)S(1)}, u32[]{:S(2)}, u32[]{:S(2)}) %all-to-all-start) | async-done | bytes 704544 | tf_op jit(solution)/shard_map/all_to_all | solution.py:51
  40.9 0.8 gather_fusion.2
  41.7 0.2 broadcast_select_fusion
  41.9 0.7 slice.95
  42.7 4.7 %collective-permute-start.3 = (bf16[6,4,2304]{2,1,0:T(4,128)(2,1)S(1)}, bf16[6,4,2304]{2,1,0:T(4,128)(2,1)S(1)}, u32[]{:S(2)}, u32[]{:S(2)}) collective-permute-start(bf16[6,4,2304]{2,1,0:T(4,128)(2,1)S(1)} %get-tuple-element.17), channel_id=1, source_target_pairs={{0,1},{1,2},{2,3},{3,4},{4,5},{5,6},{6,7},{7,0},{8,9},{9,10},{10,1... | collective-permute-start | bytes 331784 | tf_op jit(solution)/shard_map/ppermute | solution.py:26
  47.4 1.9 %collective-permute-start = (bf16[6,4,2304]{2,1,0:T(4,128)(2,1)S(1)}, bf16[6,4,2304]{2,1,0:T(4,128)(2,1)S(1)}, u32[]{:S(2)}, u32[]{:S(2)}) collective-permute-start(bf16[6,4,2304]{2,1,0:T(4,128)(2,1)S(1)} %get-tuple-element.17), channel_id=1, source_target_pairs={{0,7},{1,0},{2,1},{3,2},{4,3},{5,4},{6,5},{7,6},{8,15},{9,8},{10,9... | collective-permute-start | bytes 331784 | tf_op jit(solution)/shard_map/ppermute | solution.py:27
  49.3 0.4 collective-permute-done.3
  49.7 5.5 %collective-permute-start.4 = (bf16[6,4,2304]{2,1,0:T(4,128)(2,1)S(1)}, bf16[6,4,2304]{2,1,0:T(4,128)(2,1)S(1)}, u32[]{:S(2)}, u32[]{:S(2)}) collective-permute-start(bf16[6,4,2304]{2,1,0:T(4,128)(2,1)S(1)} %collective-permute-done.3), channel_id=1, source_target_pairs={{0,1},{1,2},{2,3},{3,4},{4,5},{5,6},{6,7},{7,0},{8,9},{9,10},{10,1... | collective-permute-start | bytes 331784 | tf_op jit(solution)/shard_map/ppermute | solution.py:26
  55.2 0.2 collective-permute-done
  55.4 1.9 %collective-permute-start.1 = (bf16[6,4,2304]{2,1,0:T(4,128)(2,1)S(1)}, bf16[6,4,2304]{2,1,0:T(4,128)(2,1)S(1)}, u32[]{:S(2)}, u32[]{:S(2)}) collective-permute-start(bf16[6,4,2304]{2,1,0:T(4,128)(2,1)S(1)} %collective-permute-done), channel_id=1, source_target_pairs={{0,7},{1,0},{2,1},{3,2},{4,3},{5,4},{6,5},{7,6},{8,15},{9,8},{10,9... | collective-permute-start | bytes 331784 | tf_op jit(solution)/shard_map/ppermute | solution.py:27
  57.3 2.0 %collective-permute-done.4 = bf16[6,4,2304]{2,1,0:T(4,128)(2,1)S(1)} collective-permute-done((bf16[6,4,2304]{2,1,0:T(4,128)(2,1)S(1)}, bf16[6,4,2304]{2,1,0:T(4,128)(2,1)S(1)}, u32[]{:S(2)}, u32[]{:S(2)}) %collective-permute-start.4) | collective-permute-done | bytes 110624 | tf_op jit(solution)/shard_map/ppermute | solution.py:26
  59.3 5.6 %collective-permute-start.5 = (bf16[6,4,2304]{2,1,0:T(4,128)(2,1)S(1)}, bf16[6,4,2304]{2,1,0:T(4,128)(2,1)S(1)}, u32[]{:S(2)}, u32[]{:S(2)}) collective-permute-start(bf16[6,4,2304]{2,1,0:T(4,128)(2,1)S(1)} %collective-permute-done.4), channel_id=1, source_target_pairs={{0,1},{1,2},{2,3},{3,4},{4,5},{5,6},{6,7},{7,0},{8,9},{9,10},{10,1... | collective-permute-start | bytes 331784 | tf_op jit(solution)/shard_map/ppermute | solution.py:26
  64.9 1.9 %collective-permute-start.2 = (bf16[6,4,2304]{2,1,0:T(4,128)(2,1)S(1)}, bf16[6,4,2304]{2,1,0:T(4,128)(2,1)S(1)}, u32[]{:S(2)}, u32[]{:S(2)}) collective-permute-start(bf16[6,4,2304]{2,1,0:T(4,128)(2,1)S(1)} %collective-permute-done.1), channel_id=1, source_target_pairs={{0,7},{1,0},{2,1},{3,2},{4,3},{5,4},{6,5},{7,6},{8,15},{9,8},{10,9... | collective-permute-start | bytes 331784 | tf_op jit(solution)/shard_map/ppermute | solution.py:27
  66.9 1.8 %collective-permute-done.5 = bf16[6,4,2304]{2,1,0:T(4,128)(2,1)S(1)} collective-permute-done((bf16[6,4,2304]{2,1,0:T(4,128)(2,1)S(1)}, bf16[6,4,2304]{2,1,0:T(4,128)(2,1)S(1)}, u32[]{:S(2)}, u32[]{:S(2)}) %collective-permute-start.5) | collective-permute-done | bytes 110624 | tf_op jit(solution)/shard_map/ppermute | solution.py:26
  68.7 5.6 %collective-permute-start.6 = (bf16[3,4,2304]{2,1,0:T(4,128)(2,1)S(1)}, bf16[3,4,2304]{2,1,0:T(4,128)(2,1)S(1)}, u32[]{:S(2)}, u32[]{:S(2)}) collective-permute-start(bf16[3,4,2304]{2,1,0:T(4,128)(2,1)S(1)} %slice.86), channel_id=1, source_target_pairs={{0,1},{1,2},{2,3},{3,4},{4,5},{5,6},{6,7},{7,0},{8,9},{9,10},{10,1... | collective-permute-start | bytes 165896 | tf_op jit(solution)/shard_map/ppermute | solution.py:22
  74.4 1.9 %collective-permute-start.7 = (bf16[3,4,2304]{2,1,0:T(4,128)(2,1)S(1)}, bf16[3,4,2304]{2,1,0:T(4,128)(2,1)S(1)}, u32[]{:S(2)}, u32[]{:S(2)}) collective-permute-start(bf16[3,4,2304]{2,1,0:T(4,128)(2,1)S(1)} %slice.87), channel_id=1, source_target_pairs={{0,7},{1,0},{2,1},{3,2},{4,3},{5,4},{6,5},{7,6},{8,15},{9,8},{10,9... | collective-permute-start | bytes 165896 | tf_op jit(solution)/shard_map/ppermute | solution.py:23
  77.0 0.2 copy.156
  77.1 0.2 copy.157
  77.3 0.2 copy.163
  77.5 0.2 copy.158
  77.7 0.2 copy.162
  77.9 0.2 copy.159
  78.0 0.2 copy.161
  78.2 3.5 %collective-permute-done.7 = bf16[3,4,2304]{2,1,0:T(4,128)(2,1)S(1)} collective-permute-done((bf16[3,4,2304]{2,1,0:T(4,128)(2,1)S(1)}, bf16[3,4,2304]{2,1,0:T(4,128)(2,1)S(1)}, u32[]{:S(2)}, u32[]{:S(2)}) %collective-permute-start.7) | collective-permute-done | bytes 55328 | tf_op jit(solution)/shard_map/ppermute | solution.py:23
  81.8 0.2 copy.160
  82.0 2.8 %stack.41 = bf16[8,6,4,2304]{3,0,2,1:T(8,128)(2,1)S(1)} concatenate(bf16[1,6,4,2304]{3,0,2,1:T(2,128)(2,1)S(1)} %copy.156, bf16[1,6,4,2304]{3,0,2,1:T(2,128)(2,1)S(1)} %copy.157, bf16[1,6,4,2304]{3,0,2,1:T(2,128)(2,1)S(1)} %copy.158, bf16[1,6,4,2304]{3,0,2,1:T(2,128)(2,1)S(1)} %copy.159, bf16[1,6,4,2304]{3,0,2,1:T(2,128)(2,1)S(1)} %copy.160, bf16[1,6,4,2304]{3,0,2,1:T(2,128)(2,1)S(1)} %copy.161, ...), dimensions={0} | concatenate | bytes 1769472 | tf_op jit(solution)/shard_map/stack | solution.py:76
  84.8 3.3 %collective-permute-start.9 = (bf16[8,6,4,2304]{3,0,2,1:T(8,128)(2,1)S(1)}, bf16[8,6,4,2304]{3,0,2,1:T(8,128)(2,1)}, u32[]{:S(2)}, u32[]{:S(2)}) collective-permute-start(bf16[8,6,4,2304]{3,0,2,1:T(8,128)(2,1)S(1)} %stack.41), channel_id=1, source_target_pairs={{0,8},{8,16},{16,24},{24,0},{1,9},{9,17},{17,25},{25,1},{2,10},{10... | collective-permute-start | bytes 2654216 | tf_op jit(solution)/shard_map/ppermute | solution.py:26
  88.0 2.6 %collective-permute-start.8 = (bf16[8,6,4,2304]{3,0,2,1:T(8,128)(2,1)S(1)}, bf16[8,6,4,2304]{3,0,2,1:T(8,128)(2,1)}, u32[]{:S(2)}, u32[]{:S(2)}) collective-permute-start(bf16[8,6,4,2304]{3,0,2,1:T(8,128)(2,1)S(1)} %stack.41), channel_id=1, source_target_pairs={{0,24},{8,0},{16,8},{24,16},{1,25},{9,1},{17,9},{25,17},{2,26},{10... | collective-permute-start | bytes 2654216 | tf_op jit(solution)/shard_map/ppermute | solution.py:27
  90.7 1.6 slice.97
  92.4 0.6 fusion.7
  93.0 0.8 bitcast_dynamic-update-slice_fusion.6
  93.8 24.4 %collective-permute-done.9 = bf16[8,6,4,2304]{3,0,2,1:T(8,128)(2,1)} collective-permute-done((bf16[8,6,4,2304]{3,0,2,1:T(8,128)(2,1)S(1)}, bf16[8,6,4,2304]{3,0,2,1:T(8,128)(2,1)}, u32[]{:S(2)}, u32[]{:S(2)}) %collective-permute-start.9) | collective-permute-done | bytes 884768 | tf_op jit(solution)/shard_map/ppermute | solution.py:26
  118.2 1.3 slice.90
  119.5 3.3 %collective-permute-start.10 = (bf16[4,6,4,2304]{3,0,2,1:T(4,128)(2,1)S(1)}, bf16[4,6,4,2304]{3,0,2,1:T(4,128)(2,1)S(1)}, u32[]{:S(2)}, u32[]{:S(2)}) collective-permute-start(bf16[4,6,4,2304]{3,0,2,1:T(4,128)(2,1)S(1)} %slice.90), channel_id=1, source_target_pairs={{0,8},{8,16},{16,24},{24,0},{1,9},{9,17},{17,25},{25,1},{2,10},{10... | collective-permute-start | bytes 1327112 | tf_op jit(solution)/shard_map/ppermute | solution.py:22
  122.9 1.1 collective-permute-done.8
  124.0 1.5 slice.91
  125.5 2.9 %collective-permute-start.11 = (bf16[4,6,4,2304]{3,0,2,1:T(4,128)(2,1)S(1)}, bf16[4,6,4,2304]{3,0,2,1:T(4,128)(2,1)S(1)}, u32[]{:S(2)}, u32[]{:S(2)}) collective-permute-start(bf16[4,6,4,2304]{3,0,2,1:T(4,128)(2,1)S(1)} %slice.91), channel_id=1, source_target_pairs={{0,24},{8,0},{16,8},{24,16},{1,25},{9,1},{17,9},{25,17},{2,26},{10... | collective-permute-start | bytes 1327112 | tf_op jit(solution)/shard_map/ppermute | solution.py:23
  128.4 0.9 slice_reduce_fusion.1
  129.3 0.9 slice_reduce_fusion
  130.2 1.8 %fusion.5 = f32[8,6,4,3,128]{4,0,3,2,1:T(8,128)S(1)} fusion(bf16[3,2176,128]{2,1,0:T(8,128)(2,1)S(1)} %slice.97, bf16[8,6,4,2304]{3,0,2,1:T(8,128)(2,1)} %collective-permute-done.8), kind=kOutput, calls=%fused_computation.13 | convolution fusion | flops 339738624 | bytes 2850816 | tf_op jit(solution)/shard_map/rd,edc->rec/dot_general | solution.py:71
  132.0 0.8 bitcast_dynamic-update-slice_fusion.4
  132.8 1.8 %fusion.1 = f32[8,6,4,3,128]{4,0,3,2,1:T(8,128)S(1)} fusion(bf16[3,2176,128]{2,1,0:T(8,128)(2,1)S(1)} %slice.97, bf16[8,6,4,2304]{3,0,2,1:T(8,128)(2,1)} %collective-permute-done.9), kind=kOutput, calls=%fused_computation.9 | convolution fusion | flops 339738624 | bytes 2850816 | tf_op jit(solution)/shard_map/rd,edc->rec/dot_general | solution.py:71
  134.6 1.3 collective-permute-done.10
  135.9 3.4 %collective-permute-done.11 = bf16[4,6,4,2304]{3,0,2,1:T(4,128)(2,1)S(1)} collective-permute-done((bf16[4,6,4,2304]{3,0,2,1:T(4,128)(2,1)S(1)}, bf16[4,6,4,2304]{3,0,2,1:T(4,128)(2,1)S(1)}, u32[]{:S(2)}, u32[]{:S(2)}) %collective-permute-start.11) | collective-permute-done | bytes 442400 | tf_op jit(solution)/shard_map/ppermute | solution.py:23
  139.4 0.1 fusion.26
  139.5 0.6 copy-done.3
  140.2 0.1 fusion.27
  140.4 0.2 copy.164
  140.7 0.6 gather_fusion.3
  141.3 2.0 %fusion.3 = f32[8,6,4,3,128]{4,0,3,2,1:T(8,128)S(1)} fusion(bf16[3,2176,128]{2,1,0:T(8,128)(2,1)S(1)} %slice.97, bf16[4,6,4,2304]{3,0,2,1:T(4,128)(2,1)} %copy-done.3, bf16[4,6,4,2304]{3,0,2,1:T(4,128)(2,1)} %copy-done.2), kind=kOutput, calls=%fused_computation.11 | convolution fusion | flops 341508096 | bytes 2850816 | tf_op jit(solution)/shard_map/rd,edc->rec/dot_general | solution.py:71
  144.0 0.2 constant_dynamic-slice_fusion
  144.2 7.5 %fusion.11 = f32[6,3,4,8,4,128]{5,4,1,0,3,2:T(4,128)S(1)} fusion(bf16[4,8,6,4,3200,1]{4,3,5,2,1,0:T(4,128)(2,1)} %bitcast.125, bf16[3,5376,128]{2,1,0:T(8,128)(2,1)} %bitcast.116, s32[]{:T(128)S(6)} %select_n.102, f32[4,8,6,4,3,128]{5,3,4,2,1,0:T(4,128)S(1)} %constant_dynamic-slice_fusion), kind=kOutput, calls=%fused_computation.20 | convolution fusion | flops 1888026624 | bytes 9732100 | tf_op jit(solution)/shard_map/rd,edc->rec/dot_general | solution.py:71
  151.8 0.3 copy.169
  152.1 0.6 gather_fusion.4
  152.7 1.2 fusion.18
  (46 shorter events, 1.4 us)
Async XLA Ops:
  6.5 1.5 copy-start
  9.2 12.6 %copy-start.4 = (s32[16,6]{0,1:T(8,128)S(1)}, s32[16,6]{0,1:T(8,128)}, u32[]{:S(2)}) copy-start(s32[16,6]{0,1:T(8,128)} %param.11) | copy-start | bytes 1156
  11.2 55.6 %copy-start.5 = (s32[1,1,18,2]{2,3,1,0:T(2,128)S(1)}, s32[1,1,18,2]{2,3,1,0:T(2,128)}, u32[]{:S(2)}) copy-start(s32[1,1,18,2]{2,3,1,0:T(2,128)} %param.12) | copy-start | bytes 436
  11.2 29.7 %all-to-all-start = ((bf16[16,4,5504]{2,1,0:T(4,128)(2,1)}), bf16[16,4,5504]{2,1,0:T(4,128)(2,1)S(1)}, u32[]{:S(2)}, u32[]{:S(2)}) async-start(bf16[16,4,5504]{2,1,0:T(4,128)(2,1)} %fusion.24), calls=%async_computation | async-start | bytes 1409024 | tf_op jit(solution)/shard_map/all_to_all | solution.py:51
  21.8 122.4 %all-gather.3.cloned.1.call-start = ((), (), s32[]{:S(2)}) async-start(), calls=%async_computation.1 | async-start | bytes 5068800 | tf_op jit(solution)/shard_map/all_gather | solution.py:73
  42.7 7.0 %collective-permute-start.3 = (bf16[6,4,2304]{2,1,0:T(4,128)(2,1)S(1)}, bf16[6,4,2304]{2,1,0:T(4,128)(2,1)S(1)}, u32[]{:S(2)}, u32[]{:S(2)}) collective-permute-start(bf16[6,4,2304]{2,1,0:T(4,128)(2,1)S(1)} %get-tuple-element.17), channel_id=1, source_target_pairs={{0,1},{1,2},{2,3},{3,4},{4,5},{5,6},{6,7},{7,0},{8,9},{9,10},{10,1... | collective-permute-start | bytes 331784 | tf_op jit(solution)/shard_map/ppermute | solution.py:26
  47.4 8.0 %collective-permute-start = (bf16[6,4,2304]{2,1,0:T(4,128)(2,1)S(1)}, bf16[6,4,2304]{2,1,0:T(4,128)(2,1)S(1)}, u32[]{:S(2)}, u32[]{:S(2)}) collective-permute-start(bf16[6,4,2304]{2,1,0:T(4,128)(2,1)S(1)} %get-tuple-element.17), channel_id=1, source_target_pairs={{0,7},{1,0},{2,1},{3,2},{4,3},{5,4},{6,5},{7,6},{8,15},{9,8},{10,9... | collective-permute-start | bytes 331784 | tf_op jit(solution)/shard_map/ppermute | solution.py:27
  49.7 9.6 %collective-permute-start.4 = (bf16[6,4,2304]{2,1,0:T(4,128)(2,1)S(1)}, bf16[6,4,2304]{2,1,0:T(4,128)(2,1)S(1)}, u32[]{:S(2)}, u32[]{:S(2)}) collective-permute-start(bf16[6,4,2304]{2,1,0:T(4,128)(2,1)S(1)} %collective-permute-done.3), channel_id=1, source_target_pairs={{0,1},{1,2},{2,3},{3,4},{4,5},{5,6},{6,7},{7,0},{8,9},{9,10},{10,1... | collective-permute-start | bytes 331784 | tf_op jit(solution)/shard_map/ppermute | solution.py:26
  55.4 9.5 %collective-permute-start.1 = (bf16[6,4,2304]{2,1,0:T(4,128)(2,1)S(1)}, bf16[6,4,2304]{2,1,0:T(4,128)(2,1)S(1)}, u32[]{:S(2)}, u32[]{:S(2)}) collective-permute-start(bf16[6,4,2304]{2,1,0:T(4,128)(2,1)S(1)} %collective-permute-done), channel_id=1, source_target_pairs={{0,7},{1,0},{2,1},{3,2},{4,3},{5,4},{6,5},{7,6},{8,15},{9,8},{10,9... | collective-permute-start | bytes 331784 | tf_op jit(solution)/shard_map/ppermute | solution.py:27
  59.3 9.4 %collective-permute-start.5 = (bf16[6,4,2304]{2,1,0:T(4,128)(2,1)S(1)}, bf16[6,4,2304]{2,1,0:T(4,128)(2,1)S(1)}, u32[]{:S(2)}, u32[]{:S(2)}) collective-permute-start(bf16[6,4,2304]{2,1,0:T(4,128)(2,1)S(1)} %collective-permute-done.4), channel_id=1, source_target_pairs={{0,1},{1,2},{2,3},{3,4},{4,5},{5,6},{6,7},{7,0},{8,9},{9,10},{10,1... | collective-permute-start | bytes 331784 | tf_op jit(solution)/shard_map/ppermute | solution.py:26
  64.9 9.4 %collective-permute-start.2 = (bf16[6,4,2304]{2,1,0:T(4,128)(2,1)S(1)}, bf16[6,4,2304]{2,1,0:T(4,128)(2,1)S(1)}, u32[]{:S(2)}, u32[]{:S(2)}) collective-permute-start(bf16[6,4,2304]{2,1,0:T(4,128)(2,1)S(1)} %collective-permute-done.1), channel_id=1, source_target_pairs={{0,7},{1,0},{2,1},{3,2},{4,3},{5,4},{6,5},{7,6},{8,15},{9,8},{10,9... | collective-permute-start | bytes 331784 | tf_op jit(solution)/shard_map/ppermute | solution.py:27
  68.7 9.5 %collective-permute-start.6 = (bf16[3,4,2304]{2,1,0:T(4,128)(2,1)S(1)}, bf16[3,4,2304]{2,1,0:T(4,128)(2,1)S(1)}, u32[]{:S(2)}, u32[]{:S(2)}) collective-permute-start(bf16[3,4,2304]{2,1,0:T(4,128)(2,1)S(1)} %slice.86), channel_id=1, source_target_pairs={{0,1},{1,2},{2,3},{3,4},{4,5},{5,6},{6,7},{7,0},{8,9},{9,10},{10,1... | collective-permute-start | bytes 165896 | tf_op jit(solution)/shard_map/ppermute | solution.py:22
  74.4 7.4 %collective-permute-start.7 = (bf16[3,4,2304]{2,1,0:T(4,128)(2,1)S(1)}, bf16[3,4,2304]{2,1,0:T(4,128)(2,1)S(1)}, u32[]{:S(2)}, u32[]{:S(2)}) collective-permute-start(bf16[3,4,2304]{2,1,0:T(4,128)(2,1)S(1)} %slice.87), channel_id=1, source_target_pairs={{0,7},{1,0},{2,1},{3,2},{4,3},{5,4},{6,5},{7,6},{8,15},{9,8},{10,9... | collective-permute-start | bytes 165896 | tf_op jit(solution)/shard_map/ppermute | solution.py:23
  84.8 33.5 %collective-permute-start.9 = (bf16[8,6,4,2304]{3,0,2,1:T(8,128)(2,1)S(1)}, bf16[8,6,4,2304]{3,0,2,1:T(8,128)(2,1)}, u32[]{:S(2)}, u32[]{:S(2)}) collective-permute-start(bf16[8,6,4,2304]{3,0,2,1:T(8,128)(2,1)S(1)} %stack.41), channel_id=1, source_target_pairs={{0,8},{8,16},{16,24},{24,0},{1,9},{9,17},{17,25},{25,1},{2,10},{10... | collective-permute-start | bytes 2654216 | tf_op jit(solution)/shard_map/ppermute | solution.py:26
  88.0 35.9 %collective-permute-start.8 = (bf16[8,6,4,2304]{3,0,2,1:T(8,128)(2,1)S(1)}, bf16[8,6,4,2304]{3,0,2,1:T(8,128)(2,1)}, u32[]{:S(2)}, u32[]{:S(2)}) collective-permute-start(bf16[8,6,4,2304]{3,0,2,1:T(8,128)(2,1)S(1)} %stack.41), channel_id=1, source_target_pairs={{0,24},{8,0},{16,8},{24,16},{1,25},{9,1},{17,9},{25,17},{2,26},{10... | collective-permute-start | bytes 2654216 | tf_op jit(solution)/shard_map/ppermute | solution.py:27
  119.5 16.4 %collective-permute-start.10 = (bf16[4,6,4,2304]{3,0,2,1:T(4,128)(2,1)S(1)}, bf16[4,6,4,2304]{3,0,2,1:T(4,128)(2,1)S(1)}, u32[]{:S(2)}, u32[]{:S(2)}) collective-permute-start(bf16[4,6,4,2304]{3,0,2,1:T(4,128)(2,1)S(1)} %slice.90), channel_id=1, source_target_pairs={{0,8},{8,16},{16,24},{24,0},{1,9},{9,17},{17,25},{25,1},{2,10},{10... | collective-permute-start | bytes 1327112 | tf_op jit(solution)/shard_map/ppermute | solution.py:22
  125.5 13.9 %collective-permute-start.11 = (bf16[4,6,4,2304]{3,0,2,1:T(4,128)(2,1)S(1)}, bf16[4,6,4,2304]{3,0,2,1:T(4,128)(2,1)S(1)}, u32[]{:S(2)}, u32[]{:S(2)}) collective-permute-start(bf16[4,6,4,2304]{3,0,2,1:T(4,128)(2,1)S(1)} %slice.91), channel_id=1, source_target_pairs={{0,24},{8,0},{16,8},{24,16},{1,25},{9,1},{17,9},{25,17},{2,26},{10... | collective-permute-start | bytes 1327112 | tf_op jit(solution)/shard_map/ppermute | solution.py:23
  135.9 3.5 %copy-start.2 = (bf16[4,6,4,2304]{3,0,2,1:T(4,128)(2,1)}, bf16[4,6,4,2304]{3,0,2,1:T(4,128)(2,1)S(1)}, u32[]{:S(2)}) copy-start(bf16[4,6,4,2304]{3,0,2,1:T(4,128)(2,1)S(1)} %collective-permute-done.10) | copy-start | bytes 1327108
  139.4 0.8 copy-start.3
  141.3 2.0 %copy-start.1 = (f32[8,8,6,4,3,128]{5,3,4,2,1,0:T(4,128)S(1)}, f32[8,8,6,4,3,128]{5,3,4,2,1,0:T(4,128)}, u32[]{:S(2)}) copy-start(f32[8,8,6,4,3,128]{5,3,4,2,1,0:T(4,128)} %bitcast_dynamic-update-slice_fusion.4) | copy-start | bytes 7077892
Sparse Core Ops, SparseCore 0:
  42.7 99.2 all-gather.2

commit v9 on v8

--- a/solution.py
+++ b/solution.py
@@ -63,12 +63,14 @@
 
     weights = encoder[0, 0]
     enc_count, _, tile_cols = weights.shape
-    enc_a = weights[:, :split, :]
+    enc_a = jnp.transpose(weights[:, :split, :], (1, 0, 2)).reshape(split, enc_count * tile_cols)
     enc_b = jnp.pad(weights[:, split:, :], ((0, 0), (0, ext_width - width), (0, 0)))
+    enc_b = jnp.transpose(enc_b, (1, 0, 2)).reshape(ext_width - split, enc_count * tile_cols)
 
     def mm(block, enc):
         flat = block.reshape(-1, block.shape[-1])
-        return jnp.einsum("rd,edc->rec", flat, enc, preferred_element_type=jnp.float32)
+        out = jnp.dot(flat, enc, preferred_element_type=jnp.float32)
+        return out.reshape(-1, enc_count, tile_cols)
 
     a_all = lax.all_gather(part_a, SHARD, axis=0, tiled=False)
     prod_a = mm(a_all, enc_a).reshape(n_x, n_y, slots, rows_dev, enc_count, tile_cols)

time: 162 us -> 161 us (level)
  waiting for transfers between devices: 56.9 us -> 50 us
  local copies, waits for them, and re-layouts: 20 us -> 26.5 us
    ppermute x4, waiting for transfers between devices: 28.6 us -> 21.9 us  [ring_parts(): left = lax.ppermute(left, axis, up)]
    unnamed x28 -> x29, local copies, waits for them, and re-layouts: 3.73 us -> 10.2 us
  transfers between devices with their start and end apart: 14 -> 14, of which waited for: 10 -> 10; matrix products, arithmetic and copies ran while one was open for 13% -> 17% of each run, Pallas kernels for 0% -> 0%
where the time goes in v9:
time: 161 us; the launch traced here: 160 us
  starting transfers between devices  51.8 us (32%)
  waiting for transfers between devices  50 us (31%)
  local copies, waits for them, and re-layouts  26.5 us (16%)
  between operations  14.6 us (9%)
  matrix products  13.3 us (8%)
  other arithmetic  3.9 us (2%)
    ppermute x4, waiting for transfers between devices, ring_parts(): left = lax.ppermute(left, axis, up)  21.9 us
    ppermute x4, starting transfers between devices, ring_parts(): left = lax.ppermute(left, axis, up)  19.1 us
    all_to_all x1, waiting for transfers between devices, local(): recv = lax.all_to_all(send, GRP, 0, 0, tiled=True)  18.7 us
    dot_general x5, matrix products, mm(): out = jnp.dot(flat, enc, preferred_element_type=jnp.float32)  13.3 us
    all_to_all x1, starting transfers between devices, local(): recv = lax.all_to_all(send, GRP, 0, 0, tiled=True)  10.6 us
    unnamed x29, local copies, waits for them, and re-layouts  10.2 us
    ppermute x2, starting transfers between devices, ring_parts(): got_left = lax.ppermute(left[:half], axis, up)  8.92 us
    ppermute x4, starting transfers between devices, ring_parts(): right = lax.ppermute(right, axis, down)  8.31 us
  transfers between devices with their start and end apart: 14, of which 10 were waited for; matrix products, arithmetic and copies ran while one was open for 17% of the time, Pallas kernels for 0%

profile of v9, /device:TPU:26, one launch (start us, length us, event | category | flops | bytes accessed | tf_op | source)
XLA Modules:
  0.0 160.1 jit_solution(10366651018081856016)
XLA Ops:
  6.5 0.8 fusion.30
  7.3 0.8 copy.161
  8.1 1.1 gather_fusion
  9.2 0.6 gather_fusion.1
  9.9 0.1 copy.186
  10.0 1.2 fusion.24
  11.2 10.6 %all-to-all-start = ((bf16[16,4,5504]{2,1,0:T(4,128)(2,1)}), bf16[16,4,5504]{2,1,0:T(4,128)(2,1)S(1)}, u32[]{:S(2)}, u32[]{:S(2)}) async-start(bf16[16,4,5504]{2,1,0:T(4,128)(2,1)} %fusion.24), calls=%async_computation | async-start | bytes 1409024 | tf_op jit(solution)/shard_map/all_to_all | solution.py:51
  21.8 0.2 dynamic-slice_reduce_fusion
  22.0 0.2 compare_reduce_fusion
  22.2 18.7 %all-to-all-done = bf16[16,4,5504]{2,1,0:T(4,128)(2,1)S(1)} async-done(((bf16[16,4,5504]{2,1,0:T(4,128)(2,1)}), bf16[16,4,5504]{2,1,0:T(4,128)(2,1)S(1)}, u32[]{:S(2)}, u32[]{:S(2)}) %all-to-all-start) | async-done | bytes 704544 | tf_op jit(solution)/shard_map/all_to_all | solution.py:51
  40.9 0.8 gather_fusion.2
  41.7 0.2 broadcast_select_fusion
  41.9 0.7 slice.95
  42.7 4.7 %collective-permute-start.3 = (bf16[6,4,2304]{2,1,0:T(4,128)(2,1)S(1)}, bf16[6,4,2304]{2,1,0:T(4,128)(2,1)S(1)}, u32[]{:S(2)}, u32[]{:S(2)}) collective-permute-start(bf16[6,4,2304]{2,1,0:T(4,128)(2,1)S(1)} %get-tuple-element.17), channel_id=1, source_target_pairs={{0,1},{1,2},{2,3},{3,4},{4,5},{5,6},{6,7},{7,0},{8,9},{9,10},{10,1... | collective-permute-start | bytes 331784 | tf_op jit(solution)/shard_map/ppermute | solution.py:26
  47.4 1.9 %collective-permute-start = (bf16[6,4,2304]{2,1,0:T(4,128)(2,1)S(1)}, bf16[6,4,2304]{2,1,0:T(4,128)(2,1)S(1)}, u32[]{:S(2)}, u32[]{:S(2)}) collective-permute-start(bf16[6,4,2304]{2,1,0:T(4,128)(2,1)S(1)} %get-tuple-element.17), channel_id=1, source_target_pairs={{0,7},{1,0},{2,1},{3,2},{4,3},{5,4},{6,5},{7,6},{8,15},{9,8},{10,9... | collective-permute-start | bytes 331784 | tf_op jit(solution)/shard_map/ppermute | solution.py:27
  49.3 0.4 collective-permute-done.3
  49.7 5.5 %collective-permute-start.4 = (bf16[6,4,2304]{2,1,0:T(4,128)(2,1)S(1)}, bf16[6,4,2304]{2,1,0:T(4,128)(2,1)S(1)}, u32[]{:S(2)}, u32[]{:S(2)}) collective-permute-start(bf16[6,4,2304]{2,1,0:T(4,128)(2,1)S(1)} %collective-permute-done.3), channel_id=1, source_target_pairs={{0,1},{1,2},{2,3},{3,4},{4,5},{5,6},{6,7},{7,0},{8,9},{9,10},{10,1... | collective-permute-start | bytes 331784 | tf_op jit(solution)/shard_map/ppermute | solution.py:26
  55.2 0.2 collective-permute-done
  55.4 1.9 %collective-permute-start.1 = (bf16[6,4,2304]{2,1,0:T(4,128)(2,1)S(1)}, bf16[6,4,2304]{2,1,0:T(4,128)(2,1)S(1)}, u32[]{:S(2)}, u32[]{:S(2)}) collective-permute-start(bf16[6,4,2304]{2,1,0:T(4,128)(2,1)S(1)} %collective-permute-done), channel_id=1, source_target_pairs={{0,7},{1,0},{2,1},{3,2},{4,3},{5,4},{6,5},{7,6},{8,15},{9,8},{10,9... | collective-permute-start | bytes 331784 | tf_op jit(solution)/shard_map/ppermute | solution.py:27
  57.3 2.0 %collective-permute-done.4 = bf16[6,4,2304]{2,1,0:T(4,128)(2,1)S(1)} collective-permute-done((bf16[6,4,2304]{2,1,0:T(4,128)(2,1)S(1)}, bf16[6,4,2304]{2,1,0:T(4,128)(2,1)S(1)}, u32[]{:S(2)}, u32[]{:S(2)}) %collective-permute-start.4) | collective-permute-done | bytes 110624 | tf_op jit(solution)/shard_map/ppermute | solution.py:26
  59.3 5.6 %collective-permute-start.5 = (bf16[6,4,2304]{2,1,0:T(4,128)(2,1)S(1)}, bf16[6,4,2304]{2,1,0:T(4,128)(2,1)S(1)}, u32[]{:S(2)}, u32[]{:S(2)}) collective-permute-start(bf16[6,4,2304]{2,1,0:T(4,128)(2,1)S(1)} %collective-permute-done.4), channel_id=1, source_target_pairs={{0,1},{1,2},{2,3},{3,4},{4,5},{5,6},{6,7},{7,0},{8,9},{9,10},{10,1... | collective-permute-start | bytes 331784 | tf_op jit(solution)/shard_map/ppermute | solution.py:26
  64.9 1.9 %collective-permute-start.2 = (bf16[6,4,2304]{2,1,0:T(4,128)(2,1)S(1)}, bf16[6,4,2304]{2,1,0:T(4,128)(2,1)S(1)}, u32[]{:S(2)}, u32[]{:S(2)}) collective-permute-start(bf16[6,4,2304]{2,1,0:T(4,128)(2,1)S(1)} %collective-permute-done.1), channel_id=1, source_target_pairs={{0,7},{1,0},{2,1},{3,2},{4,3},{5,4},{6,5},{7,6},{8,15},{9,8},{10,9... | collective-permute-start | bytes 331784 | tf_op jit(solution)/shard_map/ppermute | solution.py:27
  66.9 1.8 %collective-permute-done.5 = bf16[6,4,2304]{2,1,0:T(4,128)(2,1)S(1)} collective-permute-done((bf16[6,4,2304]{2,1,0:T(4,128)(2,1)S(1)}, bf16[6,4,2304]{2,1,0:T(4,128)(2,1)S(1)}, u32[]{:S(2)}, u32[]{:S(2)}) %collective-permute-start.5) | collective-permute-done | bytes 110624 | tf_op jit(solution)/shard_map/ppermute | solution.py:26
  68.7 5.6 %collective-permute-start.6 = (bf16[3,4,2304]{2,1,0:T(4,128)(2,1)S(1)}, bf16[3,4,2304]{2,1,0:T(4,128)(2,1)S(1)}, u32[]{:S(2)}, u32[]{:S(2)}) collective-permute-start(bf16[3,4,2304]{2,1,0:T(4,128)(2,1)S(1)} %slice.86), channel_id=1, source_target_pairs={{0,1},{1,2},{2,3},{3,4},{4,5},{5,6},{6,7},{7,0},{8,9},{9,10},{10,1... | collective-permute-start | bytes 165896 | tf_op jit(solution)/shard_map/ppermute | solution.py:22
  74.4 1.9 %collective-permute-start.7 = (bf16[3,4,2304]{2,1,0:T(4,128)(2,1)S(1)}, bf16[3,4,2304]{2,1,0:T(4,128)(2,1)S(1)}, u32[]{:S(2)}, u32[]{:S(2)}) collective-permute-start(bf16[3,4,2304]{2,1,0:T(4,128)(2,1)S(1)} %slice.87), channel_id=1, source_target_pairs={{0,7},{1,0},{2,1},{3,2},{4,3},{5,4},{6,5},{7,6},{8,15},{9,8},{10,9... | collective-permute-start | bytes 165896 | tf_op jit(solution)/shard_map/ppermute | solution.py:23
  76.9 0.2 copy.164
  77.1 0.2 copy.165
  77.3 0.2 copy.171
  77.5 0.2 copy.166
  77.7 0.2 copy.170
  77.8 0.2 copy.167
  78.0 0.2 copy.169
  78.2 3.5 %collective-permute-done.7 = bf16[3,4,2304]{2,1,0:T(4,128)(2,1)S(1)} collective-permute-done((bf16[3,4,2304]{2,1,0:T(4,128)(2,1)S(1)}, bf16[3,4,2304]{2,1,0:T(4,128)(2,1)S(1)}, u32[]{:S(2)}, u32[]{:S(2)}) %collective-permute-start.7) | collective-permute-done | bytes 55328 | tf_op jit(solution)/shard_map/ppermute | solution.py:23
  81.8 0.2 copy.168
  82.0 2.8 %stack.37 = bf16[8,6,4,2304]{3,0,2,1:T(8,128)(2,1)S(1)} concatenate(bf16[1,6,4,2304]{3,0,2,1:T(2,128)(2,1)S(1)} %copy.164, bf16[1,6,4,2304]{3,0,2,1:T(2,128)(2,1)S(1)} %copy.165, bf16[1,6,4,2304]{3,0,2,1:T(2,128)(2,1)S(1)} %copy.166, bf16[1,6,4,2304]{3,0,2,1:T(2,128)(2,1)S(1)} %copy.167, bf16[1,6,4,2304]{3,0,2,1:T(2,128)(2,1)S(1)} %copy.168, bf16[1,6,4,2304]{3,0,2,1:T(2,128)(2,1)S(1)} %copy.169, ...), dimensions={0} | concatenate | bytes 1769472 | tf_op jit(solution)/shard_map/stack | solution.py:78
  84.7 3.3 %collective-permute-start.9 = (bf16[8,6,4,2304]{3,0,2,1:T(8,128)(2,1)S(1)}, bf16[8,6,4,2304]{3,0,2,1:T(8,128)(2,1)}, u32[]{:S(2)}, u32[]{:S(2)}) collective-permute-start(bf16[8,6,4,2304]{3,0,2,1:T(8,128)(2,1)S(1)} %stack.37), channel_id=1, source_target_pairs={{0,8},{8,16},{16,24},{24,0},{1,9},{9,17},{17,25},{25,1},{2,10},{10... | collective-permute-start | bytes 2654216 | tf_op jit(solution)/shard_map/ppermute | solution.py:26
  88.0 2.6 %collective-permute-start.8 = (bf16[8,6,4,2304]{3,0,2,1:T(8,128)(2,1)S(1)}, bf16[8,6,4,2304]{3,0,2,1:T(8,128)(2,1)}, u32[]{:S(2)}, u32[]{:S(2)}) collective-permute-start(bf16[8,6,4,2304]{3,0,2,1:T(8,128)(2,1)S(1)} %stack.37), channel_id=1, source_target_pairs={{0,24},{8,0},{16,8},{24,16},{1,25},{9,1},{17,9},{25,17},{2,26},{10... | collective-permute-start | bytes 2654216 | tf_op jit(solution)/shard_map/ppermute | solution.py:27
  90.6 6.5 %copy.173 = bf16[1,1,3,5376,128]{3,4,2,1,0:T(8,128)(2,1)} copy(bf16[1,1,3,5376,128]{4,3,2,1,0:T(8,128)(2,1)} %param.10) | data formatting | bytes 8257536 | tf_op args[2]
  97.1 1.6 %slice.97 = bf16[3,2176,128]{1,2,0:T(8,128)(2,1)S(1)} slice(bf16[3,5376,128]{1,2,0:T(8,128)(2,1)} %bitcast.130), slice={[0:3], [3200:5376], [0:128]} | slice | bytes 3342336 | tf_op jit(solution)/shard_map/slice | solution.py:67
  98.9 0.7 fusion.7
  99.6 0.8 bitcast_dynamic-update-slice_fusion.6
  100.4 17.8 %collective-permute-done.9 = bf16[8,6,4,2304]{3,0,2,1:T(8,128)(2,1)} collective-permute-done((bf16[8,6,4,2304]{3,0,2,1:T(8,128)(2,1)S(1)}, bf16[8,6,4,2304]{3,0,2,1:T(8,128)(2,1)}, u32[]{:S(2)}, u32[]{:S(2)}) %collective-permute-start.9) | collective-permute-done | bytes 884768 | tf_op jit(solution)/shard_map/ppermute | solution.py:26
  118.2 1.3 slice.90
  119.5 3.3 %collective-permute-start.10 = (bf16[4,6,4,2304]{3,0,2,1:T(4,128)(2,1)S(1)}, bf16[4,6,4,2304]{3,0,2,1:T(4,128)(2,1)S(1)}, u32[]{:S(2)}, u32[]{:S(2)}) collective-permute-start(bf16[4,6,4,2304]{3,0,2,1:T(4,128)(2,1)S(1)} %slice.90), channel_id=1, source_target_pairs={{0,8},{8,16},{16,24},{24,0},{1,9},{9,17},{17,25},{25,1},{2,10},{10... | collective-permute-start | bytes 1327112 | tf_op jit(solution)/shard_map/ppermute | solution.py:22
  122.9 1.1 collective-permute-done.8
  124.0 1.5 slice.91
  125.5 2.9 %collective-permute-start.11 = (bf16[4,6,4,2304]{3,0,2,1:T(4,128)(2,1)S(1)}, bf16[4,6,4,2304]{3,0,2,1:T(4,128)(2,1)S(1)}, u32[]{:S(2)}, u32[]{:S(2)}) collective-permute-start(bf16[4,6,4,2304]{3,0,2,1:T(4,128)(2,1)S(1)} %slice.91), channel_id=1, source_target_pairs={{0,24},{8,0},{16,8},{24,16},{1,25},{9,1},{17,9},{25,17},{2,26},{10... | collective-permute-start | bytes 1327112 | tf_op jit(solution)/shard_map/ppermute | solution.py:23
  128.4 0.9 slice_reduce_fusion.1
  129.3 0.9 slice_reduce_fusion
  130.2 1.9 %fusion.5 = f32[8,6,4,3,128]{4,0,3,2,1:T(8,128)S(1)} fusion(bf16[3,2176,128]{1,2,0:T(8,128)(2,1)S(1)} %slice.97, bf16[8,6,4,2304]{3,0,2,1:T(8,128)(2,1)} %collective-permute-done.8), kind=kOutput, calls=%fused_computation.13 | convolution fusion | flops 339738624 | bytes 2850816 | tf_op jit(solution)/shard_map/dot_general | solution.py:72
  132.1 0.8 bitcast_dynamic-update-slice_fusion.4
  132.9 1.9 %fusion.1 = f32[8,6,4,3,128]{4,0,3,2,1:T(8,128)S(1)} fusion(bf16[3,2176,128]{1,2,0:T(8,128)(2,1)S(1)} %slice.97, bf16[8,6,4,2304]{3,0,2,1:T(8,128)(2,1)} %collective-permute-done.9), kind=kOutput, calls=%fused_computation.9 | convolution fusion | flops 339738624 | bytes 2850816 | tf_op jit(solution)/shard_map/dot_general | solution.py:72
  134.8 1.1 collective-permute-done.10
  135.9 3.4 %collective-permute-done.11 = bf16[4,6,4,2304]{3,0,2,1:T(4,128)(2,1)S(1)} collective-permute-done((bf16[4,6,4,2304]{3,0,2,1:T(4,128)(2,1)S(1)}, bf16[4,6,4,2304]{3,0,2,1:T(4,128)(2,1)S(1)}, u32[]{:S(2)}, u32[]{:S(2)}) %collective-permute-start.11) | collective-permute-done | bytes 442400 | tf_op jit(solution)/shard_map/ppermute | solution.py:23
  139.5 0.6 copy-done.3
  140.2 0.1 fusion.27
  140.4 0.2 copy.172
  140.7 0.6 gather_fusion.3
  141.3 2.0 %fusion.3 = f32[8,6,4,3,128]{4,0,3,2,1:T(8,128)S(1)} fusion(bf16[3,2176,128]{1,2,0:T(8,128)(2,1)S(1)} %slice.97, bf16[4,6,4,2304]{3,0,2,1:T(4,128)(2,1)} %copy-done.3, bf16[4,6,4,2304]{3,0,2,1:T(4,128)(2,1)} %copy-done.2), kind=kOutput, calls=%fused_computation.11 | convolution fusion | flops 341508096 | bytes 2850816 | tf_op jit(solution)/shard_map/dot_general | solution.py:72
  144.0 0.2 constant_dynamic-slice_fusion
  144.3 6.8 %fusion.11 = f32[6,3,4,8,4,128]{5,4,1,0,3,2:T(4,128)S(1)} fusion(bf16[4,8,6,4,3200,1]{4,3,5,2,1,0:T(4,128)(2,1)} %bitcast.141, bf16[3,5376,128]{1,2,0:T(8,128)(2,1)} %bitcast.131, s32[]{:T(128)S(6)} %select_n.102, f32[4,8,6,4,3,128]{5,3,4,2,1,0:T(4,128)S(1)} %constant_dynamic-slice_fusion), kind=kOutput, calls=%fused_computation.20 | convolution fusion | flops 1888026624 | bytes 9732100 | tf_op jit(solution)/shard_map/dot_general | solution.py:72
  151.1 0.3 copy.178
  151.4 0.6 gather_fusion.4
  152.1 1.2 fusion.18
  (47 shorter events, 1.5 us)
Async XLA Ops:
  6.5 1.5 copy-start
  9.2 12.6 %copy-start.4 = (s32[16,6]{0,1:T(8,128)S(1)}, s32[16,6]{0,1:T(8,128)}, u32[]{:S(2)}) copy-start(s32[16,6]{0,1:T(8,128)} %param.11) | copy-start | bytes 1156
  11.2 55.6 %copy-start.5 = (s32[1,1,18,2]{2,3,1,0:T(2,128)S(1)}, s32[1,1,18,2]{2,3,1,0:T(2,128)}, u32[]{:S(2)}) copy-start(s32[1,1,18,2]{2,3,1,0:T(2,128)} %param.12) | copy-start | bytes 436
  11.2 29.7 %all-to-all-start = ((bf16[16,4,5504]{2,1,0:T(4,128)(2,1)}), bf16[16,4,5504]{2,1,0:T(4,128)(2,1)S(1)}, u32[]{:S(2)}, u32[]{:S(2)}) async-start(bf16[16,4,5504]{2,1,0:T(4,128)(2,1)} %fusion.24), calls=%async_computation | async-start | bytes 1409024 | tf_op jit(solution)/shard_map/all_to_all | solution.py:51
  21.8 122.5 %all-gather.3.cloned.1.call-start = ((), (), s32[]{:S(2)}) async-start(), calls=%async_computation.1 | async-start | bytes 5068800 | tf_op jit(solution)/shard_map/all_gather | solution.py:75
  42.7 7.0 %collective-permute-start.3 = (bf16[6,4,2304]{2,1,0:T(4,128)(2,1)S(1)}, bf16[6,4,2304]{2,1,0:T(4,128)(2,1)S(1)}, u32[]{:S(2)}, u32[]{:S(2)}) collective-permute-start(bf16[6,4,2304]{2,1,0:T(4,128)(2,1)S(1)} %get-tuple-element.17), channel_id=1, source_target_pairs={{0,1},{1,2},{2,3},{3,4},{4,5},{5,6},{6,7},{7,0},{8,9},{9,10},{10,1... | collective-permute-start | bytes 331784 | tf_op jit(solution)/shard_map/ppermute | solution.py:26
  47.4 8.0 %collective-permute-start = (bf16[6,4,2304]{2,1,0:T(4,128)(2,1)S(1)}, bf16[6,4,2304]{2,1,0:T(4,128)(2,1)S(1)}, u32[]{:S(2)}, u32[]{:S(2)}) collective-permute-start(bf16[6,4,2304]{2,1,0:T(4,128)(2,1)S(1)} %get-tuple-element.17), channel_id=1, source_target_pairs={{0,7},{1,0},{2,1},{3,2},{4,3},{5,4},{6,5},{7,6},{8,15},{9,8},{10,9... | collective-permute-start | bytes 331784 | tf_op jit(solution)/shard_map/ppermute | solution.py:27
  49.7 9.6 %collective-permute-start.4 = (bf16[6,4,2304]{2,1,0:T(4,128)(2,1)S(1)}, bf16[6,4,2304]{2,1,0:T(4,128)(2,1)S(1)}, u32[]{:S(2)}, u32[]{:S(2)}) collective-permute-start(bf16[6,4,2304]{2,1,0:T(4,128)(2,1)S(1)} %collective-permute-done.3), channel_id=1, source_target_pairs={{0,1},{1,2},{2,3},{3,4},{4,5},{5,6},{6,7},{7,0},{8,9},{9,10},{10,1... | collective-permute-start | bytes 331784 | tf_op jit(solution)/shard_map/ppermute | solution.py:26
  55.4 9.5 %collective-permute-start.1 = (bf16[6,4,2304]{2,1,0:T(4,128)(2,1)S(1)}, bf16[6,4,2304]{2,1,0:T(4,128)(2,1)S(1)}, u32[]{:S(2)}, u32[]{:S(2)}) collective-permute-start(bf16[6,4,2304]{2,1,0:T(4,128)(2,1)S(1)} %collective-permute-done), channel_id=1, source_target_pairs={{0,7},{1,0},{2,1},{3,2},{4,3},{5,4},{6,5},{7,6},{8,15},{9,8},{10,9... | collective-permute-start | bytes 331784 | tf_op jit(solution)/shard_map/ppermute | solution.py:27
  59.3 9.4 %collective-permute-start.5 = (bf16[6,4,2304]{2,1,0:T(4,128)(2,1)S(1)}, bf16[6,4,2304]{2,1,0:T(4,128)(2,1)S(1)}, u32[]{:S(2)}, u32[]{:S(2)}) collective-permute-start(bf16[6,4,2304]{2,1,0:T(4,128)(2,1)S(1)} %collective-permute-done.4), channel_id=1, source_target_pairs={{0,1},{1,2},{2,3},{3,4},{4,5},{5,6},{6,7},{7,0},{8,9},{9,10},{10,1... | collective-permute-start | bytes 331784 | tf_op jit(solution)/shard_map/ppermute | solution.py:26
  64.9 9.4 %collective-permute-start.2 = (bf16[6,4,2304]{2,1,0:T(4,128)(2,1)S(1)}, bf16[6,4,2304]{2,1,0:T(4,128)(2,1)S(1)}, u32[]{:S(2)}, u32[]{:S(2)}) collective-permute-start(bf16[6,4,2304]{2,1,0:T(4,128)(2,1)S(1)} %collective-permute-done.1), channel_id=1, source_target_pairs={{0,7},{1,0},{2,1},{3,2},{4,3},{5,4},{6,5},{7,6},{8,15},{9,8},{10,9... | collective-permute-start | bytes 331784 | tf_op jit(solution)/shard_map/ppermute | solution.py:27
  68.7 9.5 %collective-permute-start.6 = (bf16[3,4,2304]{2,1,0:T(4,128)(2,1)S(1)}, bf16[3,4,2304]{2,1,0:T(4,128)(2,1)S(1)}, u32[]{:S(2)}, u32[]{:S(2)}) collective-permute-start(bf16[3,4,2304]{2,1,0:T(4,128)(2,1)S(1)} %slice.86), channel_id=1, source_target_pairs={{0,1},{1,2},{2,3},{3,4},{4,5},{5,6},{6,7},{7,0},{8,9},{9,10},{10,1... | collective-permute-start | bytes 165896 | tf_op jit(solution)/shard_map/ppermute | solution.py:22
  74.4 7.4 %collective-permute-start.7 = (bf16[3,4,2304]{2,1,0:T(4,128)(2,1)S(1)}, bf16[3,4,2304]{2,1,0:T(4,128)(2,1)S(1)}, u32[]{:S(2)}, u32[]{:S(2)}) collective-permute-start(bf16[3,4,2304]{2,1,0:T(4,128)(2,1)S(1)} %slice.87), channel_id=1, source_target_pairs={{0,7},{1,0},{2,1},{3,2},{4,3},{5,4},{6,5},{7,6},{8,15},{9,8},{10,9... | collective-permute-start | bytes 165896 | tf_op jit(solution)/shard_map/ppermute | solution.py:23
  84.7 33.5 %collective-permute-start.9 = (bf16[8,6,4,2304]{3,0,2,1:T(8,128)(2,1)S(1)}, bf16[8,6,4,2304]{3,0,2,1:T(8,128)(2,1)}, u32[]{:S(2)}, u32[]{:S(2)}) collective-permute-start(bf16[8,6,4,2304]{3,0,2,1:T(8,128)(2,1)S(1)} %stack.37), channel_id=1, source_target_pairs={{0,8},{8,16},{16,24},{24,0},{1,9},{9,17},{17,25},{25,1},{2,10},{10... | collective-permute-start | bytes 2654216 | tf_op jit(solution)/shard_map/ppermute | solution.py:26
  88.0 35.9 %collective-permute-start.8 = (bf16[8,6,4,2304]{3,0,2,1:T(8,128)(2,1)S(1)}, bf16[8,6,4,2304]{3,0,2,1:T(8,128)(2,1)}, u32[]{:S(2)}, u32[]{:S(2)}) collective-permute-start(bf16[8,6,4,2304]{3,0,2,1:T(8,128)(2,1)S(1)} %stack.37), channel_id=1, source_target_pairs={{0,24},{8,0},{16,8},{24,16},{1,25},{9,1},{17,9},{25,17},{2,26},{10... | collective-permute-start | bytes 2654216 | tf_op jit(solution)/shard_map/ppermute | solution.py:27
  119.5 16.4 %collective-permute-start.10 = (bf16[4,6,4,2304]{3,0,2,1:T(4,128)(2,1)S(1)}, bf16[4,6,4,2304]{3,0,2,1:T(4,128)(2,1)S(1)}, u32[]{:S(2)}, u32[]{:S(2)}) collective-permute-start(bf16[4,6,4,2304]{3,0,2,1:T(4,128)(2,1)S(1)} %slice.90), channel_id=1, source_target_pairs={{0,8},{8,16},{16,24},{24,0},{1,9},{9,17},{17,25},{25,1},{2,10},{10... | collective-permute-start | bytes 1327112 | tf_op jit(solution)/shard_map/ppermute | solution.py:22
  125.5 13.9 %collective-permute-start.11 = (bf16[4,6,4,2304]{3,0,2,1:T(4,128)(2,1)S(1)}, bf16[4,6,4,2304]{3,0,2,1:T(4,128)(2,1)S(1)}, u32[]{:S(2)}, u32[]{:S(2)}) collective-permute-start(bf16[4,6,4,2304]{3,0,2,1:T(4,128)(2,1)S(1)} %slice.91), channel_id=1, source_target_pairs={{0,24},{8,0},{16,8},{24,16},{1,25},{9,1},{17,9},{25,17},{2,26},{10... | collective-permute-start | bytes 1327112 | tf_op jit(solution)/shard_map/ppermute | solution.py:23
  135.9 3.5 %copy-start.2 = (bf16[4,6,4,2304]{3,0,2,1:T(4,128)(2,1)}, bf16[4,6,4,2304]{3,0,2,1:T(4,128)(2,1)S(1)}, u32[]{:S(2)}) copy-start(bf16[4,6,4,2304]{3,0,2,1:T(4,128)(2,1)S(1)} %collective-permute-done.10) | copy-start | bytes 1327108
  139.4 0.8 copy-start.3
  141.3 2.1 %copy-start.1 = (f32[8,8,6,4,3,128]{5,3,4,2,1,0:T(4,128)S(1)}, f32[8,8,6,4,3,128]{5,3,4,2,1,0:T(4,128)}, u32[]{:S(2)}) copy-start(f32[8,8,6,4,3,128]{5,3,4,2,1,0:T(4,128)} %bitcast_dynamic-update-slice_fusion.4) | copy-start | bytes 7077892
Sparse Core Ops, SparseCore 0:
  42.7 99.2 all-gather.2

commit v10 on v9

--- a/solution.py
+++ b/solution.py
@@ -72,8 +72,12 @@
         out = jnp.dot(flat, enc, preferred_element_type=jnp.float32)
         return out.reshape(-1, enc_count, tile_cols)
 
-    a_all = lax.all_gather(part_a, SHARD, axis=0, tiled=False)
-    prod_a = mm(a_all, enc_a).reshape(n_x, n_y, slots, rows_dev, enc_count, tile_cols)
+    cut = (split // 2) // LANES * LANES
+    a_lo = lax.all_gather(part_a[..., :cut], SHARD, axis=0, tiled=False)
+    prod_lo = lax.optimization_barrier(mm(a_lo, enc_a[:cut]))
+    a_hi = lax.all_gather(part_a[..., cut:], SHARD, axis=0, tiled=False)
+    prod_a = prod_lo + mm(a_hi, enc_a[cut:])
+    prod_a = prod_a.reshape(n_x, n_y, slots, rows_dev, enc_count, tile_cols)
 
     b_y = jnp.stack(ring_parts(part_b, "y", n_y), axis=0)
     b_parts = ring_parts(b_y, "x", n_x)

time: 161 us -> 231 us (1.43)
  the two profiles are of different devices: /device:TPU:26 before, /device:TPU:6 now
where the time goes in v10:
time: 231 us; the launch traced here: 229 us
  waiting for transfers between devices  98.8 us (43%)
  starting transfers between devices  51 us (22%)
  local copies, waits for them, and re-layouts  45.3 us (20%)
  between operations  14.5 us (6%)
  matrix products  13.9 us (6%)
  other arithmetic  5.04 us (2%)
    all_gather x1, waiting for transfers between devices, local(): a_hi = lax.all_gather(part_a[..., cut:], SHARD, axis=0, tiled=False)  44.7 us
    ppermute x4, waiting for transfers between devices, ring_parts(): left = lax.ppermute(left, axis, up)  24.2 us
    all_to_all x1, waiting for transfers between devices, local(): recv = lax.all_to_all(send, GRP, 0, 0, tiled=True)  18.7 us
    ppermute x4, starting transfers between devices, ring_parts(): right = lax.ppermute(right, axis, down)  17.2 us
    dot_general x6, matrix products, mm(): out = jnp.dot(flat, enc, preferred_element_type=jnp.float32)  13.9 us
    another operation x9, local copies, waits for them, and re-layouts, local(): b_y = jnp.stack(ring_parts(part_b, 'y', n_y), axis=0)  10.5 us
    all_to_all x1, starting transfers between devices, local(): recv = lax.all_to_all(send, GRP, 0, 0, tiled=True)  10.4 us
    reshape x2, local copies, waits for them, and re-layouts, mm(): flat = block.reshape(-1, block.shape[-1])  10.1 us
  transfers between devices with their start and end apart: 15, of which 7 were waited for; matrix products, arithmetic and copies ran while one was open for 20% of the time, Pallas kernels for 0%

profile of v10, /device:TPU:6, one launch (start us, length us, event | category | flops | bytes accessed | tf_op | source)
XLA Modules:
  0.0 228.7 jit_solution(15422019866978839716)
XLA Ops:
  6.5 0.8 fusion.42
  7.3 0.8 copy.141
  8.1 1.1 gather_fusion
  9.2 0.6 gather_fusion.1
  10.0 1.2 fusion.36
  11.2 10.4 %all-to-all-start = ((bf16[16,4,5504]{2,1,0:T(4,128)(2,1)}), bf16[16,4,5504]{2,1,0:T(4,128)(2,1)S(1)}, u32[]{:S(2)}, u32[]{:S(2)}) async-start(bf16[16,4,5504]{2,1,0:T(4,128)(2,1)} %fusion.36), calls=%async_computation | async-start | bytes 1409024 | tf_op jit(solution)/shard_map/all_to_all | solution.py:51
  21.7 0.2 dynamic-slice_reduce_fusion
  21.9 0.2 compare_reduce_fusion
  22.1 18.7 %all-to-all-done = bf16[16,4,5504]{2,1,0:T(4,128)(2,1)S(1)} async-done(((bf16[16,4,5504]{2,1,0:T(4,128)(2,1)}), bf16[16,4,5504]{2,1,0:T(4,128)(2,1)S(1)}, u32[]{:S(2)}, u32[]{:S(2)}) %all-to-all-start) | async-done | bytes 704544 | tf_op jit(solution)/shard_map/all_to_all | solution.py:51
  40.8 0.8 gather_fusion.2
  41.6 0.2 broadcast_select_fusion
  41.7 0.6 slice.118
  42.5 3.5 %collective-permute-start.3 = (bf16[6,4,2304]{2,1,0:T(4,128)(2,1)S(1)}, bf16[6,4,2304]{2,1,0:T(4,128)(2,1)S(1)}, u32[]{:S(2)}, u32[]{:S(2)}) collective-permute-start(bf16[6,4,2304]{2,1,0:T(4,128)(2,1)S(1)} %get-tuple-element.17), channel_id=1, source_target_pairs={{0,1},{1,2},{2,3},{3,4},{4,5},{5,6},{6,7},{7,0},{8,9},{9,10},{10,1... | collective-permute-start | bytes 331784 | tf_op jit(solution)/shard_map/ppermute | solution.py:26
  46.0 3.8 %collective-permute-start = (bf16[6,4,2304]{2,1,0:T(4,128)(2,1)S(1)}, bf16[6,4,2304]{2,1,0:T(4,128)(2,1)S(1)}, u32[]{:S(2)}, u32[]{:S(2)}) collective-permute-start(bf16[6,4,2304]{2,1,0:T(4,128)(2,1)S(1)} %get-tuple-element.17), channel_id=1, source_target_pairs={{0,7},{1,0},{2,1},{3,2},{4,3},{5,4},{6,5},{7,6},{8,15},{9,8},{10,9... | collective-permute-start | bytes 331784 | tf_op jit(solution)/shard_map/ppermute | solution.py:27
  49.9 0.8 collective-permute-done.3
  50.6 2.0 collective-permute-start.4
  52.7 0.2 collective-permute-done
  52.9 4.8 %collective-permute-start.1 = (bf16[6,4,2304]{2,1,0:T(4,128)(2,1)S(1)}, bf16[6,4,2304]{2,1,0:T(4,128)(2,1)S(1)}, u32[]{:S(2)}, u32[]{:S(2)}) collective-permute-start(bf16[6,4,2304]{2,1,0:T(4,128)(2,1)S(1)} %collective-permute-done), channel_id=1, source_target_pairs={{0,7},{1,0},{2,1},{3,2},{4,3},{5,4},{6,5},{7,6},{8,15},{9,8},{10,9... | collective-permute-start | bytes 331784 | tf_op jit(solution)/shard_map/ppermute | solution.py:27
  57.7 6.4 %copy.153 = bf16[1,1,3,5376,128]{3,4,2,1,0:T(8,128)(2,1)} copy(bf16[1,1,3,5376,128]{4,3,2,1,0:T(8,128)(2,1)} %param.10) | data formatting | bytes 8257536 | tf_op args[2]
  64.1 1.9 collective-permute-start.5
  66.1 5.1 %collective-permute-start.2 = (bf16[6,4,2304]{2,1,0:T(4,128)(2,1)S(1)}, bf16[6,4,2304]{2,1,0:T(4,128)(2,1)S(1)}, u32[]{:S(2)}, u32[]{:S(2)}) collective-permute-start(bf16[6,4,2304]{2,1,0:T(4,128)(2,1)S(1)} %collective-permute-done.1), channel_id=1, source_target_pairs={{0,7},{1,0},{2,1},{3,2},{4,3},{5,4},{6,5},{7,6},{8,15},{9,8},{10,9... | collective-permute-start | bytes 331784 | tf_op jit(solution)/shard_map/ppermute | solution.py:27
  71.2 3.3 %slice_bitcast_fusion = bf16[3200,3,128]{0,2,1:T(8,128)(2,1)} fusion(bf16[3,5376,128]{1,2,0:T(8,128)(2,1)} %bitcast.146), kind=kLoop, calls=%fused_computation.5 | loop fusion | bytes 4915200 | tf_op jit(solution)/shard_map/transpose | solution.py:66
  75.2 0.7 slice.121
  75.9 1.9 collective-permute-start.6
  77.9 5.1 %collective-permute-start.7 = (bf16[3,4,2304]{2,1,0:T(4,128)(2,1)S(1)}, bf16[3,4,2304]{2,1,0:T(4,128)(2,1)S(1)}, u32[]{:S(2)}, u32[]{:S(2)}) collective-permute-start(bf16[3,4,2304]{2,1,0:T(4,128)(2,1)S(1)} %slice.110), channel_id=1, source_target_pairs={{0,7},{1,0},{2,1},{3,2},{4,3},{5,4},{6,5},{7,6},{8,15},{9,8},{10,9... | collective-permute-start | bytes 165896 | tf_op jit(solution)/shard_map/ppermute | solution.py:23
  83.1 1.6 slice.123
  84.7 0.2 copy.144
  85.0 0.9 copy.151
  85.9 0.9 copy.146
  86.7 0.9 copy.150
  87.6 0.9 copy.147
  88.5 0.9 copy.149
  89.4 0.9 copy.148
  90.3 5.0 %stack.37 = bf16[8,6,4,2304]{3,0,2,1:T(8,128)(2,1)S(1)} concatenate(bf16[1,6,4,2304]{3,0,2,1:T(2,128)(2,1)S(1)} %copy.144, bf16[1,6,4,2304]{3,0,2,1:T(2,128)(2,1)S(1)} %copy.145, bf16[1,6,4,2304]{3,0,2,1:T(2,128)(2,1)} %copy.146, bf16[1,6,4,2304]{3,0,2,1:T(2,128)(2,1)} %copy.147, bf16[1,6,4,2304]{3,0,2,1:T(2,128)(2,1)} %copy.148, bf16[1,6,4,2304]{3,0,2,1:T(2,128)(2,1)} %copy.149, ...), dimensions={0} | concatenate | bytes 1769472 | tf_op jit(solution)/shard_map/stack | solution.py:82
  95.3 2.4 %collective-permute-start.9 = (bf16[8,6,4,2304]{3,0,2,1:T(8,128)(2,1)S(1)}, bf16[8,6,4,2304]{3,0,2,1:T(8,128)(2,1)S(1)}, u32[]{:S(2)}, u32[]{:S(2)}) collective-permute-start(bf16[8,6,4,2304]{3,0,2,1:T(8,128)(2,1)S(1)} %stack.37), channel_id=1, source_target_pairs={{0,8},{8,16},{16,24},{24,0},{1,9},{9,17},{17,25},{25,1},{2,10},{10... | collective-permute-start | bytes 2654216 | tf_op jit(solution)/shard_map/ppermute | solution.py:26
  97.6 3.5 %collective-permute-start.8 = (bf16[8,6,4,2304]{3,0,2,1:T(8,128)(2,1)S(1)}, bf16[8,6,4,2304]{3,0,2,1:T(8,128)(2,1)S(1)}, u32[]{:S(2)}, u32[]{:S(2)}) collective-permute-start(bf16[8,6,4,2304]{3,0,2,1:T(8,128)(2,1)S(1)} %stack.37), channel_id=1, source_target_pairs={{0,24},{8,0},{16,8},{24,16},{1,25},{9,1},{17,9},{25,17},{2,26},{10... | collective-permute-start | bytes 2654216 | tf_op jit(solution)/shard_map/ppermute | solution.py:27
  101.3 1.4 constant_dynamic-update-slice_fusion.15
  102.7 23.4 %collective-permute-done.9 = bf16[8,6,4,2304]{3,0,2,1:T(8,128)(2,1)S(1)} collective-permute-done((bf16[8,6,4,2304]{3,0,2,1:T(8,128)(2,1)S(1)}, bf16[8,6,4,2304]{3,0,2,1:T(8,128)(2,1)S(1)}, u32[]{:S(2)}, u32[]{:S(2)}) %collective-permute-start.9) | collective-permute-done | bytes 884768 | tf_op jit(solution)/shard_map/ppermute | solution.py:26
  126.3 4.3 %collective-permute-start.10 = (bf16[4,6,4,2304]{3,0,2,1:T(4,128)(2,1)S(1)}, bf16[4,6,4,2304]{3,0,2,1:T(4,128)(2,1)S(1)}, u32[]{:S(2)}, u32[]{:S(2)}) collective-permute-start(bf16[4,6,4,2304]{3,0,2,1:T(4,128)(2,1)S(1)} %slice.113), channel_id=1, source_target_pairs={{0,8},{8,16},{16,24},{24,0},{1,9},{9,17},{17,25},{25,1},{2,10},{10... | collective-permute-start | bytes 1327112 | tf_op jit(solution)/shard_map/ppermute | solution.py:22
  130.6 0.2 slice.114
  130.8 2.1 collective-permute-start.11
  133.2 1.4 constant_dynamic-update-slice_fusion.14
  134.6 5.3 %collective-permute-done.10 = bf16[4,6,4,2304]{3,0,2,1:T(4,128)(2,1)S(1)} collective-permute-done((bf16[4,6,4,2304]{3,0,2,1:T(4,128)(2,1)S(1)}, bf16[4,6,4,2304]{3,0,2,1:T(4,128)(2,1)S(1)}, u32[]{:S(2)}, u32[]{:S(2)}) %collective-permute-start.10) | collective-permute-done | bytes 442400 | tf_op jit(solution)/shard_map/ppermute | solution.py:22
  140.0 5.6 %collective-permute-done.11 = bf16[4,6,4,2304]{3,0,2,1:T(4,128)(2,1)S(1)} collective-permute-done((bf16[4,6,4,2304]{3,0,2,1:T(4,128)(2,1)S(1)}, bf16[4,6,4,2304]{3,0,2,1:T(4,128)(2,1)S(1)}, u32[]{:S(2)}, u32[]{:S(2)}) %collective-permute-start.11) | collective-permute-done | bytes 442400 | tf_op jit(solution)/shard_map/ppermute | solution.py:23
  145.8 0.5 copy-done.4
  146.3 0.7 fusion.39
  147.1 1.0 copy.152
  148.2 0.6 gather_fusion.3
  148.8 2.6 %constant_dynamic-update-slice_fusion.13 = (f32[8,8,6,4,3,128]{5,1,4,3,2,0:T(8,128)}, f32[1,8,6,4,3,128]{5,1,4,3,2,0:T(8,128)S(1)}) fusion(f32[8,8,6,4,3,128]{5,1,4,3,2,0:T(8,128)} %get-tuple-element.23, bf16[3,2176,128]{1,2,0:T(8,128)(2,1)S(1)} %slice.123, bf16[4,6,4,2304]{3,0,2,1:T(4,128)(2,1)} %copy-done.4, bf16[4,6,4,2304]{3,0,2,1:T(4,128)(2,1)} %copy-done.3), kind=kOutput, calls=%fused_computation.64 | convolution fusion | flops 341508096 | bytes 3145728 | tf_op jit(solution)/shard_map/dot_general | solution.py:72
  151.4 1.4 constant_dynamic-update-slice_fusion.12
  152.9 0.7 constant_dynamic-update-slice_fusion.11
  153.6 0.7 constant_dynamic-update-slice_fusion.10
  154.3 0.7 constant_dynamic-update-slice_fusion.9
  155.1 0.7 constant_dynamic-update-slice_fusion.8
  155.8 1.3 constant_dynamic-slice_fusion
  157.2 4.9 %reshape.278 = bf16[768,1536,1]{1,0,2:T(8,128)(2,1)} reshape(bf16[192,4,1536]{2,1,0:T(4,128)(2,1)} %all-gather.5.cloned.1.call-done) | data formatting | bytes 4718592 | tf_op jit(solution)/shard_map/reshape | solution.py:71
  162.1 3.4 %fusion.16 = f32[768,3,128]{2,0,1:T(8,128)S(1)} fusion(bf16[768,1536,1]{1,0,2:T(8,128)(2,1)} %reshape.278, bf16[3200,3,128]{0,2,1:T(8,128)(2,1)} %slice_bitcast_fusion), kind=kOutput, calls=%fused_computation.28 | convolution fusion | flops 905969664 | bytes 4718592 | tf_op jit(solution)/shard_map/dot_general | solution.py:72
  165.5 44.7 %all-gather.7.cloned.1.call-done = bf16[192,4,1664]{2,1,0:T(4,128)(2,1)} async-done(((bf16[6,4,1664]{2,1,0:T(4,128)(2,1)}), bf16[192,4,1664]{2,1,0:T(4,128)(2,1)}) %all-gather.7.cloned.1.call-update) | async-done | bytes 2555920 | tf_op jit(solution)/shard_map/all_gather | solution.py:78
  210.2 5.2 %reshape.279 = bf16[768,1664,1]{1,0,2:T(8,128)(2,1)} reshape(bf16[192,4,1664]{2,1,0:T(4,128)(2,1)} %all-gather.7.cloned.1.call-done) | data formatting | bytes 5111808 | tf_op jit(solution)/shard_map/reshape | solution.py:71
  215.4 3.6 %convolution_add_fusion = f32[768,3,128]{2,0,1:T(8,128)S(1)} fusion(f32[768,3,128]{2,0,1:T(8,128)S(1)} %fusion.16, bf16[768,1664,1]{1,0,2:T(8,128)(2,1)} %reshape.279, bf16[3200,3,128]{0,2,1:T(8,128)(2,1)} %slice_bitcast_fusion), kind=kOutput, calls=%fused_computation.18 | convolution fusion | flops 981762048 | bytes 6193152 | tf_op jit(solution)/shard_map/dot_general | solution.py:72
  219.1 0.5 fusion.15
  219.6 0.4 copy.155
  220.0 0.6 gather_fusion.4
  220.6 1.2 fusion.18
  (54 shorter events, 1.6 us)
Async XLA Ops:
  6.5 1.5 copy-start
  9.2 12.5 %copy-start.5 = (s32[16,6]{0,1:T(8,128)S(1)}, s32[16,6]{0,1:T(8,128)}, u32[]{:S(2)}) copy-start(s32[16,6]{0,1:T(8,128)} %param.11) | copy-start | bytes 1156
  11.2 29.6 %all-to-all-start = ((bf16[16,4,5504]{2,1,0:T(4,128)(2,1)}), bf16[16,4,5504]{2,1,0:T(4,128)(2,1)S(1)}, u32[]{:S(2)}, u32[]{:S(2)}) async-start(bf16[16,4,5504]{2,1,0:T(4,128)(2,1)} %fusion.36), calls=%async_computation | async-start | bytes 1409024 | tf_op jit(solution)/shard_map/all_to_all | solution.py:51
  21.6 135.5 %all-gather.5.cloned.1.call-start = ((), (), s32[]{:S(2)}) async-start(), calls=%async_computation.1 | async-start | bytes 2433024 | tf_op jit(solution)/shard_map/all_gather | solution.py:76
  42.4 167.8 %all-gather.7.cloned.1.call-start = ((), (), s32[]{:S(2)}) async-start(), calls=%async_computation.2 | async-start | bytes 2635776 | tf_op jit(solution)/shard_map/all_gather | solution.py:78
  42.5 8.1 %collective-permute-start.3 = (bf16[6,4,2304]{2,1,0:T(4,128)(2,1)S(1)}, bf16[6,4,2304]{2,1,0:T(4,128)(2,1)S(1)}, u32[]{:S(2)}, u32[]{:S(2)}) collective-permute-start(bf16[6,4,2304]{2,1,0:T(4,128)(2,1)S(1)} %get-tuple-element.17), channel_id=1, source_target_pairs={{0,1},{1,2},{2,3},{3,4},{4,5},{5,6},{6,7},{7,0},{8,9},{9,10},{10,1... | collective-permute-start | bytes 331784 | tf_op jit(solution)/shard_map/ppermute | solution.py:26
  46.0 6.8 %collective-permute-start = (bf16[6,4,2304]{2,1,0:T(4,128)(2,1)S(1)}, bf16[6,4,2304]{2,1,0:T(4,128)(2,1)S(1)}, u32[]{:S(2)}, u32[]{:S(2)}) collective-permute-start(bf16[6,4,2304]{2,1,0:T(4,128)(2,1)S(1)} %get-tuple-element.17), channel_id=1, source_target_pairs={{0,7},{1,0},{2,1},{3,2},{4,3},{5,4},{6,5},{7,6},{8,15},{9,8},{10,9... | collective-permute-start | bytes 331784 | tf_op jit(solution)/shard_map/ppermute | solution.py:27
  50.6 13.5 %collective-permute-start.4 = (bf16[6,4,2304]{2,1,0:T(4,128)(2,1)S(1)}, bf16[6,4,2304]{2,1,0:T(4,128)(2,1)S(1)}, u32[]{:S(2)}, u32[]{:S(2)}) collective-permute-start(bf16[6,4,2304]{2,1,0:T(4,128)(2,1)S(1)} %collective-permute-done.3), channel_id=1, source_target_pairs={{0,1},{1,2},{2,3},{3,4},{4,5},{5,6},{6,7},{7,0},{8,9},{9,10},{10,1... | collective-permute-start | bytes 331784 | tf_op jit(solution)/shard_map/ppermute | solution.py:26
  52.9 13.2 %collective-permute-start.1 = (bf16[6,4,2304]{2,1,0:T(4,128)(2,1)S(1)}, bf16[6,4,2304]{2,1,0:T(4,128)(2,1)S(1)}, u32[]{:S(2)}, u32[]{:S(2)}) collective-permute-start(bf16[6,4,2304]{2,1,0:T(4,128)(2,1)S(1)} %collective-permute-done), channel_id=1, source_target_pairs={{0,7},{1,0},{2,1},{3,2},{4,3},{5,4},{6,5},{7,6},{8,15},{9,8},{10,9... | collective-permute-start | bytes 331784 | tf_op jit(solution)/shard_map/ppermute | solution.py:27
  64.1 11.8 %collective-permute-start.5 = (bf16[6,4,2304]{2,1,0:T(4,128)(2,1)S(1)}, bf16[6,4,2304]{2,1,0:T(4,128)(2,1)S(1)}, u32[]{:S(2)}, u32[]{:S(2)}) collective-permute-start(bf16[6,4,2304]{2,1,0:T(4,128)(2,1)S(1)} %collective-permute-done.4), channel_id=1, source_target_pairs={{0,1},{1,2},{2,3},{3,4},{4,5},{5,6},{6,7},{7,0},{8,9},{9,10},{10,1... | collective-permute-start | bytes 331784 | tf_op jit(solution)/shard_map/ppermute | solution.py:26
  66.1 11.8 %collective-permute-start.2 = (bf16[6,4,2304]{2,1,0:T(4,128)(2,1)S(1)}, bf16[6,4,2304]{2,1,0:T(4,128)(2,1)S(1)}, u32[]{:S(2)}, u32[]{:S(2)}) collective-permute-start(bf16[6,4,2304]{2,1,0:T(4,128)(2,1)S(1)} %collective-permute-done.1), channel_id=1, source_target_pairs={{0,7},{1,0},{2,1},{3,2},{4,3},{5,4},{6,5},{7,6},{8,15},{9,8},{10,9... | collective-permute-start | bytes 331784 | tf_op jit(solution)/shard_map/ppermute | solution.py:27
  75.9 13.4 %collective-permute-start.6 = (bf16[3,4,2304]{2,1,0:T(4,128)(2,1)S(1)}, bf16[3,4,2304]{2,1,0:T(4,128)(2,1)S(1)}, u32[]{:S(2)}, u32[]{:S(2)}) collective-permute-start(bf16[3,4,2304]{2,1,0:T(4,128)(2,1)S(1)} %slice.109), channel_id=1, source_target_pairs={{0,1},{1,2},{2,3},{3,4},{4,5},{5,6},{6,7},{7,0},{8,9},{9,10},{10,1... | collective-permute-start | bytes 165896 | tf_op jit(solution)/shard_map/ppermute | solution.py:22
  77.9 11.4 %collective-permute-start.7 = (bf16[3,4,2304]{2,1,0:T(4,128)(2,1)S(1)}, bf16[3,4,2304]{2,1,0:T(4,128)(2,1)S(1)}, u32[]{:S(2)}, u32[]{:S(2)}) collective-permute-start(bf16[3,4,2304]{2,1,0:T(4,128)(2,1)S(1)} %slice.110), channel_id=1, source_target_pairs={{0,7},{1,0},{2,1},{3,2},{4,3},{5,4},{6,5},{7,6},{8,15},{9,8},{10,9... | collective-permute-start | bytes 165896 | tf_op jit(solution)/shard_map/ppermute | solution.py:23
  88.5 12.7 %copy-start.6 = (s32[1,1,18,2]{2,3,1,0:T(2,128)S(1)}, s32[1,1,18,2]{2,3,1,0:T(2,128)}, u32[]{:S(2)}) copy-start(s32[1,1,18,2]{2,3,1,0:T(2,128)} %param.12) | copy-start | bytes 436
  95.3 30.9 %collective-permute-start.9 = (bf16[8,6,4,2304]{3,0,2,1:T(8,128)(2,1)S(1)}, bf16[8,6,4,2304]{3,0,2,1:T(8,128)(2,1)S(1)}, u32[]{:S(2)}, u32[]{:S(2)}) collective-permute-start(bf16[8,6,4,2304]{3,0,2,1:T(8,128)(2,1)S(1)} %stack.37), channel_id=1, source_target_pairs={{0,8},{8,16},{16,24},{24,0},{1,9},{9,17},{17,25},{25,1},{2,10},{10... | collective-permute-start | bytes 2654216 | tf_op jit(solution)/shard_map/ppermute | solution.py:26
  97.6 32.9 %collective-permute-start.8 = (bf16[8,6,4,2304]{3,0,2,1:T(8,128)(2,1)S(1)}, bf16[8,6,4,2304]{3,0,2,1:T(8,128)(2,1)S(1)}, u32[]{:S(2)}, u32[]{:S(2)}) collective-permute-start(bf16[8,6,4,2304]{3,0,2,1:T(8,128)(2,1)S(1)} %stack.37), channel_id=1, source_target_pairs={{0,24},{8,0},{16,8},{24,16},{1,25},{9,1},{17,9},{25,17},{2,26},{10... | collective-permute-start | bytes 2654216 | tf_op jit(solution)/shard_map/ppermute | solution.py:27
  126.1 8.5 %copy-start.1 = (bf16[8,6,4,2304]{3,0,2,1:T(8,128)(2,1)}, bf16[8,6,4,2304]{3,0,2,1:T(8,128)(2,1)S(1)}, u32[]{:S(2)}) copy-start(bf16[8,6,4,2304]{3,0,2,1:T(8,128)(2,1)S(1)} %collective-permute-done.9) | copy-start | bytes 2654212
  126.3 13.7 %collective-permute-start.10 = (bf16[4,6,4,2304]{3,0,2,1:T(4,128)(2,1)S(1)}, bf16[4,6,4,2304]{3,0,2,1:T(4,128)(2,1)S(1)}, u32[]{:S(2)}, u32[]{:S(2)}) collective-permute-start(bf16[4,6,4,2304]{3,0,2,1:T(4,128)(2,1)S(1)} %slice.113), channel_id=1, source_target_pairs={{0,8},{8,16},{16,24},{24,0},{1,9},{9,17},{17,25},{25,1},{2,10},{10... | collective-permute-start | bytes 1327112 | tf_op jit(solution)/shard_map/ppermute | solution.py:22
  130.8 14.8 %collective-permute-start.11 = (bf16[4,6,4,2304]{3,0,2,1:T(4,128)(2,1)S(1)}, bf16[4,6,4,2304]{3,0,2,1:T(4,128)(2,1)S(1)}, u32[]{:S(2)}, u32[]{:S(2)}) collective-permute-start(bf16[4,6,4,2304]{3,0,2,1:T(4,128)(2,1)S(1)} %slice.114), channel_id=1, source_target_pairs={{0,24},{8,0},{16,8},{24,16},{1,25},{9,1},{17,9},{25,17},{2,26},{10... | collective-permute-start | bytes 1327112 | tf_op jit(solution)/shard_map/ppermute | solution.py:23
  140.0 5.9 %copy-start.3 = (bf16[4,6,4,2304]{3,0,2,1:T(4,128)(2,1)}, bf16[4,6,4,2304]{3,0,2,1:T(4,128)(2,1)S(1)}, u32[]{:S(2)}) copy-start(bf16[4,6,4,2304]{3,0,2,1:T(4,128)(2,1)S(1)} %collective-permute-done.10) | copy-start | bytes 1327108
  145.6 0.8 copy-start.4
  147.1 4.3 %copy-start.2 = (bf16[8,6,4,2304]{3,0,2,1:T(8,128)(2,1)S(1)}, bf16[8,6,4,2304]{3,0,2,1:T(8,128)(2,1)}, u32[]{:S(2)}) copy-start(bf16[8,6,4,2304]{3,0,2,1:T(8,128)(2,1)} %copy-done.1) | copy-start | bytes 2654212
Sparse Core Ops, SparseCore 0:
  42.5 83.3 all-gather.4
  129.1 81.0 all-gather.6

commit v11 on v9

--- a/solution.py
+++ b/solution.py
@@ -57,7 +57,7 @@
     slot_rows = jnp.where(my_valid[:, None, None], slot_rows, jnp.zeros((), slot_rows.dtype))
     slots, rows_dev, _ = slot_rows.shape
 
-    split = (ext_width * 3 // 5) // LANES * LANES
+    split = (ext_width * 3 // 5 + LANES - 1) // LANES * LANES
     part_a = slot_rows[..., :split]
     part_b = slot_rows[..., split:]
 

time: 161 us -> 161 us (level)
  the two profiles are of different devices: /device:TPU:26 before, /device:TPU:30 now
where the time goes in v11:
time: 161 us; the launch traced here: 160 us
  starting transfers between devices  51.2 us (32%)
  waiting for transfers between devices  50.6 us (31%)
  local copies, waits for them, and re-layouts  26.3 us (16%)
  between operations  14.6 us (9%)
  matrix products  13.6 us (8%)
  other arithmetic  3.89 us (2%)
    ppermute x4, waiting for transfers between devices, ring_parts(): left = lax.ppermute(left, axis, up)  19 us
    all_to_all x1, waiting for transfers between devices, local(): recv = lax.all_to_all(send, GRP, 0, 0, tiled=True)  18.7 us
    ppermute x4, starting transfers between devices, ring_parts(): left = lax.ppermute(left, axis, up)  18.4 us
    dot_general x5, matrix products, mm(): out = jnp.dot(flat, enc, preferred_element_type=jnp.float32)  13.6 us
    all_to_all x1, starting transfers between devices, local(): recv = lax.all_to_all(send, GRP, 0, 0, tiled=True)  10.6 us
    unnamed x27, local copies, waits for them, and re-layouts  10.3 us
    ppermute x2, starting transfers between devices, ring_parts(): got_left = lax.ppermute(left[:half], axis, up)  9.21 us
    ppermute x4, starting transfers between devices, ring_parts(): right = lax.ppermute(right, axis, down)  8.96 us
  transfers between devices with their start and end apart: 14, of which 11 were waited for; matrix products, arithmetic and copies ran while one was open for 17% of the time, Pallas kernels for 0%

profile of v11, /device:TPU:30, one launch (start us, length us, event | category | flops | bytes accessed | tf_op | source)
XLA Modules:
  0.0 160.2 jit_solution(7287781554922117536)
XLA Ops:
  6.5 0.8 fusion.30
  7.3 0.8 copy.161
  8.1 1.1 gather_fusion
  9.2 0.6 gather_fusion.1
  9.9 0.1 copy.186
  10.0 1.2 fusion.24
  11.2 10.6 %all-to-all-start = ((bf16[16,4,5504]{2,1,0:T(4,128)(2,1)}), bf16[16,4,5504]{2,1,0:T(4,128)(2,1)S(1)}, u32[]{:S(2)}, u32[]{:S(2)}) async-start(bf16[16,4,5504]{2,1,0:T(4,128)(2,1)} %fusion.24), calls=%async_computation | async-start | bytes 1409024 | tf_op jit(solution)/shard_map/all_to_all | solution.py:51
  21.8 0.2 dynamic-slice_reduce_fusion
  22.0 0.2 compare_reduce_fusion
  22.2 18.7 %all-to-all-done = bf16[16,4,5504]{2,1,0:T(4,128)(2,1)S(1)} async-done(((bf16[16,4,5504]{2,1,0:T(4,128)(2,1)}), bf16[16,4,5504]{2,1,0:T(4,128)(2,1)S(1)}, u32[]{:S(2)}, u32[]{:S(2)}) %all-to-all-start) | async-done | bytes 704544 | tf_op jit(solution)/shard_map/all_to_all | solution.py:51
  40.9 0.8 gather_fusion.2
  41.7 0.2 broadcast_select_fusion
  41.9 0.7 slice.95
  42.7 4.7 %collective-permute-start.3 = (bf16[6,4,2176]{2,1,0:T(4,128)(2,1)S(1)}, bf16[6,4,2176]{2,1,0:T(4,128)(2,1)S(1)}, u32[]{:S(2)}, u32[]{:S(2)}) collective-permute-start(bf16[6,4,2176]{2,1,0:T(4,128)(2,1)S(1)} %get-tuple-element.17), channel_id=1, source_target_pairs={{0,1},{1,2},{2,3},{3,4},{4,5},{5,6},{6,7},{7,0},{8,9},{9,10},{10,1... | collective-permute-start | bytes 313352 | tf_op jit(solution)/shard_map/ppermute | solution.py:26
  47.4 1.9 %collective-permute-start = (bf16[6,4,2176]{2,1,0:T(4,128)(2,1)S(1)}, bf16[6,4,2176]{2,1,0:T(4,128)(2,1)S(1)}, u32[]{:S(2)}, u32[]{:S(2)}) collective-permute-start(bf16[6,4,2176]{2,1,0:T(4,128)(2,1)S(1)} %get-tuple-element.17), channel_id=1, source_target_pairs={{0,7},{1,0},{2,1},{3,2},{4,3},{5,4},{6,5},{7,6},{8,15},{9,8},{10,9... | collective-permute-start | bytes 313352 | tf_op jit(solution)/shard_map/ppermute | solution.py:27
  49.3 0.3 collective-permute-done.3
  49.6 5.5 %collective-permute-start.4 = (bf16[6,4,2176]{2,1,0:T(4,128)(2,1)S(1)}, bf16[6,4,2176]{2,1,0:T(4,128)(2,1)S(1)}, u32[]{:S(2)}, u32[]{:S(2)}) collective-permute-start(bf16[6,4,2176]{2,1,0:T(4,128)(2,1)S(1)} %collective-permute-done.3), channel_id=1, source_target_pairs={{0,1},{1,2},{2,3},{3,4},{4,5},{5,6},{6,7},{7,0},{8,9},{9,10},{10,1... | collective-permute-start | bytes 313352 | tf_op jit(solution)/shard_map/ppermute | solution.py:26
  55.3 1.9 %collective-permute-start.1 = (bf16[6,4,2176]{2,1,0:T(4,128)(2,1)S(1)}, bf16[6,4,2176]{2,1,0:T(4,128)(2,1)S(1)}, u32[]{:S(2)}, u32[]{:S(2)}) collective-permute-start(bf16[6,4,2176]{2,1,0:T(4,128)(2,1)S(1)} %collective-permute-done), channel_id=1, source_target_pairs={{0,7},{1,0},{2,1},{3,2},{4,3},{5,4},{6,5},{7,6},{8,15},{9,8},{10,9... | collective-permute-start | bytes 313352 | tf_op jit(solution)/shard_map/ppermute | solution.py:27
  57.2 1.8 %collective-permute-done.4 = bf16[6,4,2176]{2,1,0:T(4,128)(2,1)S(1)} collective-permute-done((bf16[6,4,2176]{2,1,0:T(4,128)(2,1)S(1)}, bf16[6,4,2176]{2,1,0:T(4,128)(2,1)S(1)}, u32[]{:S(2)}, u32[]{:S(2)}) %collective-permute-start.4) | collective-permute-done | bytes 104480 | tf_op jit(solution)/shard_map/ppermute | solution.py:26
  59.0 5.6 %collective-permute-start.5 = (bf16[6,4,2176]{2,1,0:T(4,128)(2,1)S(1)}, bf16[6,4,2176]{2,1,0:T(4,128)(2,1)S(1)}, u32[]{:S(2)}, u32[]{:S(2)}) collective-permute-start(bf16[6,4,2176]{2,1,0:T(4,128)(2,1)S(1)} %collective-permute-done.4), channel_id=1, source_target_pairs={{0,1},{1,2},{2,3},{3,4},{4,5},{5,6},{6,7},{7,0},{8,9},{9,10},{10,1... | collective-permute-start | bytes 313352 | tf_op jit(solution)/shard_map/ppermute | solution.py:26
  64.6 0.1 collective-permute-done.1
  64.7 1.9 %collective-permute-start.2 = (bf16[6,4,2176]{2,1,0:T(4,128)(2,1)S(1)}, bf16[6,4,2176]{2,1,0:T(4,128)(2,1)S(1)}, u32[]{:S(2)}, u32[]{:S(2)}) collective-permute-start(bf16[6,4,2176]{2,1,0:T(4,128)(2,1)S(1)} %collective-permute-done.1), channel_id=1, source_target_pairs={{0,7},{1,0},{2,1},{3,2},{4,3},{5,4},{6,5},{7,6},{8,15},{9,8},{10,9... | collective-permute-start | bytes 313352 | tf_op jit(solution)/shard_map/ppermute | solution.py:27
  66.7 1.8 %collective-permute-done.5 = bf16[6,4,2176]{2,1,0:T(4,128)(2,1)S(1)} collective-permute-done((bf16[6,4,2176]{2,1,0:T(4,128)(2,1)S(1)}, bf16[6,4,2176]{2,1,0:T(4,128)(2,1)S(1)}, u32[]{:S(2)}, u32[]{:S(2)}) %collective-permute-start.5) | collective-permute-done | bytes 104480 | tf_op jit(solution)/shard_map/ppermute | solution.py:26
  68.5 5.6 %collective-permute-start.6 = (bf16[3,4,2176]{2,1,0:T(4,128)(2,1)S(1)}, bf16[3,4,2176]{2,1,0:T(4,128)(2,1)S(1)}, u32[]{:S(2)}, u32[]{:S(2)}) collective-permute-start(bf16[3,4,2176]{2,1,0:T(4,128)(2,1)S(1)} %slice.86), channel_id=1, source_target_pairs={{0,1},{1,2},{2,3},{3,4},{4,5},{5,6},{6,7},{7,0},{8,9},{9,10},{10,1... | collective-permute-start | bytes 156680 | tf_op jit(solution)/shard_map/ppermute | solution.py:22
  74.2 1.9 %collective-permute-start.7 = (bf16[3,4,2176]{2,1,0:T(4,128)(2,1)S(1)}, bf16[3,4,2176]{2,1,0:T(4,128)(2,1)S(1)}, u32[]{:S(2)}, u32[]{:S(2)}) collective-permute-start(bf16[3,4,2176]{2,1,0:T(4,128)(2,1)S(1)} %slice.87), channel_id=1, source_target_pairs={{0,7},{1,0},{2,1},{3,2},{4,3},{5,4},{6,5},{7,6},{8,15},{9,8},{10,9... | collective-permute-start | bytes 156680 | tf_op jit(solution)/shard_map/ppermute | solution.py:23
  76.8 0.2 copy.164
  76.9 0.2 copy.165
  77.1 0.2 copy.171
  77.3 0.2 copy.166
  77.4 0.2 copy.170
  77.6 0.2 copy.167
  77.8 0.2 copy.169
  78.0 3.5 %collective-permute-done.7 = bf16[3,4,2176]{2,1,0:T(4,128)(2,1)S(1)} collective-permute-done((bf16[3,4,2176]{2,1,0:T(4,128)(2,1)S(1)}, bf16[3,4,2176]{2,1,0:T(4,128)(2,1)S(1)}, u32[]{:S(2)}, u32[]{:S(2)}) %collective-permute-start.7) | collective-permute-done | bytes 52256 | tf_op jit(solution)/shard_map/ppermute | solution.py:23
  81.6 0.2 copy.168
  81.7 2.7 %stack.37 = bf16[8,6,4,2176]{3,0,2,1:T(8,128)(2,1)S(1)} concatenate(bf16[1,6,4,2176]{3,0,2,1:T(2,128)(2,1)S(1)} %copy.164, bf16[1,6,4,2176]{3,0,2,1:T(2,128)(2,1)S(1)} %copy.165, bf16[1,6,4,2176]{3,0,2,1:T(2,128)(2,1)S(1)} %copy.166, bf16[1,6,4,2176]{3,0,2,1:T(2,128)(2,1)S(1)} %copy.167, bf16[1,6,4,2176]{3,0,2,1:T(2,128)(2,1)S(1)} %copy.168, bf16[1,6,4,2176]{3,0,2,1:T(2,128)(2,1)S(1)} %copy.169, ...), dimensions={0} | concatenate | bytes 1671168 | tf_op jit(solution)/shard_map/stack | solution.py:78
  84.4 2.6 %collective-permute-start.9 = (bf16[8,6,4,2176]{3,0,2,1:T(8,128)(2,1)S(1)}, bf16[8,6,4,2176]{3,0,2,1:T(8,128)(2,1)}, u32[]{:S(2)}, u32[]{:S(2)}) collective-permute-start(bf16[8,6,4,2176]{3,0,2,1:T(8,128)(2,1)S(1)} %stack.37), channel_id=1, source_target_pairs={{0,8},{8,16},{16,24},{24,0},{1,9},{9,17},{17,25},{25,1},{2,10},{10... | collective-permute-start | bytes 2506760 | tf_op jit(solution)/shard_map/ppermute | solution.py:26
  87.0 3.2 %collective-permute-start.8 = (bf16[8,6,4,2176]{3,0,2,1:T(8,128)(2,1)S(1)}, bf16[8,6,4,2176]{3,0,2,1:T(8,128)(2,1)}, u32[]{:S(2)}, u32[]{:S(2)}) collective-permute-start(bf16[8,6,4,2176]{3,0,2,1:T(8,128)(2,1)S(1)} %stack.37), channel_id=1, source_target_pairs={{0,24},{8,0},{16,8},{24,16},{1,25},{9,1},{17,9},{25,17},{2,26},{10... | collective-permute-start | bytes 2506760 | tf_op jit(solution)/shard_map/ppermute | solution.py:27
  90.3 6.4 %copy.173 = bf16[1,1,3,5376,128]{3,4,2,1,0:T(8,128)(2,1)} copy(bf16[1,1,3,5376,128]{4,3,2,1,0:T(8,128)(2,1)} %param.10) | data formatting | bytes 8257536 | tf_op args[2]
  96.7 1.7 %slice.97 = bf16[3,2048,128]{1,2,0:T(8,128)(2,1)S(1)} slice(bf16[3,5376,128]{1,2,0:T(8,128)(2,1)} %bitcast.130), slice={[0:3], [3328:5376], [0:128]} | slice | bytes 3145728 | tf_op jit(solution)/shard_map/slice | solution.py:67
  98.6 0.7 fusion.7
  99.3 0.8 bitcast_dynamic-update-slice_fusion.6
  100.1 15.1 %collective-permute-done.9 = bf16[8,6,4,2176]{3,0,2,1:T(8,128)(2,1)} collective-permute-done((bf16[8,6,4,2176]{3,0,2,1:T(8,128)(2,1)S(1)}, bf16[8,6,4,2176]{3,0,2,1:T(8,128)(2,1)}, u32[]{:S(2)}, u32[]{:S(2)}) %collective-permute-start.9) | collective-permute-done | bytes 835616 | tf_op jit(solution)/shard_map/ppermute | solution.py:26
  115.3 1.3 slice.90
  116.5 3.6 %collective-permute-start.10 = (bf16[4,6,4,2176]{3,0,2,1:T(4,128)(2,1)S(1)}, bf16[4,6,4,2176]{3,0,2,1:T(4,128)(2,1)S(1)}, u32[]{:S(2)}, u32[]{:S(2)}) collective-permute-start(bf16[4,6,4,2176]{3,0,2,1:T(4,128)(2,1)S(1)} %slice.90), channel_id=1, source_target_pairs={{0,8},{8,16},{16,24},{24,0},{1,9},{9,17},{17,25},{25,1},{2,10},{10... | collective-permute-start | bytes 1253384 | tf_op jit(solution)/shard_map/ppermute | solution.py:22
  120.1 3.1 %collective-permute-done.8 = bf16[8,6,4,2176]{3,0,2,1:T(8,128)(2,1)} collective-permute-done((bf16[8,6,4,2176]{3,0,2,1:T(8,128)(2,1)S(1)}, bf16[8,6,4,2176]{3,0,2,1:T(8,128)(2,1)}, u32[]{:S(2)}, u32[]{:S(2)}) %collective-permute-start.8) | collective-permute-done | bytes 835616 | tf_op jit(solution)/shard_map/ppermute | solution.py:27
  123.2 1.4 slice.91
  124.5 2.1 %collective-permute-start.11 = (bf16[4,6,4,2176]{3,0,2,1:T(4,128)(2,1)S(1)}, bf16[4,6,4,2176]{3,0,2,1:T(4,128)(2,1)S(1)}, u32[]{:S(2)}, u32[]{:S(2)}) collective-permute-start(bf16[4,6,4,2176]{3,0,2,1:T(4,128)(2,1)S(1)} %slice.91), channel_id=1, source_target_pairs={{0,24},{8,0},{16,8},{24,16},{1,25},{9,1},{17,9},{25,17},{2,26},{10... | collective-permute-start | bytes 1253384 | tf_op jit(solution)/shard_map/ppermute | solution.py:23
  126.6 0.9 slice_reduce_fusion.1
  127.5 1.9 %fusion.5 = f32[8,6,4,3,128]{4,0,3,2,1:T(8,128)S(1)} fusion(bf16[3,2048,128]{1,2,0:T(8,128)(2,1)S(1)} %slice.97, bf16[8,6,4,2176]{3,0,2,1:T(8,128)(2,1)} %collective-permute-done.8), kind=kOutput, calls=%fused_computation.13 | convolution fusion | flops 320864256 | bytes 2703360 | tf_op jit(solution)/shard_map/dot_general | solution.py:72
  129.4 0.8 bitcast_dynamic-update-slice_fusion.4
  130.2 0.9 slice_reduce_fusion
  131.1 1.9 %fusion.1 = f32[8,6,4,3,128]{4,0,3,2,1:T(8,128)S(1)} fusion(bf16[3,2048,128]{1,2,0:T(8,128)(2,1)S(1)} %slice.97, bf16[8,6,4,2176]{3,0,2,1:T(8,128)(2,1)} %collective-permute-done.9), kind=kOutput, calls=%fused_computation.9 | convolution fusion | flops 320864256 | bytes 2703360 | tf_op jit(solution)/shard_map/dot_general | solution.py:72
  133.0 2.1 %collective-permute-done.10 = bf16[4,6,4,2176]{3,0,2,1:T(4,128)(2,1)S(1)} collective-permute-done((bf16[4,6,4,2176]{3,0,2,1:T(4,128)(2,1)S(1)}, bf16[4,6,4,2176]{3,0,2,1:T(4,128)(2,1)S(1)}, u32[]{:S(2)}, u32[]{:S(2)}) %collective-permute-start.10) | collective-permute-done | bytes 417824 | tf_op jit(solution)/shard_map/ppermute | solution.py:22
  135.1 3.9 %collective-permute-done.11 = bf16[4,6,4,2176]{3,0,2,1:T(4,128)(2,1)S(1)} collective-permute-done((bf16[4,6,4,2176]{3,0,2,1:T(4,128)(2,1)S(1)}, bf16[4,6,4,2176]{3,0,2,1:T(4,128)(2,1)S(1)}, u32[]{:S(2)}, u32[]{:S(2)}) %collective-permute-start.11) | collective-permute-done | bytes 417824 | tf_op jit(solution)/shard_map/ppermute | solution.py:23
  139.0 0.8 copy-done.2
  140.0 0.1 fusion.27
  140.2 0.2 copy.172
  140.5 0.6 gather_fusion.3
  141.1 1.9 %fusion.3 = f32[8,6,4,3,128]{4,0,3,2,1:T(8,128)S(1)} fusion(bf16[3,2048,128]{1,2,0:T(8,128)(2,1)S(1)} %slice.97, bf16[4,6,4,2176]{3,0,2,1:T(4,128)(2,1)} %copy-done.2, bf16[4,6,4,2176]{3,0,2,1:T(4,128)(2,1)S(1)} %collective-permute-done.10), kind=kOutput, calls=%fused_computation.11 | convolution fusion | flops 322535424 | bytes 2703360 | tf_op jit(solution)/shard_map/dot_general | solution.py:72
  143.7 0.2 constant_dynamic-slice_fusion
  143.9 7.2 %fusion.11 = f32[6,3,4,8,4,128]{5,4,1,0,3,2:T(4,128)S(1)} fusion(bf16[4,8,6,4,3328,1]{4,3,5,2,1,0:T(4,128)(2,1)} %bitcast.141, bf16[3,5376,128]{1,2,0:T(8,128)(2,1)} %bitcast.131, s32[]{:T(128)S(6)} %select_n.102, f32[4,8,6,4,3,128]{5,3,4,2,1,0:T(4,128)S(1)} %constant_dynamic-slice_fusion), kind=kOutput, calls=%fused_computation.20 | convolution fusion | flops 1963524096 | bytes 10027012 | tf_op jit(solution)/shard_map/dot_general | solution.py:72
  151.2 0.3 copy.178
  151.5 0.6 gather_fusion.4
  152.1 1.2 fusion.18
  (45 shorter events, 1.6 us)
Async XLA Ops:
  6.5 1.5 copy-start
  9.2 12.6 %copy-start.3 = (s32[16,6]{0,1:T(8,128)S(1)}, s32[16,6]{0,1:T(8,128)}, u32[]{:S(2)}) copy-start(s32[16,6]{0,1:T(8,128)} %param.11) | copy-start | bytes 1156
  11.2 55.4 %copy-start.4 = (s32[1,1,18,2]{2,3,1,0:T(2,128)S(1)}, s32[1,1,18,2]{2,3,1,0:T(2,128)}, u32[]{:S(2)}) copy-start(s32[1,1,18,2]{2,3,1,0:T(2,128)} %param.12) | copy-start | bytes 436
  11.2 29.7 %all-to-all-start = ((bf16[16,4,5504]{2,1,0:T(4,128)(2,1)}), bf16[16,4,5504]{2,1,0:T(4,128)(2,1)S(1)}, u32[]{:S(2)}, u32[]{:S(2)}) async-start(bf16[16,4,5504]{2,1,0:T(4,128)(2,1)} %fusion.24), calls=%async_computation | async-start | bytes 1409024 | tf_op jit(solution)/shard_map/all_to_all | solution.py:51
  21.8 122.2 %all-gather.3.cloned.1.call-start = ((), (), s32[]{:S(2)}) async-start(), calls=%async_computation.1 | async-start | bytes 5271552 | tf_op jit(solution)/shard_map/all_gather | solution.py:75
  42.7 7.0 %collective-permute-start.3 = (bf16[6,4,2176]{2,1,0:T(4,128)(2,1)S(1)}, bf16[6,4,2176]{2,1,0:T(4,128)(2,1)S(1)}, u32[]{:S(2)}, u32[]{:S(2)}) collective-permute-start(bf16[6,4,2176]{2,1,0:T(4,128)(2,1)S(1)} %get-tuple-element.17), channel_id=1, source_target_pairs={{0,1},{1,2},{2,3},{3,4},{4,5},{5,6},{6,7},{7,0},{8,9},{9,10},{10,1... | collective-permute-start | bytes 313352 | tf_op jit(solution)/shard_map/ppermute | solution.py:26
  47.4 7.9 %collective-permute-start = (bf16[6,4,2176]{2,1,0:T(4,128)(2,1)S(1)}, bf16[6,4,2176]{2,1,0:T(4,128)(2,1)S(1)}, u32[]{:S(2)}, u32[]{:S(2)}) collective-permute-start(bf16[6,4,2176]{2,1,0:T(4,128)(2,1)S(1)} %get-tuple-element.17), channel_id=1, source_target_pairs={{0,7},{1,0},{2,1},{3,2},{4,3},{5,4},{6,5},{7,6},{8,15},{9,8},{10,9... | collective-permute-start | bytes 313352 | tf_op jit(solution)/shard_map/ppermute | solution.py:27
  49.6 9.3 %collective-permute-start.4 = (bf16[6,4,2176]{2,1,0:T(4,128)(2,1)S(1)}, bf16[6,4,2176]{2,1,0:T(4,128)(2,1)S(1)}, u32[]{:S(2)}, u32[]{:S(2)}) collective-permute-start(bf16[6,4,2176]{2,1,0:T(4,128)(2,1)S(1)} %collective-permute-done.3), channel_id=1, source_target_pairs={{0,1},{1,2},{2,3},{3,4},{4,5},{5,6},{6,7},{7,0},{8,9},{9,10},{10,1... | collective-permute-start | bytes 313352 | tf_op jit(solution)/shard_map/ppermute | solution.py:26
  55.3 9.4 %collective-permute-start.1 = (bf16[6,4,2176]{2,1,0:T(4,128)(2,1)S(1)}, bf16[6,4,2176]{2,1,0:T(4,128)(2,1)S(1)}, u32[]{:S(2)}, u32[]{:S(2)}) collective-permute-start(bf16[6,4,2176]{2,1,0:T(4,128)(2,1)S(1)} %collective-permute-done), channel_id=1, source_target_pairs={{0,7},{1,0},{2,1},{3,2},{4,3},{5,4},{6,5},{7,6},{8,15},{9,8},{10,9... | collective-permute-start | bytes 313352 | tf_op jit(solution)/shard_map/ppermute | solution.py:27
  59.0 9.5 %collective-permute-start.5 = (bf16[6,4,2176]{2,1,0:T(4,128)(2,1)S(1)}, bf16[6,4,2176]{2,1,0:T(4,128)(2,1)S(1)}, u32[]{:S(2)}, u32[]{:S(2)}) collective-permute-start(bf16[6,4,2176]{2,1,0:T(4,128)(2,1)S(1)} %collective-permute-done.4), channel_id=1, source_target_pairs={{0,1},{1,2},{2,3},{3,4},{4,5},{5,6},{6,7},{7,0},{8,9},{9,10},{10,1... | collective-permute-start | bytes 313352 | tf_op jit(solution)/shard_map/ppermute | solution.py:26
  64.7 9.4 %collective-permute-start.2 = (bf16[6,4,2176]{2,1,0:T(4,128)(2,1)S(1)}, bf16[6,4,2176]{2,1,0:T(4,128)(2,1)S(1)}, u32[]{:S(2)}, u32[]{:S(2)}) collective-permute-start(bf16[6,4,2176]{2,1,0:T(4,128)(2,1)S(1)} %collective-permute-done.1), channel_id=1, source_target_pairs={{0,7},{1,0},{2,1},{3,2},{4,3},{5,4},{6,5},{7,6},{8,15},{9,8},{10,9... | collective-permute-start | bytes 313352 | tf_op jit(solution)/shard_map/ppermute | solution.py:27
  68.5 9.5 %collective-permute-start.6 = (bf16[3,4,2176]{2,1,0:T(4,128)(2,1)S(1)}, bf16[3,4,2176]{2,1,0:T(4,128)(2,1)S(1)}, u32[]{:S(2)}, u32[]{:S(2)}) collective-permute-start(bf16[3,4,2176]{2,1,0:T(4,128)(2,1)S(1)} %slice.86), channel_id=1, source_target_pairs={{0,1},{1,2},{2,3},{3,4},{4,5},{5,6},{6,7},{7,0},{8,9},{9,10},{10,1... | collective-permute-start | bytes 156680 | tf_op jit(solution)/shard_map/ppermute | solution.py:22
  74.2 7.3 %collective-permute-start.7 = (bf16[3,4,2176]{2,1,0:T(4,128)(2,1)S(1)}, bf16[3,4,2176]{2,1,0:T(4,128)(2,1)S(1)}, u32[]{:S(2)}, u32[]{:S(2)}) collective-permute-start(bf16[3,4,2176]{2,1,0:T(4,128)(2,1)S(1)} %slice.87), channel_id=1, source_target_pairs={{0,7},{1,0},{2,1},{3,2},{4,3},{5,4},{6,5},{7,6},{8,15},{9,8},{10,9... | collective-permute-start | bytes 156680 | tf_op jit(solution)/shard_map/ppermute | solution.py:23
  84.4 30.9 %collective-permute-start.9 = (bf16[8,6,4,2176]{3,0,2,1:T(8,128)(2,1)S(1)}, bf16[8,6,4,2176]{3,0,2,1:T(8,128)(2,1)}, u32[]{:S(2)}, u32[]{:S(2)}) collective-permute-start(bf16[8,6,4,2176]{3,0,2,1:T(8,128)(2,1)S(1)} %stack.37), channel_id=1, source_target_pairs={{0,8},{8,16},{16,24},{24,0},{1,9},{9,17},{17,25},{25,1},{2,10},{10... | collective-permute-start | bytes 2506760 | tf_op jit(solution)/shard_map/ppermute | solution.py:26
  87.0 36.1 %collective-permute-start.8 = (bf16[8,6,4,2176]{3,0,2,1:T(8,128)(2,1)S(1)}, bf16[8,6,4,2176]{3,0,2,1:T(8,128)(2,1)}, u32[]{:S(2)}, u32[]{:S(2)}) collective-permute-start(bf16[8,6,4,2176]{3,0,2,1:T(8,128)(2,1)S(1)} %stack.37), channel_id=1, source_target_pairs={{0,24},{8,0},{16,8},{24,16},{1,25},{9,1},{17,9},{25,17},{2,26},{10... | collective-permute-start | bytes 2506760 | tf_op jit(solution)/shard_map/ppermute | solution.py:27
  116.5 18.6 %collective-permute-start.10 = (bf16[4,6,4,2176]{3,0,2,1:T(4,128)(2,1)S(1)}, bf16[4,6,4,2176]{3,0,2,1:T(4,128)(2,1)S(1)}, u32[]{:S(2)}, u32[]{:S(2)}) collective-permute-start(bf16[4,6,4,2176]{3,0,2,1:T(4,128)(2,1)S(1)} %slice.90), channel_id=1, source_target_pairs={{0,8},{8,16},{16,24},{24,0},{1,9},{9,17},{17,25},{25,1},{2,10},{10... | collective-permute-start | bytes 1253384 | tf_op jit(solution)/shard_map/ppermute | solution.py:22
  124.5 14.5 %collective-permute-start.11 = (bf16[4,6,4,2176]{3,0,2,1:T(4,128)(2,1)S(1)}, bf16[4,6,4,2176]{3,0,2,1:T(4,128)(2,1)S(1)}, u32[]{:S(2)}, u32[]{:S(2)}) collective-permute-start(bf16[4,6,4,2176]{3,0,2,1:T(4,128)(2,1)S(1)} %slice.91), channel_id=1, source_target_pairs={{0,24},{8,0},{16,8},{24,16},{1,25},{9,1},{17,9},{25,17},{2,26},{10... | collective-permute-start | bytes 1253384 | tf_op jit(solution)/shard_map/ppermute | solution.py:23
  139.0 0.8 copy-start.2
  141.1 1.9 %copy-start.1 = (f32[8,8,6,4,3,128]{5,3,4,2,1,0:T(4,128)S(1)}, f32[8,8,6,4,3,128]{5,3,4,2,1,0:T(4,128)}, u32[]{:S(2)}) copy-start(f32[8,8,6,4,3,128]{5,3,4,2,1,0:T(4,128)} %bitcast_dynamic-update-slice_fusion.4) | copy-start | bytes 7077892
Sparse Core Ops, SparseCore 0:
  42.7 98.4 all-gather.2
